TPU v7x, 128 devices: a whole 4x4x4 slice. The times are simulated.
128 devices in a mesh: dp: 32 (over z_hi, x, y), mp: 4 (over z_lo, core).
Axes of the slice: x: 4, y: 4, z: 4 (z_hi: 2, z_lo: 2; z = z_hi * 2 + z_lo), core: 2. Of those that a mesh axis runs over, the one named last changes fastest.
Arguments:
- sample_grad: bfloat16 [4608, 8192], P('dp', 'mp'), may hold values from -3 to 3
- advantage: int32 [4608], P('dp'), may hold values from 1024 to 8191
- route_rows: int32 [32, 144], P('dp'), may hold values from 0 to 143, each once within a row
- route_count: int32 [32, 32], P('dp'), may hold values from 1 to 4, 80 in all within a row
- gate_pre: bfloat16 [4096, 16384], P('mp', 'dp'), may hold values from -5 to 5
- up_pre: bfloat16 [4096, 16384], P('mp', 'dp'), may hold values from -5 to 5
- down_weight: bfloat16 [16384, 8192], P('dp', 'mp'), may hold values from -0.046875 to 0.046875
Outputs:
- grad_down: float32 [16384, 8192], P('dp', 'mp')
- grad_gate: bfloat16 [4096, 16384], P('mp', 'dp')
- grad_up: bfloat16 [4096, 16384], P('mp', 'dp')
Inputs may be any that keep to these rules, and one draw needn't show every extreme that they name: Each row of route_rows is a permutation of the sampler's 144 row numbers. `route_count`: each sampler sends every learner at least one row and 80 rows in all; in each sampler's row some learner receives exactly 4.
All inputs are finite; a program needn't handle non-finite values.
Results may differ from a plain program's by a relative error of at most 0.005.
Values may be sent and summed in bfloat16 or wider, within the bound.
No kernel may reach another device: no remote copies, remote signals or barrier semaphores. Data moves between devices by JAX's collectives and lax.ppermute only.
A program may use at most 128 MiB of HBM per device.

v0:
```python
import jax
import jax.numpy as jnp
from jax import lax
from jax.sharding import PartitionSpec as P

SLOTS = 128


def silu_parts(gate_in):
    sigmoid_val = jax.nn.sigmoid(gate_in)
    return (gate_in * sigmoid_val, sigmoid_val * (1.0 + gate_in * (1.0 - sigmoid_val)))


def shards(sample_grad, advantage, route_rows, route_count, gate_pre, up_pre, down_weight):
    learners = lax.axis_size("dp")
    capacity = SLOTS // learners
    weights = advantage.astype(jnp.float32) * (1.0 / 4096.0)
    scaled = (sample_grad.astype(jnp.float32) * weights[:, None]).astype(jnp.bfloat16)
    gate_in = gate_pre.astype(jnp.float32)
    up_in = up_pre.astype(jnp.float32)
    activated, slopes = silu_parts(gate_in)
    hidden = (activated * up_in).astype(jnp.bfloat16)
    hidden_all = lax.all_gather(hidden, "mp", axis=0, tiled=True)
    everything, tables, counts = (
        lax.all_gather(scaled, "dp", axis=0, tiled=True),
        lax.all_gather(route_rows, "dp", axis=0, tiled=True),
        lax.all_gather(route_count, "dp", axis=0, tiled=True),
    )
    route_table = tables[:, :SLOTS].reshape(learners, learners, capacity)
    offsets = (jnp.arange(learners, dtype=jnp.int32) * scaled.shape[0])[:, None, None]
    source_rows = jnp.transpose(route_table + offsets, (1, 0, 2)).reshape(-1).astype(jnp.int32)
    live_mask = jnp.arange(capacity, dtype=jnp.int32)[None, None, :] < counts[:, :, None]
    live_mask = jnp.transpose(live_mask, (1, 0, 2)).reshape(-1)
    slot_rows = jnp.where(live_mask[:, None], everything[source_rows], jnp.zeros((), jnp.bfloat16))
    grad_down = lax.dot_general(
        hidden_all, slot_rows, (((0,), (0,)), ((), ())), preferred_element_type=jnp.float32
    )
    partial_value = lax.dot_general(
        slot_rows, down_weight, (((1,), (1,)), ((), ())), preferred_element_type=jnp.float32
    )
    hidden_grad = lax.psum_scatter(partial_value, "mp", scatter_dimension=0, tiled=True)
    grad_gate = (hidden_grad * up_in * slopes).astype(jnp.bfloat16)
    grad_up = (hidden_grad * activated).astype(jnp.bfloat16)
    return (grad_down, grad_gate, grad_up)


def solution(mesh):
    placed = (
        P("dp", "mp"),
        P("dp"),
        P("dp", None),
        P("dp", None),
        P("mp", "dp"),
        P("mp", "dp"),
        P("dp", "mp"),
    )
    return jax.shard_map(
        shards,
        mesh=mesh,
        in_specs=placed,
        out_specs=(P("dp", "mp"), P("mp", "dp"), P("mp", "dp")),
        check_vma=False,
    )
```

profile of v0, /device:TPU:1, one launch (start us, length us, event | category | flops | bytes accessed | tf_op | source)
XLA Modules:
  0.0 401.4 jit_solution(10951082151051512233)
XLA Ops:
  7.2 0.0 copy-start
  7.2 0.0 all-gather.7.cloned.1.call-start
  7.2 0.8 convert_multiply_fusion.4
  8.0 2.0 multiply_convert_fusion.1
  10.1 0.0 all-gather.7.cloned.1.call-update
  10.1 0.0 reduce-scatter.2.cloned.1.call-start
  10.2 83.0 %all-gather.1 = s32[32,1,144]{2,1,0:T(1,128)S(1)} all-gather(s32[1,1,144]{2,1,0:T(1,128)} %bitcast.16), channel_id=1, replica_groups=mesh['dp'=32,'mp'=4] {'dp'}, dimensions={0}, use_global_device_ids=true | all-gather | bytes 19008 | tf_op jit(solution)/shard_map/all_gather | solution.py:26
  93.2 0.1 copy.17
  93.3 0.3 copy.18
  93.6 0.3 reshape.61
  93.9 74.1 %all-gather = s32[32,1,32]{2,1,0:T(1,128)S(1)} all-gather(s32[1,1,32]{2,1,0:T(1,128)} %bitcast.17), channel_id=1, replica_groups=mesh['dp'=32,'mp'=4] {'dp'}, dimensions={0}, use_global_device_ids=true | all-gather | bytes 4224 | tf_op jit(solution)/shard_map/all_gather | solution.py:27
  168.1 0.1 copy.16
  168.1 0.2 iota_compare_fusion
  168.3 0.3 lt.40
  168.7 14.5 %all-gather.7.cloned.1.call-done = bf16[4608,2048]{1,0:T(8,128)(2,1)} async-done(((bf16[144,2048]{1,0:T(8,128)(2,1)}), bf16[4608,2048]{1,0:T(8,128)(2,1)}) %all-gather.7.cloned.1.call-update) | async-done | bytes 18874384 | tf_op jit(solution)/shard_map/all_gather | solution.py:25
  183.2 40.1 %gather_fusion = bf16[4096,2048]{1,0:T(8,128)(2,1)} fusion(bf16[4608,2048]{1,0:T(8,128)(2,1)} %all-gather.7.cloned.1.call-done, s32[4096]{0:T(1024)S(1)} %broadcast_clamp_fusion), kind=kCustom, calls=%fused_computation | custom fusion | bytes 33570816 | tf_op jit(solution)/shard_map/gather | solution.py:34
  223.3 0.0 copy-done
  223.3 14.5 %fusion = f32[4096,512]{1,0:T(8,128)} fusion(bf16[512,2048]{1,0:T(8,128)(2,1)S(1)} %copy-done, bf16[4096,2048]{1,0:T(8,128)(2,1)} %gather_fusion, pred[4096]{0:T(1024)(128)(4,1)S(1)} %lt.40), kind=kOutput, calls=%fused_computation.2 | convolution fusion | flops 8598323200 | bytes 27267072 | tf_op jit(solution)/shard_map/dot_general | solution.py:38
  237.9 0.0 copy-start.1
  237.9 0.0 reduce-scatter.2.cloned.1.call-update
  237.9 0.2 all-gather.5.cloned.1.call-start
  238.1 88.9 %reduce-scatter.2.cloned.1.call-done = f32[1024,512]{1,0:T(8,128)} async-done(((f32[4096,512]{1,0:T(8,128)}), f32[1024,512]{1,0:T(8,128)}) %reduce-scatter.2.cloned.1.call-update) | async-done | bytes 2097168 | tf_op jit(solution)/shard_map/reduce_scatter | solution.py:41
  327.0 0.0 copy-done.1
  327.0 5.0 %multiply_convert_fusion = (bf16[1024,512]{1,0:T(8,128)(2,1)}, bf16[1024,512]{1,0:T(8,128)(2,1)}, bf16[1024,512]{1,0:T(8,128)(2,1)}) fusion(f32[1024,512]{1,0:T(8,128)} %reduce-scatter.2.cloned.1.call-done, bf16[1024,512]{1,0:T(8,128)(2,1)S(1)} %copy-done.1, bf16[1024,512]{1,0:T(8,128)(2,1)} %param.12), kind=kLoop, calls=%fused_computation.17 | loop fusion | flops 8912896 | bytes 7340032 | tf_op jit(solution)/shard_map/convert_element_type | solution.py:43
  332.0 0.0 all-gather.5.cloned.1.call-update
  332.0 47.8 %all-gather.5.cloned.1.call-done = bf16[4096,512]{1,0:T(8,128)(2,1)} async-done(((bf16[1024,512]{1,0:T(8,128)(2,1)}), bf16[4096,512]{1,0:T(8,128)(2,1)}) %all-gather.5.cloned.1.call-update) | async-done | bytes 4194320 | tf_op jit(solution)/shard_map/all_gather | solution.py:23
  379.8 15.0 %fusion.1 = f32[512,2048]{1,0:T(8,128)} fusion(bf16[4096,512]{1,0:T(8,128)(2,1)} %all-gather.5.cloned.1.call-done, bf16[4096,2048]{1,0:T(8,128)(2,1)} %gather_fusion, pred[4096]{0:T(1024)(128)(4,1)S(1)} %lt.40), kind=kOutput, calls=%fused_computation.3 | convolution fusion | flops 8598323200 | bytes 25169920 | tf_op jit(solution)/shard_map/dot_general | solution.py:35
  (5 shorter events, 0.0 us)
Async XLA Ops:
  7.2 216.1 %copy-start = (bf16[512,2048]{1,0:T(8,128)(2,1)S(1)}, bf16[512,2048]{1,0:T(8,128)(2,1)}, u32[]{:S(2)}) copy-start(bf16[512,2048]{1,0:T(8,128)(2,1)} %param.13) | copy-start | bytes 6291460
  7.2 176.0 %all-gather.7.cloned.1.call-start = ((), (), s32[]{:S(2)}) async-start(), calls=%async_computation.2 | async-start | bytes 19464192 | tf_op jit(solution)/shard_map/all_gather | solution.py:25
  10.1 316.9 %reduce-scatter.2.cloned.1.call-start = ((), (), s32[]{:S(2)}) async-start(), calls=%async_computation.3 | async-start | bytes 10485760 | tf_op jit(solution)/shard_map/reduce_scatter | solution.py:41
  237.9 89.2 %copy-start.1 = (bf16[1024,512]{1,0:T(8,128)(2,1)S(1)}, bf16[1024,512]{1,0:T(8,128)(2,1)}, u32[]{:S(2)}) copy-start(bf16[1024,512]{1,0:T(8,128)(2,1)} %param.11) | copy-start | bytes 3145732
  237.9 141.9 %all-gather.5.cloned.1.call-start = ((), (), s32[]{:S(2)}) async-start(), calls=%async_computation.1 | async-start | bytes 5242880 | tf_op jit(solution)/shard_map/all_gather | solution.py:23
Sparse Core Ops, SparseCore 0:
  11.6 171.5 all-gather.6
  238.0 88.9 reduce-scatter.1
  332.1 47.6 all-gather.4
where the time goes:
time: 402 us; the launch traced here: 401 us
  blocking collectives  157 us (39%)
  waiting for transfers between devices  151 us (38%)
  local copies, waits for them, and re-layouts  41.2 us (10%)
  matrix products  29.6 us (7%)
  between operations  13.8 us (3%)
  other arithmetic  8.09 us (2%)
    reduce_scatter x1, waiting for transfers between devices, shards(): lax.psum_scatter(partial_value, 'mp', scatter_dimension=0, tiled=True)  88.9 us
    all_gather x1, blocking collectives, shards(): lax.all_gather(route_rows, 'dp', axis=0, tiled=True)  83 us
    all_gather x1, blocking collectives, shards(): lax.all_gather(route_count, 'dp', axis=0, tiled=True)  74.1 us
    all_gather x1, waiting for transfers between devices, shards(): hidden_all = lax.all_gather(hidden, 'mp', axis=0, tiled=True)  47.8 us
    gather x1, local copies, waits for them, and re-layouts, shards(): everything[source_rows]  40.1 us
    dot_general x1, matrix products, shards(): lax.dot_general(hidden_all, slot_rows, (((0,), (0,)), ((), ())), preferre...  15 us
    dot_general x1, matrix products, shards(): lax.dot_general(slot_rows, down_weight, (((1,), (1,)), ((), ())), preferr...  14.5 us
    all_gather x1, waiting for transfers between devices, shards(): lax.all_gather(scaled, 'dp', axis=0, tiled=True)  14.5 us
  transfers between devices with their start and end apart: 3, of which 3 were waited for; matrix products, arithmetic and copies ran while one was open for 0% of the time, Pallas kernels for 0%

commit v1 on v0

v1 whole, which is shorter than its diff:
```python
import jax
import jax.numpy as jnp
from jax import lax
from jax.sharding import PartitionSpec as P

SLOTS = 128
LIVE = SLOTS * 5 // 8


def silu_parts(gate_in):
    sigmoid_val = jax.nn.sigmoid(gate_in)
    return (gate_in * sigmoid_val, sigmoid_val * (1.0 + gate_in * (1.0 - sigmoid_val)))


def shards(sample_grad, advantage, route_rows, route_count, gate_pre, up_pre, down_weight):
    learners = lax.axis_size("dp")
    capacity = SLOTS // learners
    total_slots = learners * SLOTS

    counts = lax.all_gather(route_count.astype(jnp.float32), "dp", axis=0, tiled=True).astype(jnp.int32)
    own = lax.dynamic_index_in_dim(counts, lax.axis_index("dp"), axis=0, keepdims=False)

    gate_in = gate_pre.astype(jnp.float32)
    up_in = up_pre.astype(jnp.float32)
    activated, slopes = silu_parts(gate_in)
    hidden = (activated * up_in).astype(jnp.bfloat16)
    hidden, sample_grad = lax.optimization_barrier((hidden, sample_grad))
    n_mp = lax.axis_size("mp")
    pieces = [hidden] + [
        lax.ppermute(hidden, "mp", [(i, (i + s) % n_mp) for i in range(n_mp)]) for s in range(1, n_mp)
    ]
    stacked = jnp.concatenate(pieces, axis=0)

    own_end = jnp.cumsum(own)
    pos = jnp.arange(LIVE, dtype=jnp.int32)
    own_m = jnp.sum((own_end[None, :] <= pos[:, None]).astype(jnp.int32), axis=1)
    own_c = pos - (own_end[own_m] - own[own_m])
    picked = route_rows[0][own_m * capacity + own_c]
    weights = advantage.astype(jnp.float32) * (1.0 / 4096.0)
    scaled = (sample_grad[picked].astype(jnp.float32) * weights[picked][:, None]).astype(jnp.bfloat16)
    everything = lax.all_gather(scaled, "dp", axis=0, tiled=True)

    ends = jnp.cumsum(counts, axis=1)
    starts = ends - counts
    m_of = jnp.sum((ends[:, None, :] <= pos[None, :, None]).astype(jnp.int32), axis=2)
    c_of = pos[None, :] - jnp.take_along_axis(starts, m_of, axis=1)
    sender = jnp.arange(learners, dtype=jnp.int32)[:, None]
    slot_of = (m_of * SLOTS + sender * capacity + c_of).reshape(-1)

    rows_per = hidden.shape[0]
    shift = (lax.axis_index("mp") - slot_of // rows_per) % n_mp
    hidden_live = stacked[shift * rows_per + slot_of % rows_per]
    grad_down = lax.dot_general(
        hidden_live, everything, (((0,), (0,)), ((), ())), preferred_element_type=jnp.float32
    )
    partial_live = lax.dot_general(
        everything, down_weight, (((1,), (1,)), ((), ())), preferred_element_type=jnp.float32
    )

    t = jnp.arange(total_slots, dtype=jnp.int32)
    t_m = t // SLOTS
    t_k = (t % SLOTS) // capacity
    t_c = t % capacity
    live = t_c < counts[t_k, t_m]
    source = jnp.where(live, t_k * LIVE + starts[t_k, t_m] + t_c, 0)
    partial_value = jnp.where(live[:, None], partial_live[source], 0.0)
    hidden_grad = lax.psum_scatter(partial_value, "mp", scatter_dimension=0, tiled=True)
    grad_gate = (hidden_grad * up_in * slopes).astype(jnp.bfloat16)
    grad_up = (hidden_grad * activated).astype(jnp.bfloat16)
    return (grad_down, grad_gate, grad_up)


def solution(mesh):
    placed = (
        P("dp", "mp"),
        P("dp"),
        P("dp", None),
        P("dp", None),
        P("mp", "dp"),
        P("mp", "dp"),
        P("dp", "mp"),
    )
    return jax.shard_map(
        shards,
        mesh=mesh,
        in_specs=placed,
        out_specs=(P("dp", "mp"), P("mp", "dp"), P("mp", "dp")),
        check_vma=False,
    )
```

time: 402 us -> 393 us (0.978)
  blocking collectives: 157 us -> 82.5 us
  local copies, waits for them, and re-layouts: 41.2 us -> 110 us
  other arithmetic: 8.09 us -> 20.2 us
  matrix products: 29.6 us -> 20.4 us
  waiting for transfers between devices: 151 us -> 142 us
    reduce_scatter x1, waiting for transfers between devices: 88.9 us -> 3.64 us  [shards(): lax.psum_scatter(partial_value, 'mp', scatter_dimension=0, tiled=True)]
    all_gather x2 -> x1, blocking collectives: 157 us -> 82.5 us  [shards(): lax.all_gather(route_count.astype(jnp.float32), 'dp', axis=0, tiled=True)]
    gather x1 -> x11, local copies, waits for them, and re-layouts: 40.1 us -> 108 us  [the longest x1 26.7 us: shards(): live = t_c < counts[t_k, t_m]]
    ppermute x0 -> x3, waiting for transfers between devices: none -> 67.4 us  [shards(): lax.ppermute(hidden, 'mp', [(i, (i + s) % n_mp) for i in range(n_mp)])]
    dot_general x2, matrix products: 29.6 us -> 20.4 us  [the longest x1 10.6 us: shards(): lax.dot_general(hidden_live, everything, (((0,), (0,)), ((), ())), prefer...]
    all_gather x2 -> x1, waiting for transfers between devices: 62.3 us -> 70.9 us  [shards(): everything = lax.all_gather(scaled, 'dp', axis=0, tiled=True)]
    select_n x1 -> x6, other arithmetic: 0.02 us -> 6.2 us  [the longest x2 6 us: shards(): partial_value = jnp.where(live[:, None], partial_live[source], 0.0)]
  transfers between devices with their start and end apart: 3 -> 5, of which waited for: 3 -> 5; matrix products, arithmetic and copies ran while one was open for 0% -> 25% of each run, Pallas kernels for 0% -> 0%
where the time goes in v1:
time: 393 us; the launch traced here: 392 us
  waiting for transfers between devices  142 us (36%)
  local copies, waits for them, and re-layouts  110 us (28%)
  blocking collectives  82.5 us (21%)
  matrix products  20.4 us (5%)
  other arithmetic  20.2 us (5%)
  between operations  14.2 us (4%)
    all_gather x1, blocking collectives, shards(): lax.all_gather(route_count.astype(jnp.float32), 'dp', axis=0, tiled=True)  82.5 us
    all_gather x1, waiting for transfers between devices, shards(): everything = lax.all_gather(scaled, 'dp', axis=0, tiled=True)  70.9 us
    ppermute x3, waiting for transfers between devices, shards(): lax.ppermute(hidden, 'mp', [(i, (i + s) % n_mp) for i in range(n_mp)])  67.4 us
    gather x1, local copies, waits for them, and re-layouts, shards(): live = t_c < counts[t_k, t_m]  26.7 us
    gather x1, local copies, waits for them, and re-layouts, shards(): source = jnp.where(live, t_k * LIVE + starts[t_k, t_m] + t_c, 0)  26.7 us
    gather x1, local copies, waits for them, and re-layouts, shards(): partial_value = jnp.where(live[:, None], partial_live[source], 0.0)  20.5 us
    gather x2, local copies, waits for them, and re-layouts, shards(): c_of = pos[None, :] - jnp.take_along_axis(starts, m_of, axis=1)  17 us
    gather x1, local copies, waits for them, and re-layouts, shards(): hidden_live = stacked[shift * rows_per + slot_of % rows_per]  11.1 us
  transfers between devices with their start and end apart: 5, of which 5 were waited for; matrix products, arithmetic and copies ran while one was open for 25% of the time, Pallas kernels for 0%

profile of v1, /device:TPU:1, one launch (start us, length us, event | category | flops | bytes accessed | tf_op | source)
XLA Modules:
  0.0 392.2 jit_solution(13609921323734698645)
XLA Ops:
  7.2 0.0 copy-start
  7.2 0.0 all-gather.3.cloned.1.call-start
  7.2 0.8 convert_bitcast_fusion
  8.0 0.7 convert_multiply_fusion.4
  8.7 82.5 %all-gather = f32[32,1,32]{2,1,0:T(1,128)S(1)} all-gather(f32[1,1,32]{2,1,0:T(1,128)S(1)} %convert_bitcast_fusion), channel_id=1, replica_groups=mesh['dp'=32,'mp'=4] {'dp'}, dimensions={0}, use_global_device_ids=true | all-gather | bytes 4224 | tf_op jit(solution)/shard_map/all_gather | solution.py:20
  91.2 0.1 copy.17
  91.3 0.1 reduce-window.8
  91.3 0.1 reduce.1
  91.4 0.1 convert_reduce_fusion.1
  91.6 1.2 gather_fusion.1
  92.8 1.2 gather_fusion.2
  94.1 0.0 copy-start.1
  94.1 1.7 gather_fusion.3
  95.8 3.2 fusion
  99.0 1.3 gather_fusion.5
  100.2 0.0 copy-done.1
  100.2 0.8 gather_fusion.4
  101.0 0.8 multiply_convert_fusion.1
  101.9 0.0 all-gather.3.cloned.1.call-update
  101.9 0.0 reduce-scatter.2.cloned.1.call-start
  102.0 0.2 reduce_window_sum.18
  102.1 0.1 fusion.14
  102.3 26.7 %gather_fusion.6 = s32[4096]{0:T(1024)S(1)} fusion(s32[32,32]{1,0:T(8,128)S(1)} %convert_bitcast_fusion.1, s32[4096]{0:T(1024)S(1)} %bitcast.42), kind=kCustom, calls=%fused_computation.6 | custom fusion | bytes 65536 | tf_op jit(solution)/shard_map/gather | solution.py:64
  129.0 26.7 %gather_fusion.7 = s32[4096]{0:T(1024)S(1)} fusion(s32[32,32]{1,0:T(8,128)S(1)} %bitcast_subtract_fusion.1, s32[4096]{0:T(1024)S(1)} %bitcast.43), kind=kCustom, calls=%fused_computation.7 | custom fusion | bytes 65536 | tf_op jit(solution)/shard_map/gather | solution.py:65
  155.7 0.1 compare_select_fusion
  155.8 70.9 %all-gather.3.cloned.1.call-done = bf16[2560,2048]{1,0:T(8,128)(2,1)} async-done(((bf16[80,2048]{1,0:T(8,128)(2,1)}), bf16[2560,2048]{1,0:T(8,128)(2,1)}) %all-gather.3.cloned.1.call-update) | async-done | bytes 10485776 | tf_op jit(solution)/shard_map/all_gather | solution.py:41
  226.7 0.0 copy-done
  226.7 9.9 %fusion.32 = f32[2560,512]{1,0:T(8,128)} fusion(bf16[2560,2048]{1,0:T(8,128)(2,1)} %all-gather.3.cloned.1.call-done, bf16[512,2048]{1,0:T(8,128)(2,1)S(1)} %copy-done), kind=kOutput, calls=%fused_computation.99 | convolution fusion | flops 5368709120 | bytes 17825792 | tf_op jit(solution)/shard_map/dot_general | solution.py:56
  236.6 20.5 %gather_fusion.8 = f32[4096,512]{1,0:T(8,128)} fusion(f32[2560,512]{1,0:T(8,128)} %fusion.32, s32[4096]{0:T(1024)S(1)} %broadcast_clamp_fusion), kind=kCustom, calls=%fused_computation.8 | custom fusion | bytes 16793600 | tf_op jit(solution)/shard_map/gather | solution.py:66
  257.1 5.9 %broadcast_select_fusion = f32[4096,512]{1,0:T(8,128)} fusion(f32[4096,512]{1,0:T(8,128)} %gather_fusion.8, pred[4096]{0:T(1024)(128)(4,1)S(1)} %fusion.8), kind=kLoop, calls=%fused_computation.11 | loop fusion | flops 2097152 | bytes 16781312 | tf_op jit(solution)/shard_map/jit(_where)/select_n | solution.py:66
  263.0 0.0 copy-start.3
  263.0 0.0 reduce-scatter.2.cloned.1.call-update
  263.0 1.2 copy-done.3
  264.2 1.4 collective-permute-start.2
  265.6 0.4 collective-permute-start.1
  266.0 1.3 collective-permute-start
  267.2 0.1 add.280
  267.3 0.1 add.281
  267.4 0.2 convert_reduce_fusion
  267.6 0.1 reduce_sum.25
  267.7 0.1 reshape.561
  267.8 16.9 %gather_fusion.9 = s32[2560]{0:T(1024)S(1)} fusion(s32[32,32]{1,0:T(8,128)S(1)} %bitcast_subtract_fusion.1, s32[2560]{0:T(1024)S(1)} %reshape.561), kind=kCustom, calls=%fused_computation.9 | custom fusion | bytes 40960 | tf_op jit(solution)/shard_map/jit(take_along_axis)/gather | solution.py:46
  284.7 0.1 sub.80
  284.8 0.2 fusion.21
  285.0 20.9 %collective-permute-done.2 = bf16[1024,512]{1,0:T(8,128)(2,1)} collective-permute-done((bf16[1024,512]{1,0:T(8,128)(2,1)S(1)}, bf16[1024,512]{1,0:T(8,128)(2,1)}, u32[]{:S(2)}, u32[]{:S(2)}) %collective-permute-start.2) | collective-permute-done | bytes 1048608 | tf_op jit(solution)/shard_map/ppermute | solution.py:30
  305.9 3.3 collective-permute-done.1
  309.2 43.2 %collective-permute-done = bf16[1024,512]{1,0:T(8,128)(2,1)} collective-permute-done((bf16[1024,512]{1,0:T(8,128)(2,1)S(1)}, bf16[1024,512]{1,0:T(8,128)(2,1)}, u32[]{:S(2)}, u32[]{:S(2)}) %collective-permute-start) | collective-permute-done | bytes 1048608 | tf_op jit(solution)/shard_map/ppermute | solution.py:30
  352.4 3.5 pad_maximum_fusion
  355.9 11.1 %gather_fusion = bf16[2560,512]{1,0:T(8,128)(2,1)} fusion(bf16[4096,512]{1,0:T(8,128)(2,1)} %pad_maximum_fusion, s32[3072]{0:T(1024)S(1)} %pad_clamp_fusion), kind=kCustom, calls=%fused_computation | custom fusion | bytes 5253120 | tf_op jit(solution)/shard_map/gather | solution.py:52
  367.0 0.0 copy-start.2
  367.0 10.6 %fusion.31 = f32[512,2048]{1,0:T(8,128)} fusion(bf16[2560,512]{1,0:T(8,128)(2,1)} %gather_fusion, bf16[2560,2048]{1,0:T(8,128)(2,1)} %all-gather.3.cloned.1.call-done), kind=kOutput, calls=%fused_computation.98 | convolution fusion | flops 5368709120 | bytes 17301504 | tf_op jit(solution)/shard_map/dot_general | solution.py:53
  377.6 3.6 reduce-scatter.2.cloned.1.call-done
  381.2 0.0 copy-done.2
  381.2 4.2 %multiply_convert_fusion = (bf16[1024,512]{1,0:T(8,128)(2,1)}, bf16[1024,512]{1,0:T(8,128)(2,1)}) fusion(f32[1024,512]{1,0:T(8,128)} %reduce-scatter.2.cloned.1.call-done, bf16[1024,512]{1,0:T(8,128)(2,1)} %param.11, bf16[1024,512]{1,0:T(8,128)(2,1)S(1)} %copy-done.2), kind=kLoop, calls=%fused_computation.25 | loop fusion | flops 7864320 | bytes 6291456 | tf_op jit(solution)/shard_map/convert_element_type | solution.py:69
  (16 shorter events, 0.1 us)
Async XLA Ops:
  7.2 219.6 %copy-start = (bf16[512,2048]{1,0:T(8,128)(2,1)S(1)}, bf16[512,2048]{1,0:T(8,128)(2,1)}, u32[]{:S(2)}) copy-start(bf16[512,2048]{1,0:T(8,128)(2,1)} %param.13) | copy-start | bytes 6291460
  7.2 219.5 %all-gather.3.cloned.1.call-start = ((), (), s32[]{:S(2)}) async-start(), calls=%async_computation.1 | async-start | bytes 10813440 | tf_op jit(solution)/shard_map/all_gather | solution.py:41
  94.1 6.2 %copy-start.1 = (bf16[144,2048]{1,0:T(8,128)(2,1)S(1)}, bf16[144,2048]{1,0:T(8,128)(2,1)}, u32[]{:S(2)}) copy-start(bf16[144,2048]{1,0:T(8,128)(2,1)} %param.7) | copy-start | bytes 1769476
  101.9 279.3 %reduce-scatter.2.cloned.1.call-start = ((), (), s32[]{:S(2)}) async-start(), calls=%async_computation.2 | async-start | bytes 10485760 | tf_op jit(solution)/shard_map/reduce_scatter | solution.py:67
  263.0 1.2 copy-start.3
  264.2 41.7 %collective-permute-start.2 = (bf16[1024,512]{1,0:T(8,128)(2,1)S(1)}, bf16[1024,512]{1,0:T(8,128)(2,1)}, u32[]{:S(2)}, u32[]{:S(2)}) collective-permute-start(bf16[1024,512]{1,0:T(8,128)(2,1)S(1)} %copy-done.3), channel_id=1, source_target_pairs={{0,3},{1,0},{2,1},{3,2},{4,7},{5,4},{6,5},{7,6},{8,11},{9,8},{10,9... | collective-permute-start | bytes 3145736 | tf_op jit(solution)/shard_map/ppermute | solution.py:30
  265.6 43.6 %collective-permute-start.1 = (bf16[1024,512]{1,0:T(8,128)(2,1)S(1)}, bf16[1024,512]{1,0:T(8,128)(2,1)}, u32[]{:S(2)}, u32[]{:S(2)}) collective-permute-start(bf16[1024,512]{1,0:T(8,128)(2,1)S(1)} %copy-done.3), channel_id=1, source_target_pairs={{0,2},{1,3},{2,0},{3,1},{4,6},{5,7},{6,4},{7,5},{8,10},{9,11},{10,... | collective-permute-start | bytes 3145736 | tf_op jit(solution)/shard_map/ppermute | solution.py:30
  266.0 86.4 %collective-permute-start = (bf16[1024,512]{1,0:T(8,128)(2,1)S(1)}, bf16[1024,512]{1,0:T(8,128)(2,1)}, u32[]{:S(2)}, u32[]{:S(2)}) collective-permute-start(bf16[1024,512]{1,0:T(8,128)(2,1)S(1)} %copy-done.3), channel_id=1, source_target_pairs={{0,1},{1,2},{2,3},{3,0},{4,5},{5,6},{6,7},{7,4},{8,9},{9,10},{10,1... | collective-permute-start | bytes 3145736 | tf_op jit(solution)/shard_map/ppermute | solution.py:30
  367.0 14.2 %copy-start.2 = (bf16[1024,512]{1,0:T(8,128)(2,1)S(1)}, bf16[1024,512]{1,0:T(8,128)(2,1)}, u32[]{:S(2)}) copy-start(bf16[1024,512]{1,0:T(8,128)(2,1)} %param.12) | copy-start | bytes 3145732
Sparse Core Ops, SparseCore 0:
  102.0 124.6 all-gather.2
  263.1 118.0 reduce-scatter.1

commit v2 on v1

v2 whole, which is shorter than its diff:
```python
import jax
import jax.numpy as jnp
from jax import lax
from jax.sharding import PartitionSpec as P

SLOTS = 128
LIVE = SLOTS * 5 // 8
INFO = 128


def silu_parts(gate_in):
    sigmoid_val = jax.nn.sigmoid(gate_in)
    return (gate_in * sigmoid_val, sigmoid_val * (1.0 + gate_in * (1.0 - sigmoid_val)))


def mp_gather(hidden):
    n_mp = lax.axis_size("mp")
    half = n_mp // 2
    me = lax.axis_index("mp")
    far = lax.ppermute(hidden, "mp", [(i, (i + half) % n_mp) for i in range(n_mp)])
    pair = jnp.stack([hidden, far])
    near = lax.ppermute(pair, "mp", [(i, i ^ 1) for i in range(n_mp)])
    held = jnp.concatenate([pair, near])
    block = jnp.arange(n_mp, dtype=jnp.int32)
    where = jnp.where(((block ^ me) % half) == 0, 0, 1) * 2 + jnp.where((block ^ me) >= half, 1, 0)
    return jnp.take(held, where, axis=0, mode="clip").reshape(n_mp * hidden.shape[0], hidden.shape[1])


def shards(sample_grad, advantage, route_rows, route_count, gate_pre, up_pre, down_weight):
    learners = lax.axis_size("dp")
    capacity = SLOTS // learners
    d_cols = sample_grad.shape[1]

    gate_in = gate_pre.astype(jnp.float32)
    up_in = up_pre.astype(jnp.float32)
    activated, slopes = silu_parts(gate_in)
    hidden = (activated * up_in).astype(jnp.bfloat16)
    hidden_all = mp_gather(hidden)

    own = route_count[0]
    own_end = jnp.cumsum(own)
    pos = jnp.arange(LIVE, dtype=jnp.int32)
    before = own_end[None, :] <= pos[:, None]
    own_m = jnp.sum(before.astype(jnp.int32), axis=1)
    own_c = pos - jnp.sum(jnp.where(before, own[None, :], 0), axis=1)
    picked = route_rows[0][own_m * capacity + own_c]
    weights = advantage.astype(jnp.float32) * (1.0 / 4096.0)
    scaled = (sample_grad[picked].astype(jnp.float32) * weights[picked][:, None]).astype(jnp.bfloat16)
    info = jnp.zeros((LIVE, INFO), jnp.bfloat16).at[0, :learners].set(own.astype(jnp.bfloat16))
    hidden_all, scaled = lax.optimization_barrier((hidden_all, scaled))
    sent = jnp.concatenate([scaled, info], axis=1)
    gathered = lax.all_gather(sent, "dp", axis=0, tiled=True)
    everything = gathered[:, :d_cols]
    counts = gathered.reshape(learners, LIVE, d_cols + INFO)[:, 0, d_cols:d_cols + learners]
    counts = counts.astype(jnp.int32)

    ends = jnp.cumsum(counts, axis=1)
    starts = ends - counts
    done = ends[:, None, :] <= pos[None, :, None]
    m_of = jnp.sum(done.astype(jnp.int32), axis=2)
    c_of = pos[None, :] - jnp.sum(jnp.where(done, counts[:, None, :], 0), axis=2)
    sender = jnp.arange(learners, dtype=jnp.int32)[:, None]
    slot_of = (m_of * SLOTS + sender * capacity + c_of).reshape(-1)

    hidden_live = hidden_all[slot_of]
    grad_down = lax.dot_general(
        hidden_live, everything, (((0,), (0,)), ((), ())), preferred_element_type=jnp.float32
    )
    partial_live = lax.dot_general(
        everything, down_weight, (((1,), (1,)), ((), ())), preferred_element_type=jnp.float32
    )

    lane = jnp.arange(capacity, dtype=jnp.int32)
    live = (lane[None, None, :] < counts.T[:, :, None]).reshape(-1)
    first = jnp.arange(learners, dtype=jnp.int32)[None, :] * LIVE + starts.T
    source = jnp.where(live, (first[:, :, None] + lane[None, None, :]).reshape(-1), 0)
    partial_value = jnp.where(live[:, None], partial_live[source], 0.0)
    hidden_grad = lax.psum_scatter(partial_value, "mp", scatter_dimension=0, tiled=True)
    grad_gate = (hidden_grad * up_in * slopes).astype(jnp.bfloat16)
    grad_up = (hidden_grad * activated).astype(jnp.bfloat16)
    return (grad_down, grad_gate, grad_up)


def solution(mesh):
    placed = (
        P("dp", "mp"),
        P("dp"),
        P("dp", None),
        P("dp", None),
        P("mp", "dp"),
        P("mp", "dp"),
        P("dp", "mp"),
    )
    return jax.shard_map(
        shards,
        mesh=mesh,
        in_specs=placed,
        out_specs=(P("dp", "mp"), P("mp", "dp"), P("mp", "dp")),
        check_vma=False,
    )
```

time: 393 us -> 302 us (0.77)
  blocking collectives: 82.5 us -> 0 us
  local copies, waits for them, and re-layouts: 110 us -> 41.9 us
  waiting for transfers between devices: 142 us -> 201 us
    all_gather x1 -> x0, blocking collectives: 82.5 us -> none  [shards(): lax.all_gather(route_count.astype(jnp.float32), 'dp', axis=0, tiled=True)]
    gather x7 -> x2, local copies, waits for them, and re-layouts: 83.9 us -> 16.1 us  [the longest x1 11 us: shards(): hidden_live = hidden_all[slot_of]]
    reduce_scatter x1, waiting for transfers between devices: 3.64 us -> 55.6 us  [shards(): lax.psum_scatter(partial_value, 'mp', scatter_dimension=0, tiled=True)]
    all_gather x1, waiting for transfers between devices: 70.9 us -> 122 us  [shards(): gathered = lax.all_gather(sent, 'dp', axis=0, tiled=True)]
    ppermute x3 -> x2, waiting for transfers between devices: 67.4 us -> 23 us  [the longest x1 22.9 us: mp_gather(): lax.ppermute(hidden, 'mp', [(i, (i + half) % n_mp) for i in range(n_mp)])]
  transfers between devices with their start and end apart: 5 -> 4, of which waited for: 5 -> 4; matrix products, arithmetic and copies ran while one was open for 25% -> 9% of each run, Pallas kernels for 0% -> 0%
where the time goes in v2:
time: 302 us; the launch traced here: 301 us
  waiting for transfers between devices  201 us (67%)
  local copies, waits for them, and re-layouts  41.9 us (14%)
  matrix products  20.4 us (7%)
  other arithmetic  20.2 us (7%)
  between operations  14.3 us (5%)
  starting transfers between devices  4.04 us (1%)
    all_gather x1, waiting for transfers between devices, shards(): gathered = lax.all_gather(sent, 'dp', axis=0, tiled=True)  122 us
    reduce_scatter x1, waiting for transfers between devices, shards(): lax.psum_scatter(partial_value, 'mp', scatter_dimension=0, tiled=True)  55.6 us
    ppermute x1, waiting for transfers between devices, mp_gather(): lax.ppermute(hidden, 'mp', [(i, (i + half) % n_mp) for i in range(n_mp)])  22.9 us
    gather x1, local copies, waits for them, and re-layouts, shards(): partial_value = jnp.where(live[:, None], partial_live[source], 0.0)  20.4 us
    gather x1, local copies, waits for them, and re-layouts, shards(): hidden_live = hidden_all[slot_of]  11 us
    dot_general x1, matrix products, shards(): lax.dot_general(hidden_live, everything, (((0,), (0,)), ((), ())), prefer...  10.6 us
    dot_general x1, matrix products, shards(): lax.dot_general(everything, down_weight, (((1,), (1,)), ((), ())), prefer...  9.82 us
  transfers between devices with their start and end apart: 4, of which 4 were waited for; matrix products, arithmetic and copies ran while one was open for 9% of the time, Pallas kernels for 0%

profile of v2, /device:TPU:1, one launch (start us, length us, event | category | flops | bytes accessed | tf_op | source)
XLA Modules:
  0.0 301.5 jit_solution(9117716242402274284)
XLA Ops:
  7.2 0.0 copy-start
  7.2 0.0 all-gather.2.cloned.1.call-start
  7.2 2.3 fusion.4
  9.6 0.0 copy-start.3
  9.6 0.0 copy-start.6
  9.6 0.0 copy-start.1
  9.6 0.0 copy-start.7
  9.6 2.5 collective-permute-start
  12.1 22.9 %collective-permute-done = bf16[1024,512]{1,0:T(8,128)(2,1)S(1)} collective-permute-done((bf16[1024,512]{1,0:T(8,128)(2,1)S(1)}, bf16[1024,512]{1,0:T(8,128)(2,1)S(1)}, u32[]{:S(2)}, u32[]{:S(2)}) %collective-permute-start) | collective-permute-done | bytes 1048608 | tf_op jit(solution)/shard_map/ppermute | solution.py:20
  35.0 0.0 copy-start.5
  35.0 0.0 copy-done.3
  35.0 0.0 copy-start.2
  35.0 1.5 pad_maximum_fusion.1
  36.5 0.2 copy-done.5
  36.7 1.3 collective-permute-start.1
  37.9 0.0 copy-done.6
  37.9 0.1 copy.17
  38.0 0.1 reduce-window.8
  38.1 0.1 reduce.2
  38.2 0.1 convert_reduce_fusion.1
  38.3 0.0 copy-done.1
  38.3 1.3 gather_fusion.1
  39.6 0.0 copy-done.7
  39.6 1.3 gather_fusion.3
  40.9 0.0 copy-done.2
  40.9 0.8 gather_fusion.2
  41.7 0.1 multiply_convert_fusion.1
  41.9 0.2 collective-permute-done.1
  42.0 3.7 %pad_maximum_fusion = bf16[4,1024,512]{2,1,0:T(8,128)(2,1)} fusion(bf16[2,1024,512]{2,1,0:T(8,128)(2,1)} %collective-permute-done.1, bf16[1,1024,512]{2,1,0:T(8,128)(2,1)} %bitcast.44, bf16[1,1024,512]{2,1,0:T(8,128)(2,1)} %bitcast.42), kind=kLoop, calls=%fused_computation.10 | loop fusion | flops 4194304 | bytes 8388608 | tf_op jit(solution)/shard_map/concatenate | solution.py:23
  45.8 5.0 %gather_fusion = bf16[4,1024,512]{2,1,0:T(8,128)(2,1)} fusion(bf16[4,1024,512]{2,1,0:T(8,128)(2,1)} %pad_maximum_fusion, s32[1024]{0:T(1024)S(1)} %pad_clamp_fusion.3), kind=kCustom, calls=%fused_computation | custom fusion | bytes 8388624 | tf_op jit(solution)/shard_map/jit(_take)/gather | solution.py:26
  50.8 0.8 fusion.13
  51.6 0.0 all-gather.2.cloned.1.call-update
  51.6 0.2 reduce-scatter.2.cloned.1.call-start
  51.8 122.0 %all-gather.2.cloned.1.call-done = bf16[2560,2176]{1,0:T(8,128)(2,1)} async-done(((bf16[80,2176]{1,0:T(8,128)(2,1)}), bf16[2560,2176]{1,0:T(8,128)(2,1)}) %all-gather.2.cloned.1.call-update) | async-done | bytes 11141136 | tf_op jit(solution)/shard_map/all_gather | solution.py:52
  173.8 0.8 slice.36
  174.7 0.1 copy.19
  174.8 0.2 reduce_window_sum.18
  175.0 0.1 add_bitcast_fusion
  175.1 0.1 copy.20
  175.1 0.2 iota_compare_fusion.1
  175.4 0.3 lt.89
  175.7 0.3 add_select_fusion
  176.0 0.3 select_n.111
  176.4 0.0 copy-done
  176.4 9.8 %fusion = f32[2560,512]{1,0:T(8,128)} fusion(bf16[512,2048]{1,0:T(8,128)(2,1)S(1)} %copy-done, bf16[2560,2176]{1,0:T(8,128)(2,1)} %all-gather.2.cloned.1.call-done), kind=kOutput, calls=%fused_computation.6 | convolution fusion | flops 5368709120 | bytes 17825792 | tf_op jit(solution)/shard_map/dot_general | solution.py:69
  186.2 20.4 %gather_fusion.5 = f32[4096,512]{1,0:T(8,128)} fusion(f32[2560,512]{1,0:T(8,128)} %fusion, s32[4096]{0:T(1024)S(1)} %broadcast_clamp_fusion), kind=kCustom, calls=%fused_computation.5 | custom fusion | bytes 16793600 | tf_op jit(solution)/shard_map/gather | solution.py:77
  206.7 5.9 %broadcast_select_fusion = f32[4096,512]{1,0:T(8,128)} fusion(f32[4096,512]{1,0:T(8,128)} %gather_fusion.5, pred[4096]{0:T(1024)(128)(4,1)S(1)} %lt.89), kind=kLoop, calls=%fused_computation.11 | loop fusion | flops 2097152 | bytes 16781312 | tf_op jit(solution)/shard_map/jit(_where)/select_n | solution.py:77
  212.6 0.0 reduce-scatter.2.cloned.1.call-update
  212.6 0.4 convert_reduce_fusion
  213.0 0.1 subtract_add_fusion
  213.0 0.1 add.163
  213.2 11.0 %gather_fusion.4 = bf16[2560,512]{1,0:T(8,128)(2,1)} fusion(bf16[4096,512]{1,0:T(8,128)(2,1)} %bitcast.40, s32[3072]{0:T(1024)S(1)} %pad_clamp_fusion), kind=kCustom, calls=%fused_computation.4 | custom fusion | bytes 5253120 | tf_op jit(solution)/shard_map/gather | solution.py:65
  224.2 0.0 copy-start.4
  224.2 10.6 %fusion.2 = f32[512,2048]{1,0:T(8,128)} fusion(bf16[2560,512]{1,0:T(8,128)(2,1)} %gather_fusion.4, bf16[2560,2176]{1,0:T(8,128)(2,1)} %all-gather.2.cloned.1.call-done), kind=kOutput, calls=%fused_computation.8 | convolution fusion | flops 5368709120 | bytes 17301504 | tf_op jit(solution)/shard_map/dot_general | solution.py:66
  234.8 55.6 %reduce-scatter.2.cloned.1.call-done = f32[1024,512]{1,0:T(8,128)} async-done(((f32[4096,512]{1,0:T(8,128)}), f32[1024,512]{1,0:T(8,128)}) %reduce-scatter.2.cloned.1.call-update) | async-done | bytes 2097168 | tf_op jit(solution)/shard_map/reduce_scatter | solution.py:78
  290.5 0.0 copy-done.4
  290.5 4.2 %multiply_convert_fusion = (bf16[1024,512]{1,0:T(8,128)(2,1)}, bf16[1024,512]{1,0:T(8,128)(2,1)}) fusion(f32[1024,512]{1,0:T(8,128)} %reduce-scatter.2.cloned.1.call-done, bf16[1024,512]{1,0:T(8,128)(2,1)} %param.13, bf16[1024,512]{1,0:T(8,128)(2,1)S(1)} %copy-done.4), kind=kLoop, calls=%fused_computation.26 | loop fusion | flops 7864320 | bytes 6291456 | tf_op jit(solution)/shard_map/convert_element_type | solution.py:80
  (15 shorter events, 0.1 us)
Async XLA Ops:
  7.2 169.2 %copy-start = (bf16[512,2048]{1,0:T(8,128)(2,1)S(1)}, bf16[512,2048]{1,0:T(8,128)(2,1)}, u32[]{:S(2)}) copy-start(bf16[512,2048]{1,0:T(8,128)(2,1)} %param.15) | copy-start | bytes 6291460
  7.2 166.7 %all-gather.2.cloned.1.call-start = ((), (), s32[]{:S(2)}) async-start(), calls=%async_computation.1 | async-start | bytes 11489280 | tf_op jit(solution)/shard_map/all_gather | solution.py:52
  9.6 25.5 %copy-start.3 = (bf16[1024,512]{1,0:T(8,128)(2,1)}, bf16[1024,512]{1,0:T(8,128)(2,1)S(1)}, u32[]{:S(2)}) copy-start(bf16[1024,512]{1,0:T(8,128)(2,1)S(1)} %fusion.4) | copy-start | bytes 3145732
  9.6 28.3 %copy-start.6 = (s32[1,32]{1,0:T(1,128)S(1)}, s32[1,32]{1,0:T(1,128)}, u32[]{:S(2)}) copy-start(s32[1,32]{1,0:T(1,128)} %param.12) | copy-start | bytes 388
  9.6 28.7 %copy-start.1 = (s32[1,144]{1,0:T(1,128)S(1)}, s32[1,144]{1,0:T(1,128)}, u32[]{:S(2)}) copy-start(s32[1,144]{1,0:T(1,128)} %param.11) | copy-start | bytes 1732
  9.6 30.0 %copy-start.7 = (s32[144]{0:T(256)S(1)}, s32[144]{0:T(256)}, u32[]{:S(2)}) copy-start(s32[144]{0:T(256)} %param.10) | copy-start | bytes 1732
  9.6 25.4 %collective-permute-start = (bf16[1024,512]{1,0:T(8,128)(2,1)S(1)}, bf16[1024,512]{1,0:T(8,128)(2,1)S(1)}, u32[]{:S(2)}, u32[]{:S(2)}) collective-permute-start(bf16[1024,512]{1,0:T(8,128)(2,1)S(1)} %fusion.4), channel_id=1, source_target_pairs={{0,2},{1,3},{2,0},{3,1},{4,6},{5,7},{6,4},{7,5},{8,10},{9,11},{10,... | collective-permute-start | bytes 3145736 | tf_op jit(solution)/shard_map/ppermute | solution.py:20
  35.0 1.7 copy-start.5
  35.0 5.9 %copy-start.2 = (bf16[144,2048]{1,0:T(8,128)(2,1)S(1)}, bf16[144,2048]{1,0:T(8,128)(2,1)}, u32[]{:S(2)}) copy-start(bf16[144,2048]{1,0:T(8,128)(2,1)} %param.9) | copy-start | bytes 1769476
  36.7 5.4 %collective-permute-start.1 = (bf16[2,1024,512]{2,1,0:T(8,128)(2,1)}, bf16[2,1024,512]{2,1,0:T(8,128)(2,1)}, u32[]{:S(2)}, u32[]{:S(2)}) collective-permute-start(bf16[2,1024,512]{2,1,0:T(8,128)(2,1)} %pad_maximum_fusion.1), channel_id=1, source_target_pairs={{0,1},{1,0},{2,3},{3,2},{4,5},{5,4},{6,7},{7,6},{8,9},{9,8},{10,11... | collective-permute-start | bytes 6291464 | tf_op jit(solution)/shard_map/ppermute | solution.py:22
  51.6 238.9 %reduce-scatter.2.cloned.1.call-start = ((), (), s32[]{:S(2)}) async-start(), calls=%async_computation.2 | async-start | bytes 10485760 | tf_op jit(solution)/shard_map/reduce_scatter | solution.py:78
  224.2 66.2 %copy-start.4 = (bf16[1024,512]{1,0:T(8,128)(2,1)S(1)}, bf16[1024,512]{1,0:T(8,128)(2,1)}, u32[]{:S(2)}) copy-start(bf16[1024,512]{1,0:T(8,128)(2,1)} %param.14) | copy-start | bytes 3145732
Sparse Core Ops, SparseCore 0:
  51.7 122.1 all-gather.1
  212.7 77.7 reduce-scatter.1

commit v3 on v2

--- a/solution.py
+++ b/solution.py
@@ -35,7 +35,6 @@
     up_in = up_pre.astype(jnp.float32)
     activated, slopes = silu_parts(gate_in)
     hidden = (activated * up_in).astype(jnp.bfloat16)
-    hidden_all = mp_gather(hidden)
 
     own = route_count[0]
     own_end = jnp.cumsum(own)
@@ -47,9 +46,11 @@
     weights = advantage.astype(jnp.float32) * (1.0 / 4096.0)
     scaled = (sample_grad[picked].astype(jnp.float32) * weights[picked][:, None]).astype(jnp.bfloat16)
     info = jnp.zeros((LIVE, INFO), jnp.bfloat16).at[0, :learners].set(own.astype(jnp.bfloat16))
-    hidden_all, scaled = lax.optimization_barrier((hidden_all, scaled))
     sent = jnp.concatenate([scaled, info], axis=1)
+    sent, hidden = lax.optimization_barrier((sent, hidden))
     gathered = lax.all_gather(sent, "dp", axis=0, tiled=True)
+    hidden_all = mp_gather(hidden)
+    gathered, hidden_all = lax.optimization_barrier((gathered, hidden_all))
     everything = gathered[:, :d_cols]
     counts = gathered.reshape(learners, LIVE, d_cols + INFO)[:, 0, d_cols:d_cols + learners]
     counts = counts.astype(jnp.int32)
@@ -74,8 +75,22 @@
     live = (lane[None, None, :] < counts.T[:, :, None]).reshape(-1)
     first = jnp.arange(learners, dtype=jnp.int32)[None, :] * LIVE + starts.T
     source = jnp.where(live, (first[:, :, None] + lane[None, None, :]).reshape(-1), 0)
-    partial_value = jnp.where(live[:, None], partial_live[source], 0.0)
-    hidden_grad = lax.psum_scatter(partial_value, "mp", scatter_dimension=0, tiled=True)
+
+    me = lax.axis_index("mp")
+    n_mp = lax.axis_size("mp")
+    rows_per = hidden.shape[0]
+
+    def partial_block(b):
+        at = b * rows_per
+        src = lax.dynamic_slice_in_dim(source, at, rows_per)
+        keep = lax.dynamic_slice_in_dim(live, at, rows_per)
+        return jnp.where(keep[:, None], partial_live[src], 0.0)
+
+    to_core = jnp.stack([partial_block(me ^ 3), partial_block(me ^ 1)])
+    from_core = lax.ppermute(to_core, "mp", [(i, i ^ 1) for i in range(n_mp)])
+    to_chip = partial_block(me ^ 2) + from_core[0]
+    from_chip = lax.ppermute(to_chip, "mp", [(i, i ^ 2) for i in range(n_mp)])
+    hidden_grad = (partial_block(me) + from_core[1]) + from_chip
     grad_gate = (hidden_grad * up_in * slopes).astype(jnp.bfloat16)
     grad_up = (hidden_grad * activated).astype(jnp.bfloat16)
     return (grad_down, grad_gate, grad_up)

time: 302 us -> 245 us (0.81)
  waiting for transfers between devices: 201 us -> 130 us
  local copies, waits for them, and re-layouts: 41.9 us -> 49.5 us
  other arithmetic: 20.2 us -> 25.1 us
    reduce_scatter x1 -> x0, waiting for transfers between devices: 55.6 us -> none  [shards(): lax.psum_scatter(partial_value, 'mp', scatter_dimension=0, tiled=True)]
    all_gather x1, waiting for transfers between devices: 122 us -> 81.8 us  [shards(): gathered = lax.all_gather(sent, 'dp', axis=0, tiled=True)]
    ppermute x0 -> x2, waiting for transfers between devices: none -> 18.7 us  [the longest x1 18.1 us: shards(): from_chip = lax.ppermute(to_chip, 'mp', [(i, i ^ 2) for i in range(n_mp)])]
    gather x1 -> x4, local copies, waits for them, and re-layouts: 20.4 us -> 27.3 us  [partial_block(): return jnp.where(keep[:, None], partial_live[src], 0.0)]
    ppermute x1, waiting for transfers between devices: 0.17 us -> 4.09 us  [mp_gather(): near = lax.ppermute(pair, 'mp', [(i, i ^ 1) for i in range(n_mp)])]
    select_n x2 -> x1, other arithmetic: 5.89 us -> 1.99 us  [partial_block(): return jnp.where(keep[:, None], partial_live[src], 0.0)]
    add x0 -> x2, other arithmetic: none -> 3.37 us  [the longest x1 3.17 us: shards(): to_chip = partial_block(me ^ 2) + from_core[0]]
  transfers between devices with their start and end apart: 4 -> 5, of which waited for: 4 -> 5; matrix products, arithmetic and copies ran while one was open for 9% -> 19% of each run, Pallas kernels for 0% -> 0%
where the time goes in v3:
time: 245 us
  waiting for transfers between devices  130 us (53%)
  local copies, waits for them, and re-layouts  49.5 us (20%)
  other arithmetic  25.1 us (10%)
  matrix products  20.3 us (8%)
  between operations  14.2 us (6%)
  starting transfers between devices  5.49 us (2%)
    all_gather x1, waiting for transfers between devices, shards(): gathered = lax.all_gather(sent, 'dp', axis=0, tiled=True)  81.8 us
    gather x4, local copies, waits for them, and re-layouts, partial_block(): return jnp.where(keep[:, None], partial_live[src], 0.0)  27.3 us
    ppermute x1, waiting for transfers between devices, mp_gather(): lax.ppermute(hidden, 'mp', [(i, (i + half) % n_mp) for i in range(n_mp)])  25.4 us
    ppermute x1, waiting for transfers between devices, shards(): from_chip = lax.ppermute(to_chip, 'mp', [(i, i ^ 2) for i in range(n_mp)])  18.1 us
    gather x1, local copies, waits for them, and re-layouts, shards(): hidden_live = hidden_all[slot_of]  11.1 us
    dot_general x1, matrix products, shards(): lax.dot_general(hidden_live, everything, (((0,), (0,)), ((), ())), prefer...  10.5 us
    dot_general x1, matrix products, shards(): lax.dot_general(everything, down_weight, (((1,), (1,)), ((), ())), prefer...  9.81 us
    gather x1, local copies, waits for them, and re-layouts, mp_gather(): jnp.take(held, where, axis=0, mode='clip')  4.95 us
  transfers between devices with their start and end apart: 5, of which 5 were waited for; matrix products, arithmetic and copies ran while one was open for 19% of the time, Pallas kernels for 0%

profile of v3, /device:TPU:1, one launch (start us, length us, event | category | flops | bytes accessed | tf_op | source)
XLA Modules:
  0.0 244.7 jit_solution(3542128883145040271)
XLA Ops:
  7.2 0.0 copy-start
  7.2 0.0 copy-start.2
  7.2 0.0 all-gather.2.cloned.1.call-start
  7.2 0.8 convert_element_type.45
  8.1 0.7 convert_multiply_fusion.4
  8.8 0.7 copy.17
  9.5 0.1 reduce-window.8
  9.6 0.1 reduce.2
  9.7 0.7 convert_reduce_fusion.1
  10.4 1.6 gather_fusion
  12.1 1.3 gather_fusion.2
  13.4 0.0 copy-done.2
  13.4 0.8 gather_fusion.1
  14.2 0.1 multiply_convert_fusion.1
  14.3 0.8 fusion.16
  15.1 2.2 fusion.4
  17.2 0.0 all-gather.2.cloned.1.call-update
  17.3 2.5 %collective-permute-start = (bf16[1024,512]{1,0:T(8,128)(2,1)S(1)}, bf16[1024,512]{1,0:T(8,128)(2,1)S(1)}, u32[]{:S(2)}, u32[]{:S(2)}) collective-permute-start(bf16[1024,512]{1,0:T(8,128)(2,1)S(1)} %fusion.4), channel_id=1, source_target_pairs={{0,2},{1,3},{2,0},{3,1},{4,6},{5,7},{6,4},{7,5},{8,10},{9,11},{10,... | collective-permute-start | bytes 3145736 | tf_op jit(solution)/shard_map/ppermute | solution.py:20
  19.8 25.4 %collective-permute-done = bf16[1024,512]{1,0:T(8,128)(2,1)S(1)} collective-permute-done((bf16[1024,512]{1,0:T(8,128)(2,1)S(1)}, bf16[1024,512]{1,0:T(8,128)(2,1)S(1)}, u32[]{:S(2)}, u32[]{:S(2)}) %collective-permute-start) | collective-permute-done | bytes 1048608 | tf_op jit(solution)/shard_map/ppermute | solution.py:20
  45.3 0.0 copy-start.5
  45.3 1.6 pad_maximum_fusion.2
  46.9 0.0 copy-done.5
  46.9 1.1 collective-permute-start.1
  48.1 4.1 %collective-permute-done.1 = bf16[2,1024,512]{2,1,0:T(8,128)(2,1)} collective-permute-done((bf16[2,1024,512]{2,1,0:T(8,128)(2,1)}, bf16[2,1024,512]{2,1,0:T(8,128)(2,1)}, u32[]{:S(2)}, u32[]{:S(2)}) %collective-permute-start.1) | collective-permute-done | bytes 2097184 | tf_op jit(solution)/shard_map/ppermute | solution.py:22
  52.2 3.6 %pad_maximum_fusion = bf16[4,1024,512]{2,1,0:T(8,128)(2,1)} fusion(bf16[2,1024,512]{2,1,0:T(8,128)(2,1)} %collective-permute-done.1, bf16[1,1024,512]{2,1,0:T(8,128)(2,1)} %bitcast.58, bf16[1,1024,512]{2,1,0:T(8,128)(2,1)S(1)} %bitcast.56), kind=kLoop, calls=%fused_computation.13 | loop fusion | flops 4194304 | bytes 8388608 | tf_op jit(solution)/shard_map/concatenate | solution.py:23
  55.8 5.0 %gather_fusion.3 = bf16[4,1024,512]{2,1,0:T(8,128)(2,1)} fusion(bf16[4,1024,512]{2,1,0:T(8,128)(2,1)} %pad_maximum_fusion, s32[1024]{0:T(1024)S(1)} %pad_clamp_fusion.1), kind=kCustom, calls=%fused_computation.3 | custom fusion | bytes 8388624 | tf_op jit(solution)/shard_map/jit(_take)/gather | solution.py:26
  60.7 81.8 %all-gather.2.cloned.1.call-done = bf16[2560,2176]{1,0:T(8,128)(2,1)} async-done(((bf16[80,2176]{1,0:T(8,128)(2,1)}), bf16[2560,2176]{1,0:T(8,128)(2,1)}) %all-gather.2.cloned.1.call-update) | async-done | bytes 11141136 | tf_op jit(solution)/shard_map/all_gather | solution.py:51
  142.6 0.8 slice.50
  143.4 0.1 copy.19
  143.5 0.2 reduce_window_sum.18
  143.7 0.1 add_bitcast_fusion
  143.8 0.1 copy.20
  143.8 0.2 iota_compare_fusion.1
  144.1 0.3 lt.95
  144.4 0.2 iota_add_fusion
  144.6 0.3 add.189
  144.9 0.0 copy-done
  144.9 9.8 %fusion = f32[2560,512]{1,0:T(8,128)} fusion(bf16[512,2048]{1,0:T(8,128)(2,1)S(1)} %copy-done, bf16[2560,2176]{1,0:T(8,128)(2,1)} %all-gather.2.cloned.1.call-done), kind=kOutput, calls=%fused_computation.9 | convolution fusion | flops 5368709120 | bytes 17825792 | tf_op jit(solution)/shard_map/dot_general | solution.py:70
  154.8 6.5 %gather_fusion.7 = f32[1024,512]{1,0:T(8,128)S(1)} fusion(f32[2560,512]{1,0:T(8,128)} %fusion, s32[1024]{0:T(1024)S(1)} %get-tuple-element.31), kind=kCustom, calls=%fused_computation.7 | custom fusion | bytes 4198400 | tf_op jit(solution)/shard_map/gather | solution.py:87
  161.3 7.8 %gather_fusion.6 = f32[1024,512]{1,0:T(8,128)} fusion(f32[2560,512]{1,0:T(8,128)} %fusion, s32[1024]{0:T(1024)S(1)} %get-tuple-element.32), kind=kCustom, calls=%fused_computation.6 | custom fusion | bytes 4198400 | tf_op jit(solution)/shard_map/gather | solution.py:87
  169.0 2.0 bitcast_select_fusion
  171.0 2.5 %pad_maximum_fusion.1 = f32[2,1024,512]{2,1,0:T(8,128)} fusion(f32[1,1024,512]{2,1,0:T(8,128)S(1)} %get-tuple-element.39, f32[1,1024,512]{2,1,0:T(8,128)S(1)} %get-tuple-element.40), kind=kLoop, calls=%fused_computation.14 | loop fusion | flops 1048576 | bytes 8388608 | tf_op jit(solution)/shard_map/stack | solution.py:89
  173.5 1.4 collective-permute-start.2
  174.9 6.5 %gather_fusion.8 = f32[1024,512]{1,0:T(8,128)S(1)} fusion(f32[2560,512]{1,0:T(8,128)} %fusion, s32[1024]{0:T(1024)S(1)} %get-tuple-element.30), kind=kCustom, calls=%fused_computation.8 | custom fusion | bytes 4198400 | tf_op jit(solution)/shard_map/gather | solution.py:87
  181.4 0.6 collective-permute-done.2
  182.0 3.2 %fusion.12 = f32[1024,512]{1,0:T(8,128)} fusion(f32[2,1024,512]{2,1,0:T(8,128)} %collective-permute-done.2, f32[1024,512]{1,0:T(8,128)S(1)} %gather_fusion.8, pred[1024]{0:T(1024)(128)(4,1)S(1)} %get-tuple-element.36), kind=kLoop, calls=%fused_computation.29 | loop fusion | flops 1048576 | bytes 6292480 | tf_op jit(solution)/shard_map/add | solution.py:91
  185.2 0.4 collective-permute-start.3
  185.5 0.4 convert_reduce_fusion
  185.9 0.1 subtract_add_fusion
  186.0 0.1 add.180
  186.1 6.5 %gather_fusion.5 = f32[1024,512]{1,0:T(8,128)S(1)} fusion(f32[2560,512]{1,0:T(8,128)} %fusion, s32[1024]{0:T(1024)S(1)} %get-tuple-element.29), kind=kCustom, calls=%fused_computation.5 | custom fusion | bytes 4198400 | tf_op jit(solution)/shard_map/gather | solution.py:87
  192.7 11.1 %gather_fusion.4 = bf16[2560,512]{1,0:T(8,128)(2,1)} fusion(bf16[4096,512]{1,0:T(8,128)(2,1)} %bitcast.54, s32[3072]{0:T(1024)S(1)} %pad_clamp_fusion), kind=kCustom, calls=%fused_computation.4 | custom fusion | bytes 5253120 | tf_op jit(solution)/shard_map/gather | solution.py:66
  203.7 0.0 copy-start.3
  203.7 10.5 %fusion.2 = f32[512,2048]{1,0:T(8,128)} fusion(bf16[2560,512]{1,0:T(8,128)(2,1)} %gather_fusion.4, bf16[2560,2176]{1,0:T(8,128)(2,1)} %all-gather.2.cloned.1.call-done), kind=kOutput, calls=%fused_computation.11 | convolution fusion | flops 5368709120 | bytes 17301504 | tf_op jit(solution)/shard_map/dot_general | solution.py:67
  214.2 18.1 %collective-permute-done.3 = f32[1024,512]{1,0:T(8,128)} collective-permute-done((f32[1024,512]{1,0:T(8,128)}, f32[1024,512]{1,0:T(8,128)}, u32[]{:S(2)}, u32[]{:S(2)}) %collective-permute-start.3) | collective-permute-done | bytes 2097184 | tf_op jit(solution)/shard_map/ppermute | solution.py:92
  232.3 0.0 copy-done.3
  232.3 0.0 copy-start.4
  232.3 3.7 %multiply_convert_fusion = (bf16[1024,512]{1,0:T(8,128)(2,1)}, f32[1024,512]{1,0:T(8,128)S(1)}) fusion(bf16[1024,512]{1,0:T(8,128)(2,1)S(1)} %copy-done.3, f32[1024,512]{1,0:T(8,128)} %collective-permute-done.3, f32[2,1024,512]{2,1,0:T(8,128)} %collective-permute-done.2, f32[1024,512]{1,0:T(8,128)S(1)} %gather_fusion.5, pred[1024]{0:T(1024)(128)(4,1)S(1)} %get-tuple-element.35), kind=kLoop, calls=%fused_computation.36 | loop fusion | flops 5242880 | bytes 10486784 | tf_op jit(solution)/shard_map/convert_element_type | solution.py:95
  236.0 0.0 copy-start.1
  236.0 0.0 copy-done.4
  236.0 1.9 fusion.6
  237.9 0.0 copy-done.1
  (14 shorter events, 0.2 us)
Async XLA Ops:
  7.2 137.8 %copy-start = (bf16[512,2048]{1,0:T(8,128)(2,1)S(1)}, bf16[512,2048]{1,0:T(8,128)(2,1)}, u32[]{:S(2)}) copy-start(bf16[512,2048]{1,0:T(8,128)(2,1)} %param.15) | copy-start | bytes 6291460
  7.2 6.2 %copy-start.2 = (bf16[144,2048]{1,0:T(8,128)(2,1)S(1)}, bf16[144,2048]{1,0:T(8,128)(2,1)}, u32[]{:S(2)}) copy-start(bf16[144,2048]{1,0:T(8,128)(2,1)} %param.9) | copy-start | bytes 1769476
  7.2 135.4 %all-gather.2.cloned.1.call-start = ((), (), s32[]{:S(2)}) async-start(), calls=%async_computation | async-start | bytes 11489280 | tf_op jit(solution)/shard_map/all_gather | solution.py:51
  17.3 28.0 %collective-permute-start = (bf16[1024,512]{1,0:T(8,128)(2,1)S(1)}, bf16[1024,512]{1,0:T(8,128)(2,1)S(1)}, u32[]{:S(2)}, u32[]{:S(2)}) collective-permute-start(bf16[1024,512]{1,0:T(8,128)(2,1)S(1)} %fusion.4), channel_id=1, source_target_pairs={{0,2},{1,3},{2,0},{3,1},{4,6},{5,7},{6,4},{7,5},{8,10},{9,11},{10,... | collective-permute-start | bytes 3145736 | tf_op jit(solution)/shard_map/ppermute | solution.py:20
  45.3 1.7 copy-start.5
  46.9 5.3 %collective-permute-start.1 = (bf16[2,1024,512]{2,1,0:T(8,128)(2,1)}, bf16[2,1024,512]{2,1,0:T(8,128)(2,1)}, u32[]{:S(2)}, u32[]{:S(2)}) collective-permute-start(bf16[2,1024,512]{2,1,0:T(8,128)(2,1)} %pad_maximum_fusion.2), channel_id=1, source_target_pairs={{0,1},{1,0},{2,3},{3,2},{4,5},{5,4},{6,7},{7,6},{8,9},{9,8},{10,11... | collective-permute-start | bytes 6291464 | tf_op jit(solution)/shard_map/ppermute | solution.py:22
  173.5 8.5 %collective-permute-start.2 = (f32[2,1024,512]{2,1,0:T(8,128)}, f32[2,1024,512]{2,1,0:T(8,128)}, u32[]{:S(2)}, u32[]{:S(2)}) collective-permute-start(f32[2,1024,512]{2,1,0:T(8,128)} %pad_maximum_fusion.1), channel_id=1, source_target_pairs={{0,1},{1,0},{2,3},{3,2},{4,5},{5,4},{6,7},{7,6},{8,9},{9,8},{10,11... | collective-permute-start | bytes 12582920 | tf_op jit(solution)/shard_map/ppermute | solution.py:90
  185.2 47.1 %collective-permute-start.3 = (f32[1024,512]{1,0:T(8,128)}, f32[1024,512]{1,0:T(8,128)}, u32[]{:S(2)}, u32[]{:S(2)}) collective-permute-start(f32[1024,512]{1,0:T(8,128)} %fusion.12), channel_id=1, source_target_pairs={{0,2},{1,3},{2,0},{3,1},{4,6},{5,7},{6,4},{7,5},{8,10},{9,11},{10,... | collective-permute-start | bytes 6291464 | tf_op jit(solution)/shard_map/ppermute | solution.py:92
  203.7 28.6 %copy-start.3 = (bf16[1024,512]{1,0:T(8,128)(2,1)S(1)}, bf16[1024,512]{1,0:T(8,128)(2,1)}, u32[]{:S(2)}) copy-start(bf16[1024,512]{1,0:T(8,128)(2,1)} %param.13) | copy-start | bytes 3145732
  232.3 3.7 %copy-start.4 = (bf16[1024,512]{1,0:T(8,128)(2,1)S(1)}, bf16[1024,512]{1,0:T(8,128)(2,1)}, u32[]{:S(2)}) copy-start(bf16[1024,512]{1,0:T(8,128)(2,1)} %param.14) | copy-start | bytes 3145732
  236.0 1.9 copy-start.1
Sparse Core Ops, SparseCore 0:
  17.4 125.1 all-gather.1

commit v4 on v3

--- a/solution.py
+++ b/solution.py
@@ -48,11 +48,13 @@
     info = jnp.zeros((LIVE, INFO), jnp.bfloat16).at[0, :learners].set(own.astype(jnp.bfloat16))
     sent = jnp.concatenate([scaled, info], axis=1)
     sent, hidden = lax.optimization_barrier((sent, hidden))
-    gathered = lax.all_gather(sent, "dp", axis=0, tiled=True)
+    half = d_cols // 2
+    left = lax.all_gather(sent[:, :half], "dp", axis=0, tiled=True)
+    right = lax.all_gather(sent[:, half:], "dp", axis=0, tiled=True)
     hidden_all = mp_gather(hidden)
-    gathered, hidden_all = lax.optimization_barrier((gathered, hidden_all))
-    everything = gathered[:, :d_cols]
-    counts = gathered.reshape(learners, LIVE, d_cols + INFO)[:, 0, d_cols:d_cols + learners]
+    left, right, hidden_all = lax.optimization_barrier((left, right, hidden_all))
+    right_rows = right[:, :half]
+    counts = right.reshape(learners, LIVE, half + INFO)[:, 0, half:half + learners]
     counts = counts.astype(jnp.int32)
 
     ends = jnp.cumsum(counts, axis=1)
@@ -64,12 +66,18 @@
     slot_of = (m_of * SLOTS + sender * capacity + c_of).reshape(-1)
 
     hidden_live = hidden_all[slot_of]
-    grad_down = lax.dot_general(
-        hidden_live, everything, (((0,), (0,)), ((), ())), preferred_element_type=jnp.float32
+    by_rows = (((0,), (0,)), ((), ()))
+    grad_down = jnp.concatenate(
+        [
+            lax.dot_general(hidden_live, left, by_rows, preferred_element_type=jnp.float32),
+            lax.dot_general(hidden_live, right_rows, by_rows, preferred_element_type=jnp.float32),
+        ],
+        axis=1,
     )
+    by_cols = (((1,), (1,)), ((), ()))
     partial_live = lax.dot_general(
-        everything, down_weight, (((1,), (1,)), ((), ())), preferred_element_type=jnp.float32
-    )
+        left, down_weight[:, :half], by_cols, preferred_element_type=jnp.float32
+    ) + lax.dot_general(right_rows, down_weight[:, half:], by_cols, preferred_element_type=jnp.float32)
 
     lane = jnp.arange(capacity, dtype=jnp.int32)
     live = (lane[None, None, :] < counts.T[:, :, None]).reshape(-1)
@@ -88,9 +96,9 @@
 
     to_core = jnp.stack([partial_block(me ^ 3), partial_block(me ^ 1)])
     from_core = lax.ppermute(to_core, "mp", [(i, i ^ 1) for i in range(n_mp)])
-    to_chip = partial_block(me ^ 2) + from_core[0]
+    to_chip = (partial_block(me ^ 2) + from_core[0]).astype(jnp.bfloat16)
     from_chip = lax.ppermute(to_chip, "mp", [(i, i ^ 2) for i in range(n_mp)])
-    hidden_grad = (partial_block(me) + from_core[1]) + from_chip
+    hidden_grad = (partial_block(me) + from_core[1]) + from_chip.astype(jnp.float32)
     grad_gate = (hidden_grad * up_in * slopes).astype(jnp.bfloat16)
     grad_up = (hidden_grad * activated).astype(jnp.bfloat16)
     return (grad_down, grad_gate, grad_up)

time: 245 us -> 302 us (1.23)
  waiting for transfers between devices: 130 us -> 184 us
    all_gather x1 -> x2, waiting for transfers between devices: 81.8 us -> 139 us  [the longest x1 91.5 us: shards(): right = lax.all_gather(sent[:, half:], 'dp', axis=0, tiled=True)]
    add x1 -> x0, other arithmetic: 3.17 us -> none  [shards(): to_chip = partial_block(me ^ 2) + from_core[0]]
    dot_general x2 -> x4, matrix products: 20.3 us -> 20.8 us  [the longest x1 5.8 us: shards(): lax.dot_general(hidden_live, left, by_rows, preferred_element_type=jnp.fl...]
  transfers between devices with their start and end apart: 5 -> 6, of which waited for: 5 -> 5; matrix products, arithmetic and copies ran while one was open for 19% -> 17% of each run, Pallas kernels for 0% -> 0%
where the time goes in v4:
time: 302 us; the launch traced here: 301 us
  waiting for transfers between devices  184 us (61%)
  local copies, waits for them, and re-layouts  52.4 us (17%)
  other arithmetic  23.8 us (8%)
  matrix products  20.8 us (7%)
  between operations  14.3 us (5%)
  starting transfers between devices  6.27 us (2%)
    all_gather x1, waiting for transfers between devices, shards(): right = lax.all_gather(sent[:, half:], 'dp', axis=0, tiled=True)  91.5 us
    all_gather x1, waiting for transfers between devices, shards(): left = lax.all_gather(sent[:, :half], 'dp', axis=0, tiled=True)  47 us
    gather x4, local copies, waits for them, and re-layouts, partial_block(): return jnp.where(keep[:, None], partial_live[src], 0.0)  28.6 us
    ppermute x1, waiting for transfers between devices, mp_gather(): lax.ppermute(hidden, 'mp', [(i, (i + half) % n_mp) for i in range(n_mp)])  24 us
    ppermute x1, waiting for transfers between devices, shards(): from_chip = lax.ppermute(to_chip, 'mp', [(i, i ^ 2) for i in range(n_mp)])  16.9 us
    gather x1, local copies, waits for them, and re-layouts, shards(): hidden_live = hidden_all[slot_of]  11.1 us
  transfers between devices with their start and end apart: 6, of which 5 were waited for; matrix products, arithmetic and copies ran while one was open for 17% of the time, Pallas kernels for 0%

profile of v4, /device:TPU:1, one launch (start us, length us, event | category | flops | bytes accessed | tf_op | source)
XLA Modules:
  0.0 301.2 jit_solution(5286809468234595250)
XLA Ops:
  7.2 0.0 copy-start
  7.2 0.0 all-gather.3.cloned.1.call-start
  7.2 0.7 convert_element_type.51
  7.9 0.7 convert_multiply_fusion.4
  8.6 0.7 copy.17
  9.4 0.1 reduce-window.8
  9.4 0.1 reduce.2
  9.5 0.7 convert_reduce_fusion.1
  10.3 1.6 gather_fusion
  12.0 1.3 gather_fusion.2
  13.2 0.0 copy-start.3
  13.3 0.8 gather_fusion.1
  14.0 0.1 multiply_convert_fusion.1
  14.2 0.3 copy-done.3
  14.5 1.9 fusion.3
  16.3 0.7 slice.40
  17.0 0.0 all-gather.3.cloned.1.call-update
  17.0 0.0 all-gather.5.cloned.1.call-start
  17.1 0.7 slice.41
  17.8 0.0 all-gather.5.cloned.1.call-update
  17.8 2.5 collective-permute-start
  20.3 24.0 %collective-permute-done = bf16[1024,512]{1,0:T(8,128)(2,1)S(1)} collective-permute-done((bf16[1024,512]{1,0:T(8,128)(2,1)S(1)}, bf16[1024,512]{1,0:T(8,128)(2,1)S(1)}, u32[]{:S(2)}, u32[]{:S(2)}) %collective-permute-start) | collective-permute-done | bytes 1048608 | tf_op jit(solution)/shard_map/ppermute | solution.py:20
  44.4 1.5 pad_maximum_fusion.3
  45.9 1.3 collective-permute-start.1
  47.2 4.1 %collective-permute-done.1 = bf16[2,1024,512]{2,1,0:T(8,128)(2,1)} collective-permute-done((bf16[2,1024,512]{2,1,0:T(8,128)(2,1)}, bf16[2,1024,512]{2,1,0:T(8,128)(2,1)}, u32[]{:S(2)}, u32[]{:S(2)}) %collective-permute-start.1) | collective-permute-done | bytes 2097184 | tf_op jit(solution)/shard_map/ppermute | solution.py:22
  51.3 3.6 %pad_maximum_fusion = bf16[4,1024,512]{2,1,0:T(8,128)(2,1)} fusion(bf16[2,1024,512]{2,1,0:T(8,128)(2,1)} %collective-permute-done.1, bf16[1,1024,512]{2,1,0:T(8,128)(2,1)S(1)} %bitcast.65, bf16[1,1024,512]{2,1,0:T(8,128)(2,1)S(1)} %bitcast.63), kind=kLoop, calls=%fused_computation.13 | loop fusion | flops 4194304 | bytes 8388608 | tf_op jit(solution)/shard_map/concatenate | solution.py:23
  54.9 5.0 %gather_fusion.3 = bf16[4,1024,512]{2,1,0:T(8,128)(2,1)} fusion(bf16[4,1024,512]{2,1,0:T(8,128)(2,1)} %pad_maximum_fusion, s32[1024]{0:T(1024)S(1)} %pad_clamp_fusion.1), kind=kCustom, calls=%fused_computation.3 | custom fusion | bytes 8388624 | tf_op jit(solution)/shard_map/jit(_take)/gather | solution.py:26
  59.8 47.0 %all-gather.3.cloned.1.call-done = bf16[2560,1024]{1,0:T(8,128)(2,1)} async-done(((bf16[80,1024]{1,0:T(8,128)(2,1)}), bf16[2560,1024]{1,0:T(8,128)(2,1)}) %all-gather.3.cloned.1.call-update) | async-done | bytes 5242896 | tf_op jit(solution)/shard_map/all_gather | solution.py:52
  106.8 91.5 %all-gather.5.cloned.1.call-done = bf16[2560,1152]{1,0:T(8,128)(2,1)} async-done(((bf16[80,1152]{1,0:T(8,128)(2,1)}), bf16[2560,1152]{1,0:T(8,128)(2,1)}) %all-gather.5.cloned.1.call-update) | async-done | bytes 5898256 | tf_op jit(solution)/shard_map/all_gather | solution.py:53
  198.4 0.8 slice.66
  199.2 0.1 copy.19
  199.3 0.2 reduce_window_sum.18
  199.5 0.1 add_bitcast_fusion
  199.6 0.1 copy.20
  199.6 0.2 iota_compare_fusion.1
  199.9 0.3 lt.95
  200.2 0.2 iota_add_fusion
  200.4 0.0 slice-start
  200.4 0.3 add.193
  200.8 0.0 slice-start.1
  200.8 0.0 copy-start.7
  200.8 5.4 %fusion.16 = f32[2560,512]{1,0:T(8,128)S(1)} fusion(bf16[2560,1024]{1,0:T(8,128)(2,1)} %all-gather.3.cloned.1.call-done, bf16[512,2048]{1,0:T(8,128)(2,1)} %param.15), kind=kOutput, calls=%fused_computation.40 | convolution fusion | flops 2684354560 | bytes 11534336 | tf_op jit(solution)/shard_map/dot_general | solution.py:78
  206.2 4.8 %convolution_add_fusion = f32[2560,512]{1,0:T(8,128)} fusion(f32[2560,512]{1,0:T(8,128)S(1)} %fusion.16, bf16[2560,1152]{1,0:T(8,128)(2,1)S(1)} %bitcast.70, bf16[512,2048]{1,0:T(8,128)(2,1)S(1)} %copy-done.7), kind=kOutput, calls=%fused_computation.9 | convolution fusion | flops 2685665280 | bytes 16777216 | tf_op jit(solution)/shard_map/dot_general | solution.py:80
  211.0 6.5 %gather_fusion.7 = f32[1024,512]{1,0:T(8,128)S(1)} fusion(f32[2560,512]{1,0:T(8,128)} %convolution_add_fusion, s32[1024]{0:T(1024)S(1)} %get-tuple-element.33), kind=kCustom, calls=%fused_computation.7 | custom fusion | bytes 4198400 | tf_op jit(solution)/shard_map/gather | solution.py:95
  217.5 7.8 %gather_fusion.6 = f32[1024,512]{1,0:T(8,128)} fusion(f32[2560,512]{1,0:T(8,128)} %convolution_add_fusion, s32[1024]{0:T(1024)S(1)} %get-tuple-element.34), kind=kCustom, calls=%fused_computation.6 | custom fusion | bytes 4198400 | tf_op jit(solution)/shard_map/gather | solution.py:95
  225.2 2.0 bitcast_select_fusion
  227.2 2.5 pad_maximum_fusion.2
  229.7 2.0 collective-permute-start.2
  231.6 0.4 convert_reduce_fusion
  232.0 0.1 subtract_add_fusion
  232.1 0.1 add.183
  232.2 7.8 %gather_fusion.8 = f32[1024,512]{1,0:T(8,128)} fusion(f32[2560,512]{1,0:T(8,128)} %convolution_add_fusion, s32[1024]{0:T(1024)S(1)} %get-tuple-element.32), kind=kCustom, calls=%fused_computation.8 | custom fusion | bytes 4198400 | tf_op jit(solution)/shard_map/gather | solution.py:95
  240.0 6.5 %gather_fusion.5 = f32[1024,512]{1,0:T(8,128)S(1)} fusion(f32[2560,512]{1,0:T(8,128)} %convolution_add_fusion, s32[1024]{0:T(1024)S(1)} %get-tuple-element.31), kind=kCustom, calls=%fused_computation.5 | custom fusion | bytes 4198400 | tf_op jit(solution)/shard_map/gather | solution.py:95
  246.5 11.1 %gather_fusion.4 = bf16[2560,512]{1,0:T(8,128)(2,1)} fusion(bf16[4096,512]{1,0:T(8,128)(2,1)} %bitcast.61, s32[3072]{0:T(1024)S(1)} %pad_clamp_fusion), kind=kCustom, calls=%fused_computation.4 | custom fusion | bytes 5253120 | tf_op jit(solution)/shard_map/gather | solution.py:68
  257.6 5.8 %fusion.35 = f32[512,1024]{1,0:T(8,128)S(1)} fusion(bf16[2560,512]{1,0:T(8,128)(2,1)} %gather_fusion.4, bf16[2560,1024]{1,0:T(8,128)(2,1)} %all-gather.3.cloned.1.call-done), kind=kOutput, calls=%fused_computation.93 | convolution fusion | flops 2684354560 | bytes 9961472 | tf_op jit(solution)/shard_map/dot_general | solution.py:72
  263.4 0.0 collective-permute-done.2
  263.4 2.0 fusion.12
  265.5 0.5 collective-permute-start.3
  265.9 4.9 %fusion.1 = f32[512,1024]{1,0:T(8,128)S(1)} fusion(bf16[2560,512]{1,0:T(8,128)(2,1)S(1)} %copy-done.6, bf16[2560,1152]{1,0:T(8,128)(2,1)} %all-gather.5.cloned.1.call-done), kind=kOutput, calls=%fused_computation.11 | convolution fusion | flops 2684354560 | bytes 9961472 | tf_op jit(solution)/shard_map/dot_general | solution.py:73
  270.8 0.0 copy-start.4
  270.8 0.0 copy-start.5
  270.8 2.5 pad_maximum_fusion.1
  273.3 16.9 %collective-permute-done.3 = bf16[1024,512]{1,0:T(8,128)(2,1)S(1)} collective-permute-done((bf16[1024,512]{1,0:T(8,128)(2,1)S(1)}, bf16[1024,512]{1,0:T(8,128)(2,1)S(1)}, u32[]{:S(2)}, u32[]{:S(2)}) %collective-permute-start.3) | collective-permute-done | bytes 1048608 | tf_op jit(solution)/shard_map/ppermute | solution.py:100
  290.2 4.1 %multiply_convert_fusion = (bf16[1024,512]{1,0:T(8,128)(2,1)}, bf16[1024,512]{1,0:T(8,128)(2,1)}) fusion(bf16[1024,512]{1,0:T(8,128)(2,1)S(1)} %copy-done.5, bf16[1024,512]{1,0:T(8,128)(2,1)S(1)} %collective-permute-done.3, f32[2,1024,512]{2,1,0:T(8,128)} %collective-permute-done.2, f32[1024,512]{1,0:T(8,128)S(1)} %gather_fusion.5, ...), kind=kLoop, calls=%fused_computation.38 | loop fusion | flops 9961472 | bytes 9438208 | tf_op jit(solution)/shard_map/convert_element_type | solution.py:103
  (28 shorter events, 0.2 us)
Async XLA Ops:
  7.2 6.1 %copy-start = (bf16[144,2048]{1,0:T(8,128)(2,1)S(1)}, bf16[144,2048]{1,0:T(8,128)(2,1)}, u32[]{:S(2)}) copy-start(bf16[144,2048]{1,0:T(8,128)(2,1)} %param.9) | copy-start | bytes 1769476
  7.2 99.7 %all-gather.3.cloned.1.call-start = ((), (), s32[]{:S(2)}) async-start(), calls=%async_computation | async-start | bytes 5406720 | tf_op jit(solution)/shard_map/all_gather | solution.py:52
  13.2 1.2 copy-start.3
  17.0 181.3 %all-gather.5.cloned.1.call-start = ((), (), s32[]{:S(2)}) async-start(), calls=%async_computation.1 | async-start | bytes 6082560 | tf_op jit(solution)/shard_map/all_gather | solution.py:53
  17.8 26.6 %collective-permute-start = (bf16[1024,512]{1,0:T(8,128)(2,1)S(1)}, bf16[1024,512]{1,0:T(8,128)(2,1)S(1)}, u32[]{:S(2)}, u32[]{:S(2)}) collective-permute-start(bf16[1024,512]{1,0:T(8,128)(2,1)S(1)} %fusion.3), channel_id=1, source_target_pairs={{0,2},{1,3},{2,0},{3,1},{4,6},{5,7},{6,4},{7,5},{8,10},{9,11},{10,... | collective-permute-start | bytes 3145736 | tf_op jit(solution)/shard_map/ppermute | solution.py:20
  45.9 5.4 %collective-permute-start.1 = (bf16[2,1024,512]{2,1,0:T(8,128)(2,1)}, bf16[2,1024,512]{2,1,0:T(8,128)(2,1)}, u32[]{:S(2)}, u32[]{:S(2)}) collective-permute-start(bf16[2,1024,512]{2,1,0:T(8,128)(2,1)} %pad_maximum_fusion.3), channel_id=1, source_target_pairs={{0,1},{1,0},{2,3},{3,2},{4,5},{5,4},{6,7},{7,6},{8,9},{9,8},{10,11... | collective-permute-start | bytes 6291464 | tf_op jit(solution)/shard_map/ppermute | solution.py:22
  200.4 5.7 %slice-start = ((s8[5898240]{0:T(1024)(128)(4,1)}), s8[1703936]{0:T(1024)(128)(4,1)S(1)}, s32[]{:S(2)}) async-start(s8[5898240]{0:T(1024)(128)(4,1)} %bitcast.69), calls=%async_computation.2 | async-start | bytes 3407872
  200.8 5.4 %slice-start.1 = ((s8[5898240]{0:T(1024)(128)(4,1)}), s8[4194304]{0:T(1024)(128)(4,1)S(1)}, s32[]{:S(2)}) async-start(s8[5898240]{0:T(1024)(128)(4,1)} %bitcast.69), calls=%async_computation.3 | async-start | bytes 8388608
  200.8 5.4 %copy-start.7 = (bf16[512,2048]{1,0:T(8,128)(2,1)S(1)}, bf16[512,2048]{1,0:T(8,128)(2,1)}, u32[]{:S(2)}) copy-start(bf16[512,2048]{1,0:T(8,128)(2,1)} %param.15) | copy-start | bytes 6291460
  229.7 33.7 %collective-permute-start.2 = (f32[2,1024,512]{2,1,0:T(8,128)}, f32[2,1024,512]{2,1,0:T(8,128)}, u32[]{:S(2)}, u32[]{:S(2)}) collective-permute-start(f32[2,1024,512]{2,1,0:T(8,128)} %pad_maximum_fusion.2), channel_id=1, source_target_pairs={{0,1},{1,0},{2,3},{3,2},{4,5},{5,4},{6,7},{7,6},{8,9},{9,8},{10,11... | collective-permute-start | bytes 12582920 | tf_op jit(solution)/shard_map/ppermute | solution.py:98
  257.6 5.8 %copy-start.2 = (f32[1024,512]{1,0:T(8,128)S(1)}, f32[1024,512]{1,0:T(8,128)}, u32[]{:S(2)}) copy-start(f32[1024,512]{1,0:T(8,128)} %gather_fusion.8) | copy-start | bytes 6291460
  263.4 2.5 copy-start.6
  265.5 24.8 %collective-permute-start.3 = (bf16[1024,512]{1,0:T(8,128)(2,1)S(1)}, bf16[1024,512]{1,0:T(8,128)(2,1)S(1)}, u32[]{:S(2)}, u32[]{:S(2)}) collective-permute-start(bf16[1024,512]{1,0:T(8,128)(2,1)S(1)} %fusion.12), channel_id=1, source_target_pairs={{0,2},{1,3},{2,0},{3,1},{4,6},{5,7},{6,4},{7,5},{8,10},{9,11},{10,... | collective-permute-start | bytes 3145736 | tf_op jit(solution)/shard_map/ppermute | solution.py:100
  270.8 19.5 %copy-start.4 = (bf16[1024,512]{1,0:T(8,128)(2,1)S(1)}, bf16[1024,512]{1,0:T(8,128)(2,1)}, u32[]{:S(2)}) copy-start(bf16[1024,512]{1,0:T(8,128)(2,1)} %param.14) | copy-start | bytes 3145732
  270.8 19.4 %copy-start.5 = (bf16[1024,512]{1,0:T(8,128)(2,1)S(1)}, bf16[1024,512]{1,0:T(8,128)(2,1)}, u32[]{:S(2)}) copy-start(bf16[1024,512]{1,0:T(8,128)(2,1)} %param.13) | copy-start | bytes 3145732
  290.2 4.1 %copy-start.1 = (bf16[144,2048]{1,0:T(8,128)(2,1)S(1)}, bf16[144,2048]{1,0:T(8,128)(2,1)}, u32[]{:S(2)}) copy-start(bf16[144,2048]{1,0:T(8,128)(2,1)} %param.9) | copy-start | bytes 1769476
Sparse Core Ops, SparseCore 0:
  17.2 89.6 all-gather.2
  110.5 87.8 all-gather.4

commit v5 on v3

--- a/solution.py
+++ b/solution.py
@@ -63,10 +63,6 @@
     sender = jnp.arange(learners, dtype=jnp.int32)[:, None]
     slot_of = (m_of * SLOTS + sender * capacity + c_of).reshape(-1)
 
-    hidden_live = hidden_all[slot_of]
-    grad_down = lax.dot_general(
-        hidden_live, everything, (((0,), (0,)), ((), ())), preferred_element_type=jnp.float32
-    )
     partial_live = lax.dot_general(
         everything, down_weight, (((1,), (1,)), ((), ())), preferred_element_type=jnp.float32
     )
@@ -88,9 +84,16 @@
 
     to_core = jnp.stack([partial_block(me ^ 3), partial_block(me ^ 1)])
     from_core = lax.ppermute(to_core, "mp", [(i, i ^ 1) for i in range(n_mp)])
-    to_chip = partial_block(me ^ 2) + from_core[0]
+    to_chip = (partial_block(me ^ 2) + from_core[0]).astype(jnp.bfloat16)
     from_chip = lax.ppermute(to_chip, "mp", [(i, i ^ 2) for i in range(n_mp)])
-    hidden_grad = (partial_block(me) + from_core[1]) + from_chip
+    own_part = partial_block(me) + from_core[1]
+
+    to_chip, hidden_all = lax.optimization_barrier((to_chip, hidden_all))
+    hidden_live = hidden_all[slot_of]
+    grad_down = lax.dot_general(
+        hidden_live, everything, (((0,), (0,)), ((), ())), preferred_element_type=jnp.float32
+    )
+    hidden_grad = own_part + from_chip.astype(jnp.float32)
     grad_gate = (hidden_grad * up_in * slopes).astype(jnp.bfloat16)
     grad_up = (hidden_grad * activated).astype(jnp.bfloat16)
     return (grad_down, grad_gate, grad_up)

time: 245 us -> 229 us (0.935)
  waiting for transfers between devices: 130 us -> 114 us
    ppermute x1, waiting for transfers between devices: 18.1 us -> 2.91 us  [shards(): from_chip = lax.ppermute(to_chip, 'mp', [(i, i ^ 2) for i in range(n_mp)])]
    add x1 -> x0, other arithmetic: 3.17 us -> none  [shards(): to_chip = partial_block(me ^ 2) + from_core[0]]
  transfers between devices with their start and end apart: 5 -> 5, of which waited for: 5 -> 4; matrix products, arithmetic and copies ran while one was open for 19% -> 20% of each run, Pallas kernels for 0% -> 0%
where the time goes in v5:
time: 229 us
  waiting for transfers between devices  114 us (50%)
  local copies, waits for them, and re-layouts  50.8 us (22%)
  other arithmetic  23.4 us (10%)
  matrix products  20.4 us (9%)
  between operations  14.2 us (6%)
  starting transfers between devices  5.49 us (2%)
    all_gather x1, waiting for transfers between devices, shards(): gathered = lax.all_gather(sent, 'dp', axis=0, tiled=True)  81.8 us
    gather x4, local copies, waits for them, and re-layouts, partial_block(): return jnp.where(keep[:, None], partial_live[src], 0.0)  28.6 us
    ppermute x1, waiting for transfers between devices, mp_gather(): lax.ppermute(hidden, 'mp', [(i, (i + half) % n_mp) for i in range(n_mp)])  25.4 us
    gather x1, local copies, waits for them, and re-layouts, shards(): hidden_live = hidden_all[slot_of]  11.1 us
    dot_general x1, matrix products, shards(): lax.dot_general(hidden_live, everything, (((0,), (0,)), ((), ())), prefer...  10.6 us
    dot_general x1, matrix products, shards(): lax.dot_general(everything, down_weight, (((1,), (1,)), ((), ())), prefer...  9.81 us
    gather x1, local copies, waits for them, and re-layouts, mp_gather(): jnp.take(held, where, axis=0, mode='clip')  4.95 us
  transfers between devices with their start and end apart: 5, of which 4 were waited for; matrix products, arithmetic and copies ran while one was open for 20% of the time, Pallas kernels for 0%

profile of v5, /device:TPU:1, one launch (start us, length us, event | category | flops | bytes accessed | tf_op | source)
XLA Modules:
  0.0 228.6 jit_solution(5326573306332452433)
XLA Ops:
  7.2 0.0 copy-start
  7.2 0.0 copy-start.2
  7.2 0.0 all-gather.2.cloned.1.call-start
  7.2 0.8 convert_element_type.51
  8.1 0.7 convert_multiply_fusion.4
  8.8 0.7 copy.17
  9.5 0.1 reduce-window.8
  9.6 0.1 reduce.2
  9.7 0.7 convert_reduce_fusion.1
  10.4 1.6 gather_fusion
  12.1 1.3 gather_fusion.2
  13.4 0.0 copy-done.2
  13.4 0.8 gather_fusion.1
  14.2 0.1 multiply_convert_fusion.1
  14.3 0.8 fusion.17
  15.1 2.2 fusion.4
  17.2 0.0 all-gather.2.cloned.1.call-update
  17.3 2.5 %collective-permute-start = (bf16[1024,512]{1,0:T(8,128)(2,1)S(1)}, bf16[1024,512]{1,0:T(8,128)(2,1)S(1)}, u32[]{:S(2)}, u32[]{:S(2)}) collective-permute-start(bf16[1024,512]{1,0:T(8,128)(2,1)S(1)} %fusion.4), channel_id=1, source_target_pairs={{0,2},{1,3},{2,0},{3,1},{4,6},{5,7},{6,4},{7,5},{8,10},{9,11},{10,... | collective-permute-start | bytes 3145736 | tf_op jit(solution)/shard_map/ppermute | solution.py:20
  19.8 25.4 %collective-permute-done = bf16[1024,512]{1,0:T(8,128)(2,1)S(1)} collective-permute-done((bf16[1024,512]{1,0:T(8,128)(2,1)S(1)}, bf16[1024,512]{1,0:T(8,128)(2,1)S(1)}, u32[]{:S(2)}, u32[]{:S(2)}) %collective-permute-start) | collective-permute-done | bytes 1048608 | tf_op jit(solution)/shard_map/ppermute | solution.py:20
  45.3 0.0 copy-start.6
  45.3 1.6 pad_maximum_fusion.2
  46.9 0.0 copy-done.6
  46.9 1.1 collective-permute-start.1
  48.1 4.1 %collective-permute-done.1 = bf16[2,1024,512]{2,1,0:T(8,128)(2,1)} collective-permute-done((bf16[2,1024,512]{2,1,0:T(8,128)(2,1)}, bf16[2,1024,512]{2,1,0:T(8,128)(2,1)}, u32[]{:S(2)}, u32[]{:S(2)}) %collective-permute-start.1) | collective-permute-done | bytes 2097184 | tf_op jit(solution)/shard_map/ppermute | solution.py:22
  52.2 3.6 %pad_maximum_fusion = bf16[4,1024,512]{2,1,0:T(8,128)(2,1)} fusion(bf16[2,1024,512]{2,1,0:T(8,128)(2,1)} %collective-permute-done.1, bf16[1,1024,512]{2,1,0:T(8,128)(2,1)} %bitcast.63, bf16[1,1024,512]{2,1,0:T(8,128)(2,1)S(1)} %bitcast.61), kind=kLoop, calls=%fused_computation.13 | loop fusion | flops 4194304 | bytes 8388608 | tf_op jit(solution)/shard_map/concatenate | solution.py:23
  55.8 5.0 %gather_fusion.3 = bf16[4,1024,512]{2,1,0:T(8,128)(2,1)} fusion(bf16[4,1024,512]{2,1,0:T(8,128)(2,1)} %pad_maximum_fusion, s32[1024]{0:T(1024)S(1)} %pad_clamp_fusion.1), kind=kCustom, calls=%fused_computation.3 | custom fusion | bytes 8388624 | tf_op jit(solution)/shard_map/jit(_take)/gather | solution.py:26
  60.7 81.8 %all-gather.2.cloned.1.call-done = bf16[2560,2176]{1,0:T(8,128)(2,1)} async-done(((bf16[80,2176]{1,0:T(8,128)(2,1)}), bf16[2560,2176]{1,0:T(8,128)(2,1)}) %all-gather.2.cloned.1.call-update) | async-done | bytes 11141136 | tf_op jit(solution)/shard_map/all_gather | solution.py:51
  142.6 0.8 slice.50
  143.4 0.1 copy.19
  143.5 0.2 reduce_window_sum.18
  143.7 0.1 add_bitcast_fusion
  143.8 0.1 copy.20
  143.8 0.2 iota_compare_fusion.2
  144.1 0.3 lt.93
  144.4 0.2 iota_add_fusion
  144.6 0.3 add.183
  144.9 0.0 copy-done
  144.9 9.8 %fusion.2 = f32[2560,512]{1,0:T(8,128)} fusion(bf16[512,2048]{1,0:T(8,128)(2,1)S(1)} %copy-done, bf16[2560,2176]{1,0:T(8,128)(2,1)} %all-gather.2.cloned.1.call-done), kind=kOutput, calls=%fused_computation.11 | convolution fusion | flops 5368709120 | bytes 17825792 | tf_op jit(solution)/shard_map/dot_general | solution.py:66
  154.8 6.5 %gather_fusion.6 = f32[1024,512]{1,0:T(8,128)S(1)} fusion(f32[2560,512]{1,0:T(8,128)} %fusion.2, s32[1024]{0:T(1024)S(1)} %get-tuple-element.32), kind=kCustom, calls=%fused_computation.6 | custom fusion | bytes 4198400 | tf_op jit(solution)/shard_map/gather | solution.py:83
  161.3 7.8 %gather_fusion.5 = f32[1024,512]{1,0:T(8,128)} fusion(f32[2560,512]{1,0:T(8,128)} %fusion.2, s32[1024]{0:T(1024)S(1)} %get-tuple-element.33), kind=kCustom, calls=%fused_computation.5 | custom fusion | bytes 4198400 | tf_op jit(solution)/shard_map/gather | solution.py:83
  169.0 2.0 bitcast_select_fusion
  171.0 2.5 %pad_maximum_fusion.1 = f32[2,1024,512]{2,1,0:T(8,128)} fusion(f32[1,1024,512]{2,1,0:T(8,128)S(1)} %get-tuple-element.41, f32[1,1024,512]{2,1,0:T(8,128)S(1)} %get-tuple-element.42), kind=kLoop, calls=%fused_computation.14 | loop fusion | flops 1048576 | bytes 8388608 | tf_op jit(solution)/shard_map/stack | solution.py:85
  173.5 1.4 collective-permute-start.2
  174.9 0.4 convert_reduce_fusion
  175.3 0.1 subtract_add_fusion
  175.3 0.1 add.193
  175.4 7.8 %gather_fusion.8 = f32[1024,512]{1,0:T(8,128)} fusion(f32[2560,512]{1,0:T(8,128)} %fusion.2, s32[1024]{0:T(1024)S(1)} %get-tuple-element.31), kind=kCustom, calls=%fused_computation.8 | custom fusion | bytes 4198400 | tf_op jit(solution)/shard_map/gather | solution.py:83
  183.2 6.5 %gather_fusion.4 = f32[1024,512]{1,0:T(8,128)S(1)} fusion(f32[2560,512]{1,0:T(8,128)} %fusion.2, s32[1024]{0:T(1024)S(1)} %get-tuple-element.34), kind=kCustom, calls=%fused_computation.4 | custom fusion | bytes 4198400 | tf_op jit(solution)/shard_map/gather | solution.py:83
  189.8 0.0 collective-permute-done.2
  189.8 2.8 %fusion.15 = bf16[1024,512]{1,0:T(8,128)(2,1)} fusion(f32[2,1024,512]{2,1,0:T(8,128)} %collective-permute-done.2, f32[1024,512]{1,0:T(8,128)S(1)} %gather_fusion.4, pred[1024]{0:T(1024)(128)(4,1)S(1)} %get-tuple-element.40), kind=kLoop, calls=%fused_computation.33 | loop fusion | flops 1572864 | bytes 5243904 | tf_op jit(solution)/shard_map/convert_element_type | solution.py:87
  192.6 0.4 collective-permute-start.3
  193.0 11.1 %gather_fusion.7 = bf16[2560,512]{1,0:T(8,128)(2,1)} fusion(bf16[4096,512]{1,0:T(8,128)(2,1)} %bitcast.59, s32[3072]{0:T(1024)S(1)} %pad_clamp_fusion), kind=kCustom, calls=%fused_computation.7 | custom fusion | bytes 5253120 | tf_op jit(solution)/shard_map/gather | solution.py:92
  204.1 0.0 copy-start.3
  204.1 0.0 copy-start.4
  204.1 0.0 copy-start.5
  204.1 10.6 %fusion = f32[512,2048]{1,0:T(8,128)} fusion(bf16[2560,512]{1,0:T(8,128)(2,1)} %gather_fusion.7, bf16[2560,2176]{1,0:T(8,128)(2,1)} %all-gather.2.cloned.1.call-done), kind=kOutput, calls=%fused_computation.9 | convolution fusion | flops 5368709120 | bytes 17301504 | tf_op jit(solution)/shard_map/dot_general | solution.py:93
  214.6 2.9 %collective-permute-done.3 = bf16[1024,512]{1,0:T(8,128)(2,1)S(1)} collective-permute-done((bf16[1024,512]{1,0:T(8,128)(2,1)}, bf16[1024,512]{1,0:T(8,128)(2,1)S(1)}, u32[]{:S(2)}, u32[]{:S(2)}) %collective-permute-start.3) | collective-permute-done | bytes 1048608 | tf_op jit(solution)/shard_map/ppermute | solution.py:88
  217.6 0.0 copy-done.3
  217.6 0.0 copy-done.4
  217.6 0.0 copy-done.5
  217.6 0.0 copy-start.1
  217.6 4.2 %multiply_convert_fusion = (bf16[1024,512]{1,0:T(8,128)(2,1)}, bf16[1024,512]{1,0:T(8,128)(2,1)}) fusion(bf16[1024,512]{1,0:T(8,128)(2,1)S(1)} %copy-done.5, bf16[1024,512]{1,0:T(8,128)(2,1)S(1)} %collective-permute-done.3, f32[2,1024,512]{2,1,0:T(8,128)} %collective-permute-done.2, f32[1024,512]{1,0:T(8,128)S(1)} %copy-done.3, ...), kind=kLoop, calls=%fused_computation.37 | loop fusion | flops 9961472 | bytes 9438208 | tf_op jit(solution)/shard_map/convert_element_type | solution.py:98
  221.8 0.0 copy-done.1
  (14 shorter events, 0.2 us)
Async XLA Ops:
  7.2 137.8 %copy-start = (bf16[512,2048]{1,0:T(8,128)(2,1)S(1)}, bf16[512,2048]{1,0:T(8,128)(2,1)}, u32[]{:S(2)}) copy-start(bf16[512,2048]{1,0:T(8,128)(2,1)} %param.15) | copy-start | bytes 6291460
  7.2 6.2 %copy-start.2 = (bf16[144,2048]{1,0:T(8,128)(2,1)S(1)}, bf16[144,2048]{1,0:T(8,128)(2,1)}, u32[]{:S(2)}) copy-start(bf16[144,2048]{1,0:T(8,128)(2,1)} %param.9) | copy-start | bytes 1769476
  7.2 135.4 %all-gather.2.cloned.1.call-start = ((), (), s32[]{:S(2)}) async-start(), calls=%async_computation | async-start | bytes 11489280 | tf_op jit(solution)/shard_map/all_gather | solution.py:51
  17.3 28.0 %collective-permute-start = (bf16[1024,512]{1,0:T(8,128)(2,1)S(1)}, bf16[1024,512]{1,0:T(8,128)(2,1)S(1)}, u32[]{:S(2)}, u32[]{:S(2)}) collective-permute-start(bf16[1024,512]{1,0:T(8,128)(2,1)S(1)} %fusion.4), channel_id=1, source_target_pairs={{0,2},{1,3},{2,0},{3,1},{4,6},{5,7},{6,4},{7,5},{8,10},{9,11},{10,... | collective-permute-start | bytes 3145736 | tf_op jit(solution)/shard_map/ppermute | solution.py:20
  45.3 1.7 copy-start.6
  46.9 5.3 %collective-permute-start.1 = (bf16[2,1024,512]{2,1,0:T(8,128)(2,1)}, bf16[2,1024,512]{2,1,0:T(8,128)(2,1)}, u32[]{:S(2)}, u32[]{:S(2)}) collective-permute-start(bf16[2,1024,512]{2,1,0:T(8,128)(2,1)} %pad_maximum_fusion.2), channel_id=1, source_target_pairs={{0,1},{1,0},{2,3},{3,2},{4,5},{5,4},{6,7},{7,6},{8,9},{9,8},{10,11... | collective-permute-start | bytes 6291464 | tf_op jit(solution)/shard_map/ppermute | solution.py:22
  173.5 16.3 %collective-permute-start.2 = (f32[2,1024,512]{2,1,0:T(8,128)}, f32[2,1024,512]{2,1,0:T(8,128)}, u32[]{:S(2)}, u32[]{:S(2)}) collective-permute-start(f32[2,1024,512]{2,1,0:T(8,128)} %pad_maximum_fusion.1), channel_id=1, source_target_pairs={{0,1},{1,0},{2,3},{3,2},{4,5},{5,4},{6,7},{7,6},{8,9},{9,8},{10,11... | collective-permute-start | bytes 12582920 | tf_op jit(solution)/shard_map/ppermute | solution.py:86
  192.6 24.9 %collective-permute-start.3 = (bf16[1024,512]{1,0:T(8,128)(2,1)}, bf16[1024,512]{1,0:T(8,128)(2,1)S(1)}, u32[]{:S(2)}, u32[]{:S(2)}) collective-permute-start(bf16[1024,512]{1,0:T(8,128)(2,1)} %fusion.15), channel_id=1, source_target_pairs={{0,2},{1,3},{2,0},{3,1},{4,6},{5,7},{6,4},{7,5},{8,10},{9,11},{10,... | collective-permute-start | bytes 3145736 | tf_op jit(solution)/shard_map/ppermute | solution.py:88
  204.1 13.5 %copy-start.3 = (f32[1024,512]{1,0:T(8,128)S(1)}, f32[1024,512]{1,0:T(8,128)}, u32[]{:S(2)}) copy-start(f32[1024,512]{1,0:T(8,128)} %gather_fusion.8) | copy-start | bytes 6291460
  204.1 13.5 %copy-start.4 = (bf16[1024,512]{1,0:T(8,128)(2,1)S(1)}, bf16[1024,512]{1,0:T(8,128)(2,1)}, u32[]{:S(2)}) copy-start(bf16[1024,512]{1,0:T(8,128)(2,1)} %param.14) | copy-start | bytes 3145732
  204.1 13.5 %copy-start.5 = (bf16[1024,512]{1,0:T(8,128)(2,1)S(1)}, bf16[1024,512]{1,0:T(8,128)(2,1)}, u32[]{:S(2)}) copy-start(bf16[1024,512]{1,0:T(8,128)(2,1)} %param.13) | copy-start | bytes 3145732
  217.6 4.2 %copy-start.1 = (bf16[512,2048]{1,0:T(8,128)(2,1)S(1)}, bf16[512,2048]{1,0:T(8,128)(2,1)}, u32[]{:S(2)}) copy-start(bf16[512,2048]{1,0:T(8,128)(2,1)} %param.15) | copy-start | bytes 6291460
Sparse Core Ops, SparseCore 0:
  17.4 125.1 all-gather.1

commit v6 on v5

--- a/solution.py
+++ b/solution.py
@@ -31,10 +31,6 @@
     capacity = SLOTS // learners
     d_cols = sample_grad.shape[1]
 
-    gate_in = gate_pre.astype(jnp.float32)
-    up_in = up_pre.astype(jnp.float32)
-    activated, slopes = silu_parts(gate_in)
-    hidden = (activated * up_in).astype(jnp.bfloat16)
 
     own = route_count[0]
     own_end = jnp.cumsum(own)
@@ -47,7 +43,11 @@
     scaled = (sample_grad[picked].astype(jnp.float32) * weights[picked][:, None]).astype(jnp.bfloat16)
     info = jnp.zeros((LIVE, INFO), jnp.bfloat16).at[0, :learners].set(own.astype(jnp.bfloat16))
     sent = jnp.concatenate([scaled, info], axis=1)
-    sent, hidden = lax.optimization_barrier((sent, hidden))
+    sent, gate_late, up_late = lax.optimization_barrier((sent, gate_pre, up_pre))
+    gate_in = gate_late.astype(jnp.float32)
+    up_in = up_late.astype(jnp.float32)
+    activated, slopes = silu_parts(gate_in)
+    hidden = (activated * up_in).astype(jnp.bfloat16)
     gathered = lax.all_gather(sent, "dp", axis=0, tiled=True)
     hidden_all = mp_gather(hidden)
     gathered, hidden_all = lax.optimization_barrier((gathered, hidden_all))
@@ -76,24 +76,24 @@
     n_mp = lax.axis_size("mp")
     rows_per = hidden.shape[0]
 
-    def partial_block(b):
+    def partial_block(partial, b):
         at = b * rows_per
         src = lax.dynamic_slice_in_dim(source, at, rows_per)
         keep = lax.dynamic_slice_in_dim(live, at, rows_per)
-        return jnp.where(keep[:, None], partial_live[src], 0.0)
+        return jnp.where(keep[:, None], partial[src], 0.0)
 
-    to_core = jnp.stack([partial_block(me ^ 3), partial_block(me ^ 1)])
-    from_core = lax.ppermute(to_core, "mp", [(i, i ^ 1) for i in range(n_mp)])
-    to_chip = (partial_block(me ^ 2) + from_core[0]).astype(jnp.bfloat16)
+    pairs_core = [(i, i ^ 1) for i in range(n_mp)]
+    from_core = lax.ppermute(partial_block(partial_live, me ^ 3), "mp", pairs_core)
+    to_chip = (partial_block(partial_live, me ^ 2) + from_core).astype(jnp.bfloat16)
+    to_chip, partial_late, hidden_all = lax.optimization_barrier((to_chip, partial_live, hidden_all))
     from_chip = lax.ppermute(to_chip, "mp", [(i, i ^ 2) for i in range(n_mp)])
-    own_part = partial_block(me) + from_core[1]
-
-    to_chip, hidden_all = lax.optimization_barrier((to_chip, hidden_all))
+    from_core_own = lax.ppermute(partial_block(partial_late, me ^ 1), "mp", pairs_core)
+    own_part = partial_block(partial_late, me)
     hidden_live = hidden_all[slot_of]
     grad_down = lax.dot_general(
         hidden_live, everything, (((0,), (0,)), ((), ())), preferred_element_type=jnp.float32
     )
-    hidden_grad = own_part + from_chip.astype(jnp.float32)
+    hidden_grad = (own_part + from_core_own) + from_chip.astype(jnp.float32)
     grad_gate = (hidden_grad * up_in * slopes).astype(jnp.bfloat16)
     grad_up = (hidden_grad * activated).astype(jnp.bfloat16)
     return (grad_down, grad_gate, grad_up)

time: 229 us -> 229 us (level)
  waiting for transfers between devices: 114 us -> 109 us
  local copies, waits for them, and re-layouts: 50.8 us -> 53.3 us
  other arithmetic: 23.4 us -> 25.8 us
    select_n x1 -> x2, other arithmetic: 1.98 us -> 6.24 us  [partial_block(): return jnp.where(keep[:, None], partial[src], 0.0)]
    ppermute x1, waiting for transfers between devices: 2.91 us -> 0.01 us  [shards(): from_chip = lax.ppermute(to_chip, 'mp', [(i, i ^ 2) for i in range(n_mp)])]
    gather x4, local copies, waits for them, and re-layouts: 28.6 us -> 31.1 us  [partial_block(): return jnp.where(keep[:, None], partial[src], 0.0)]
    another operation x3 -> x2, other arithmetic: 2.62 us -> 0.17 us  [the longest x1 2.45 us: shards(): to_core = jnp.stack([partial_block(me ^ 3), partial_block(me ^ 1)])]
  transfers between devices with their start and end apart: 5 -> 6, of which waited for: 4 -> 3; matrix products, arithmetic and copies ran while one was open for 20% -> 22% of each run, Pallas kernels for 0% -> 0%
where the time goes in v6:
time: 229 us
  waiting for transfers between devices  109 us (48%)
  local copies, waits for them, and re-layouts  53.3 us (23%)
  other arithmetic  25.8 us (11%)
  matrix products  20.4 us (9%)
  between operations  14.2 us (6%)
  starting transfers between devices  5.86 us (3%)
    all_gather x1, waiting for transfers between devices, shards(): gathered = lax.all_gather(sent, 'dp', axis=0, tiled=True)  79.5 us
    gather x4, local copies, waits for them, and re-layouts, partial_block(): return jnp.where(keep[:, None], partial[src], 0.0)  31.1 us
    ppermute x1, waiting for transfers between devices, mp_gather(): lax.ppermute(hidden, 'mp', [(i, (i + half) % n_mp) for i in range(n_mp)])  25.3 us
    gather x1, local copies, waits for them, and re-layouts, shards(): hidden_live = hidden_all[slot_of]  11.1 us
    dot_general x1, matrix products, shards(): lax.dot_general(hidden_live, everything, (((0,), (0,)), ((), ())), prefer...  10.6 us
    dot_general x1, matrix products, shards(): lax.dot_general(everything, down_weight, (((1,), (1,)), ((), ())), prefer...  9.8 us
    select_n x2, other arithmetic, partial_block(): return jnp.where(keep[:, None], partial[src], 0.0)  6.24 us
    gather x1, local copies, waits for them, and re-layouts, mp_gather(): jnp.take(held, where, axis=0, mode='clip')  4.97 us
  transfers between devices with their start and end apart: 6, of which 3 were waited for; matrix products, arithmetic and copies ran while one was open for 22% of the time, Pallas kernels for 0%

profile of v6, /device:TPU:1, one launch (start us, length us, event | category | flops | bytes accessed | tf_op | source)
XLA Modules:
  0.0 228.5 jit_solution(7562548930905474692)
XLA Ops:
  7.2 0.0 copy-start
  7.2 0.0 copy-start.1
  7.2 0.0 all-gather.2.cloned.1.call-start
  7.2 0.8 convert_element_type.51
  8.1 0.7 copy.17
  8.8 0.1 reduce-window.8
  8.9 0.1 reduce.2
  9.0 0.7 convert_reduce_fusion.1
  9.8 1.6 gather_fusion
  11.4 0.7 convert_multiply_fusion.4
  12.1 0.0 copy-done.1
  12.1 0.8 gather_fusion.1
  12.9 1.3 gather_fusion.2
  14.2 0.1 multiply_convert_fusion.1
  14.3 0.8 fusion.13
  15.0 0.0 all-gather.2.cloned.1.call-update
  15.1 2.2 fusion.4
  17.3 2.5 %collective-permute-start = (bf16[1024,512]{1,0:T(8,128)(2,1)S(1)}, bf16[1024,512]{1,0:T(8,128)(2,1)S(1)}, u32[]{:S(2)}, u32[]{:S(2)}) collective-permute-start(bf16[1024,512]{1,0:T(8,128)(2,1)S(1)} %fusion.4), channel_id=1, source_target_pairs={{0,2},{1,3},{2,0},{3,1},{4,6},{5,7},{6,4},{7,5},{8,10},{9,11},{10,... | collective-permute-start | bytes 3145736 | tf_op jit(solution)/shard_map/ppermute | solution.py:20
  19.8 25.3 %collective-permute-done = bf16[1024,512]{1,0:T(8,128)(2,1)S(1)} collective-permute-done((bf16[1024,512]{1,0:T(8,128)(2,1)S(1)}, bf16[1024,512]{1,0:T(8,128)(2,1)S(1)}, u32[]{:S(2)}, u32[]{:S(2)}) %collective-permute-start) | collective-permute-done | bytes 1048608 | tf_op jit(solution)/shard_map/ppermute | solution.py:20
  45.1 0.0 copy-start.5
  45.1 1.6 pad_maximum_fusion.1
  46.8 0.0 copy-done.5
  46.8 1.3 collective-permute-start.1
  48.1 4.1 %collective-permute-done.1 = bf16[2,1024,512]{2,1,0:T(8,128)(2,1)} collective-permute-done((bf16[2,1024,512]{2,1,0:T(8,128)(2,1)}, bf16[2,1024,512]{2,1,0:T(8,128)(2,1)}, u32[]{:S(2)}, u32[]{:S(2)}) %collective-permute-start.1) | collective-permute-done | bytes 2097184 | tf_op jit(solution)/shard_map/ppermute | solution.py:22
  52.2 3.6 %pad_maximum_fusion = bf16[4,1024,512]{2,1,0:T(8,128)(2,1)} fusion(bf16[2,1024,512]{2,1,0:T(8,128)(2,1)} %collective-permute-done.1, bf16[1,1024,512]{2,1,0:T(8,128)(2,1)} %bitcast.43, bf16[1,1024,512]{2,1,0:T(8,128)(2,1)S(1)} %bitcast.41), kind=kLoop, calls=%fused_computation.13 | loop fusion | flops 4194304 | bytes 8388608 | tf_op jit(solution)/shard_map/concatenate | solution.py:23
  55.8 5.0 %gather_fusion.3 = bf16[4,1024,512]{2,1,0:T(8,128)(2,1)} fusion(bf16[4,1024,512]{2,1,0:T(8,128)(2,1)} %pad_maximum_fusion, s32[1024]{0:T(1024)S(1)} %pad_clamp_fusion.1), kind=kCustom, calls=%fused_computation.3 | custom fusion | bytes 8388624 | tf_op jit(solution)/shard_map/jit(_take)/gather | solution.py:26
  60.8 79.5 %all-gather.2.cloned.1.call-done = bf16[2560,2176]{1,0:T(8,128)(2,1)} async-done(((bf16[80,2176]{1,0:T(8,128)(2,1)}), bf16[2560,2176]{1,0:T(8,128)(2,1)}) %all-gather.2.cloned.1.call-update) | async-done | bytes 11141136 | tf_op jit(solution)/shard_map/all_gather | solution.py:51
  140.3 0.0 copy-done
  140.4 9.8 %fusion.2 = f32[2560,512]{1,0:T(8,128)} fusion(bf16[512,2048]{1,0:T(8,128)(2,1)S(1)} %copy-done, bf16[2560,2176]{1,0:T(8,128)(2,1)} %all-gather.2.cloned.1.call-done), kind=kOutput, calls=%fused_computation.11 | convolution fusion | flops 5368709120 | bytes 17825792 | tf_op jit(solution)/shard_map/dot_general | solution.py:66
  150.2 0.8 slice.42
  151.0 0.1 copy.19
  151.1 0.2 iota_compare_fusion.2
  151.3 0.3 lt.93
  151.6 0.2 reduce_window_sum.18
  151.8 0.1 add_bitcast_fusion
  151.9 0.1 copy.20
  152.0 0.2 iota_add_fusion
  152.2 0.3 add.183
  152.5 7.8 %gather_fusion.5 = f32[1024,512]{1,0:T(8,128)} fusion(f32[2560,512]{1,0:T(8,128)} %fusion.2, s32[1024]{0:T(1024)S(1)} %get-tuple-element.39), kind=kCustom, calls=%fused_computation.5 | custom fusion | bytes 4198400 | tf_op jit(solution)/shard_map/gather | solution.py:83
  160.3 3.1 %broadcast_select_fusion.1 = f32[1024,512]{1,0:T(8,128)} fusion(f32[1024,512]{1,0:T(8,128)} %gather_fusion.5, pred[1024]{0:T(1024)(128)(4,1)S(1)} %get-tuple-element.45), kind=kLoop, calls=%fused_computation.32 | loop fusion | flops 524288 | bytes 4195328 | tf_op jit(solution)/shard_map/jit(_where)/select_n | solution.py:83
  163.4 1.4 collective-permute-start.2
  164.8 7.7 %gather_fusion.4 = f32[1024,512]{1,0:T(8,128)} fusion(f32[2560,512]{1,0:T(8,128)} %fusion.2, s32[1024]{0:T(1024)S(1)} %get-tuple-element.40), kind=kCustom, calls=%fused_computation.4 | custom fusion | bytes 4198400 | tf_op jit(solution)/shard_map/gather | solution.py:83
  172.6 0.0 collective-permute-done.2
  172.6 3.5 %add_convert_fusion = bf16[1024,512]{1,0:T(8,128)(2,1)} fusion(f32[1024,512]{1,0:T(8,128)} %collective-permute-done.2, f32[1024,512]{1,0:T(8,128)} %gather_fusion.4, pred[1024]{0:T(1024)(128)(4,1)S(1)} %get-tuple-element.46), kind=kLoop, calls=%fused_computation.30 | loop fusion | flops 1572864 | bytes 5243904 | tf_op jit(solution)/shard_map/convert_element_type | solution.py:87
  176.0 7.8 %gather_fusion.8 = f32[1024,512]{1,0:T(8,128)} fusion(f32[2560,512]{1,0:T(8,128)} %fusion.2, s32[1024]{0:T(1024)S(1)} %get-tuple-element.38), kind=kCustom, calls=%fused_computation.8 | custom fusion | bytes 4198400 | tf_op jit(solution)/shard_map/gather | solution.py:83
  183.8 3.1 %broadcast_select_fusion = f32[1024,512]{1,0:T(8,128)} fusion(f32[1024,512]{1,0:T(8,128)} %gather_fusion.8, pred[1024]{0:T(1024)(128)(4,1)S(1)} %get-tuple-element.44), kind=kLoop, calls=%fused_computation.31 | loop fusion | flops 524288 | bytes 4195328 | tf_op jit(solution)/shard_map/jit(_where)/select_n | solution.py:83
  186.9 0.0 collective-permute-start.3
  186.9 0.4 convert_reduce_fusion
  187.3 0.1 subtract_add_fusion
  187.4 0.1 add.191
  187.5 0.6 collective-permute-start.4
  188.1 7.8 %gather_fusion.7 = f32[1024,512]{1,0:T(8,128)} fusion(f32[2560,512]{1,0:T(8,128)} %fusion.2, s32[1024]{0:T(1024)S(1)} %get-tuple-element.37), kind=kCustom, calls=%fused_computation.7 | custom fusion | bytes 4198400 | tf_op jit(solution)/shard_map/gather | solution.py:83
  195.9 11.1 %gather_fusion.6 = bf16[2560,512]{1,0:T(8,128)(2,1)} fusion(bf16[4096,512]{1,0:T(8,128)(2,1)} %bitcast.39, s32[3072]{0:T(1024)S(1)} %pad_clamp_fusion), kind=kCustom, calls=%fused_computation.6 | custom fusion | bytes 5253120 | tf_op jit(solution)/shard_map/gather | solution.py:92
  207.0 0.0 copy-start.2
  207.0 0.0 copy-start.3
  207.0 0.0 copy-start.4
  207.0 10.6 %fusion = f32[512,2048]{1,0:T(8,128)} fusion(bf16[2560,512]{1,0:T(8,128)(2,1)} %gather_fusion.6, bf16[2560,2176]{1,0:T(8,128)(2,1)} %all-gather.2.cloned.1.call-done), kind=kOutput, calls=%fused_computation.9 | convolution fusion | flops 5368709120 | bytes 17301504 | tf_op jit(solution)/shard_map/dot_general | solution.py:93
  217.6 0.0 collective-permute-done.4
  217.6 0.0 collective-permute-done.3
  217.6 0.0 copy-done.2
  217.6 0.0 copy-done.3
  217.6 0.0 copy-done.4
  217.6 4.0 %multiply_convert_fusion = (bf16[1024,512]{1,0:T(8,128)(2,1)}, bf16[1024,512]{1,0:T(8,128)(2,1)}) fusion(bf16[1024,512]{1,0:T(8,128)(2,1)S(1)} %copy-done.4, bf16[1024,512]{1,0:T(8,128)(2,1)S(1)} %collective-permute-done.4, f32[1024,512]{1,0:T(8,128)} %collective-permute-done.3, f32[1024,512]{1,0:T(8,128)S(1)} %copy-done.2, ...), kind=kLoop, calls=%fused_computation.28 | loop fusion | flops 9961472 | bytes 9438208 | tf_op jit(solution)/shard_map/convert_element_type | solution.py:98
  (14 shorter events, 0.2 us)
Async XLA Ops:
  7.2 133.2 %copy-start = (bf16[512,2048]{1,0:T(8,128)(2,1)S(1)}, bf16[512,2048]{1,0:T(8,128)(2,1)}, u32[]{:S(2)}) copy-start(bf16[512,2048]{1,0:T(8,128)(2,1)} %param.15) | copy-start | bytes 6291460
  7.2 4.9 %copy-start.1 = (bf16[144,2048]{1,0:T(8,128)(2,1)S(1)}, bf16[144,2048]{1,0:T(8,128)(2,1)}, u32[]{:S(2)}) copy-start(bf16[144,2048]{1,0:T(8,128)(2,1)} %param.9) | copy-start | bytes 1769476
  7.2 133.2 %all-gather.2.cloned.1.call-start = ((), (), s32[]{:S(2)}) async-start(), calls=%async_computation | async-start | bytes 11489280 | tf_op jit(solution)/shard_map/all_gather | solution.py:51
  17.3 27.9 %collective-permute-start = (bf16[1024,512]{1,0:T(8,128)(2,1)S(1)}, bf16[1024,512]{1,0:T(8,128)(2,1)S(1)}, u32[]{:S(2)}, u32[]{:S(2)}) collective-permute-start(bf16[1024,512]{1,0:T(8,128)(2,1)S(1)} %fusion.4), channel_id=1, source_target_pairs={{0,2},{1,3},{2,0},{3,1},{4,6},{5,7},{6,4},{7,5},{8,10},{9,11},{10,... | collective-permute-start | bytes 3145736 | tf_op jit(solution)/shard_map/ppermute | solution.py:20
  45.1 1.7 copy-start.5
  46.8 5.4 %collective-permute-start.1 = (bf16[2,1024,512]{2,1,0:T(8,128)(2,1)}, bf16[2,1024,512]{2,1,0:T(8,128)(2,1)}, u32[]{:S(2)}, u32[]{:S(2)}) collective-permute-start(bf16[2,1024,512]{2,1,0:T(8,128)(2,1)} %pad_maximum_fusion.1), channel_id=1, source_target_pairs={{0,1},{1,0},{2,3},{3,2},{4,5},{5,4},{6,7},{7,6},{8,9},{9,8},{10,11... | collective-permute-start | bytes 6291464 | tf_op jit(solution)/shard_map/ppermute | solution.py:22
  163.4 9.2 %collective-permute-start.2 = (f32[1024,512]{1,0:T(8,128)}, f32[1024,512]{1,0:T(8,128)}, u32[]{:S(2)}, u32[]{:S(2)}) collective-permute-start(f32[1024,512]{1,0:T(8,128)} %broadcast_select_fusion.1), channel_id=1, source_target_pairs={{0,1},{1,0},{2,3},{3,2},{4,5},{5,4},{6,7},{7,6},{8,9},{9,8},{10,11... | collective-permute-start | bytes 6291464 | tf_op jit(solution)/shard_map/ppermute | solution.py:86
  186.9 30.7 %collective-permute-start.3 = (f32[1024,512]{1,0:T(8,128)}, f32[1024,512]{1,0:T(8,128)}, u32[]{:S(2)}, u32[]{:S(2)}) collective-permute-start(f32[1024,512]{1,0:T(8,128)} %broadcast_select_fusion), channel_id=1, source_target_pairs={{0,1},{1,0},{2,3},{3,2},{4,5},{5,4},{6,7},{7,6},{8,9},{9,8},{10,11... | collective-permute-start | bytes 6291464 | tf_op jit(solution)/shard_map/ppermute | solution.py:90
  187.5 30.1 %collective-permute-start.4 = (bf16[1024,512]{1,0:T(8,128)(2,1)}, bf16[1024,512]{1,0:T(8,128)(2,1)S(1)}, u32[]{:S(2)}, u32[]{:S(2)}) collective-permute-start(bf16[1024,512]{1,0:T(8,128)(2,1)} %add_convert_fusion), channel_id=1, source_target_pairs={{0,2},{1,3},{2,0},{3,1},{4,6},{5,7},{6,4},{7,5},{8,10},{9,11},{10,... | collective-permute-start | bytes 3145736 | tf_op jit(solution)/shard_map/ppermute | solution.py:89
  207.0 10.6 %copy-start.2 = (f32[1024,512]{1,0:T(8,128)S(1)}, f32[1024,512]{1,0:T(8,128)}, u32[]{:S(2)}) copy-start(f32[1024,512]{1,0:T(8,128)} %gather_fusion.7) | copy-start | bytes 6291460
  207.0 10.6 %copy-start.3 = (bf16[1024,512]{1,0:T(8,128)(2,1)S(1)}, bf16[1024,512]{1,0:T(8,128)(2,1)}, u32[]{:S(2)}) copy-start(bf16[1024,512]{1,0:T(8,128)(2,1)} %param.14) | copy-start | bytes 3145732
  207.0 10.6 %copy-start.4 = (bf16[1024,512]{1,0:T(8,128)(2,1)S(1)}, bf16[1024,512]{1,0:T(8,128)(2,1)}, u32[]{:S(2)}) copy-start(bf16[1024,512]{1,0:T(8,128)(2,1)} %param.13) | copy-start | bytes 3145732
Sparse Core Ops, SparseCore 0:
  15.2 125.1 all-gather.1

commit v7 on v6

--- a/solution.py
+++ b/solution.py
@@ -5,7 +5,6 @@
 
 SLOTS = 128
 LIVE = SLOTS * 5 // 8
-INFO = 128
 
 
 def silu_parts(gate_in):
@@ -26,11 +25,22 @@
     return jnp.take(held, where, axis=0, mode="clip").reshape(n_mp * hidden.shape[0], hidden.shape[1])
 
 
+def dp_gather_small(block):
+    n = lax.axis_size("dp")
+    me = lax.axis_index("dp")
+    held = block
+    step = 1
+    while step < n:
+        theirs = lax.ppermute(held, "dp", [(i, i ^ step) for i in range(n)])
+        low = (me & step) == 0
+        held = jnp.where(low, jnp.concatenate([held, theirs]), jnp.concatenate([theirs, held]))
+        step *= 2
+    return held
+
+
 def shards(sample_grad, advantage, route_rows, route_count, gate_pre, up_pre, down_weight):
     learners = lax.axis_size("dp")
     capacity = SLOTS // learners
-    d_cols = sample_grad.shape[1]
-
 
     own = route_count[0]
     own_end = jnp.cumsum(own)
@@ -41,19 +51,16 @@
     picked = route_rows[0][own_m * capacity + own_c]
     weights = advantage.astype(jnp.float32) * (1.0 / 4096.0)
     scaled = (sample_grad[picked].astype(jnp.float32) * weights[picked][:, None]).astype(jnp.bfloat16)
-    info = jnp.zeros((LIVE, INFO), jnp.bfloat16).at[0, :learners].set(own.astype(jnp.bfloat16))
-    sent = jnp.concatenate([scaled, info], axis=1)
-    sent, gate_late, up_late = lax.optimization_barrier((sent, gate_pre, up_pre))
+    sent, gate_late, up_late, own_late = lax.optimization_barrier((scaled, gate_pre, up_pre, route_count))
     gate_in = gate_late.astype(jnp.float32)
     up_in = up_late.astype(jnp.float32)
     activated, slopes = silu_parts(gate_in)
     hidden = (activated * up_in).astype(jnp.bfloat16)
     gathered = lax.all_gather(sent, "dp", axis=0, tiled=True)
     hidden_all = mp_gather(hidden)
-    gathered, hidden_all = lax.optimization_barrier((gathered, hidden_all))
-    everything = gathered[:, :d_cols]
-    counts = gathered.reshape(learners, LIVE, d_cols + INFO)[:, 0, d_cols:d_cols + learners]
-    counts = counts.astype(jnp.int32)
+    counts = dp_gather_small(own_late)
+
+    everything = gathered
 
     ends = jnp.cumsum(counts, axis=1)
     starts = ends - counts
@@ -62,6 +69,8 @@
     c_of = pos[None, :] - jnp.sum(jnp.where(done, counts[:, None, :], 0), axis=2)
     sender = jnp.arange(learners, dtype=jnp.int32)[:, None]
     slot_of = (m_of * SLOTS + sender * capacity + c_of).reshape(-1)
+    hidden_live = hidden_all[slot_of]
+    everything, hidden_live = lax.optimization_barrier((everything, hidden_live))
 
     partial_live = lax.dot_general(
         everything, down_weight, (((1,), (1,)), ((), ())), preferred_element_type=jnp.float32
@@ -85,11 +94,10 @@
     pairs_core = [(i, i ^ 1) for i in range(n_mp)]
     from_core = lax.ppermute(partial_block(partial_live, me ^ 3), "mp", pairs_core)
     to_chip = (partial_block(partial_live, me ^ 2) + from_core).astype(jnp.bfloat16)
-    to_chip, partial_late, hidden_all = lax.optimization_barrier((to_chip, partial_live, hidden_all))
+    to_chip, partial_late = lax.optimization_barrier((to_chip, partial_live))
     from_chip = lax.ppermute(to_chip, "mp", [(i, i ^ 2) for i in range(n_mp)])
     from_core_own = lax.ppermute(partial_block(partial_late, me ^ 1), "mp", pairs_core)
     own_part = partial_block(partial_late, me)
-    hidden_live = hidden_all[slot_of]
     grad_down = lax.dot_general(
         hidden_live, everything, (((0,), (0,)), ((), ())), preferred_element_type=jnp.float32
     )

time: 229 us -> 217 us (0.948)
  waiting for transfers between devices: 109 us -> 83.4 us
  starting transfers between devices: 5.86 us -> 17.5 us
    all_gather x1, waiting for transfers between devices: 79.5 us -> 59.1 us  [shards(): gathered = lax.all_gather(sent, 'dp', axis=0, tiled=True)]
    ppermute x1, waiting for transfers between devices: 25.3 us -> 12.7 us  [mp_gather(): lax.ppermute(hidden, 'mp', [(i, (i + half) % n_mp) for i in range(n_mp)])]
    ppermute x0 -> x5, starting transfers between devices: none -> 11.9 us  [dp_gather_small(): theirs = lax.ppermute(held, 'dp', [(i, i ^ step) for i in range(n)])]
    ppermute x1, waiting for transfers between devices: 0.01 us -> 6.47 us  [shards(): from_chip = lax.ppermute(to_chip, 'mp', [(i, i ^ 2) for i in range(n_mp)])]
    ppermute x0 -> x5, waiting for transfers between devices: none -> 5.18 us  [dp_gather_small(): theirs = lax.ppermute(held, 'dp', [(i, i ^ step) for i in range(n)])]
    ppermute x1, waiting for transfers between devices: 4.09 us -> 0.01 us  [mp_gather(): near = lax.ppermute(pair, 'mp', [(i, i ^ 1) for i in range(n_mp)])]
  transfers between devices with their start and end apart: 6 -> 11, of which waited for: 3 -> 7; matrix products, arithmetic and copies ran while one was open for 22% -> 25% of each run, Pallas kernels for 0% -> 0%
where the time goes in v7:
time: 217 us; the launch traced here: 216 us
  waiting for transfers between devices  83.4 us (38%)
  local copies, waits for them, and re-layouts  53.8 us (25%)
  other arithmetic  27.8 us (13%)
  matrix products  19.6 us (9%)
  starting transfers between devices  17.5 us (8%)
  between operations  14.2 us (7%)
    all_gather x1, waiting for transfers between devices, shards(): gathered = lax.all_gather(sent, 'dp', axis=0, tiled=True)  59.1 us
    gather x4, local copies, waits for them, and re-layouts, partial_block(): return jnp.where(keep[:, None], partial[src], 0.0)  31.3 us
    ppermute x1, waiting for transfers between devices, mp_gather(): lax.ppermute(hidden, 'mp', [(i, (i + half) % n_mp) for i in range(n_mp)])  12.7 us
    ppermute x5, starting transfers between devices, dp_gather_small(): theirs = lax.ppermute(held, 'dp', [(i, i ^ step) for i in range(n)])  11.9 us
    gather x1, local copies, waits for them, and re-layouts, shards(): hidden_live = hidden_all[slot_of]  11.1 us
    dot_general x1, matrix products, shards(): lax.dot_general(everything, down_weight, (((1,), (1,)), ((), ())), prefer...  9.8 us
    dot_general x1, matrix products, shards(): lax.dot_general(hidden_live, everything, (((0,), (0,)), ((), ())), prefer...  9.8 us
    select_n x2, other arithmetic, partial_block(): return jnp.where(keep[:, None], partial[src], 0.0)  6.5 us
  transfers between devices with their start and end apart: 11, of which 7 were waited for; matrix products, arithmetic and copies ran while one was open for 25% of the time, Pallas kernels for 0%

profile of v7, /device:TPU:1, one launch (start us, length us, event | category | flops | bytes accessed | tf_op | source)
XLA Modules:
  0.0 216.3 jit_solution(2730747384742718730)
XLA Ops:
  7.2 0.0 copy-start
  7.2 0.0 copy-start.1
  7.2 0.0 all-gather.2.cloned.1.call-start
  7.2 0.9 convert_multiply_fusion.4
  8.1 0.7 copy.16
  8.8 0.1 reduce-window.8
  8.9 0.1 reduce
  9.0 0.7 convert_reduce_fusion.1
  9.8 1.6 gather_fusion
  11.4 1.3 gather_fusion.2
  12.7 0.0 copy-done.1
  12.7 0.8 gather_fusion.1
  13.5 0.0 copy-start.4
  13.5 0.8 multiply_convert_fusion.1
  14.4 0.0 all-gather.2.cloned.1.call-update
  14.4 2.2 %fusion = bf16[1024,512]{1,0:T(8,128)(2,1)S(1)} fusion(bf16[1024,512]{1,0:T(8,128)(2,1)} %param.12, bf16[1024,512]{1,0:T(8,128)(2,1)} %param.11), kind=kLoop, calls=%fused_computation.15 | loop fusion | flops 4194304 | bytes 3145728 | tf_op jit(solution)/shard_map/convert_element_type | solution.py:58
  16.6 2.5 %collective-permute-start = (bf16[1024,512]{1,0:T(8,128)(2,1)S(1)}, bf16[1024,512]{1,0:T(8,128)(2,1)}, u32[]{:S(2)}, u32[]{:S(2)}) collective-permute-start(bf16[1024,512]{1,0:T(8,128)(2,1)S(1)} %fusion), channel_id=1, source_target_pairs={{0,2},{1,3},{2,0},{3,1},{4,6},{5,7},{6,4},{7,5},{8,10},{9,11},{10,... | collective-permute-start | bytes 3145736 | tf_op jit(solution)/shard_map/ppermute | solution.py:19
  19.1 0.0 copy-done.4
  19.1 1.3 collective-permute-start.2
  20.4 1.5 collective-permute-done.2
  22.0 3.0 %collective-permute-start.3 = (s32[2,32]{1,0:T(2,128)S(1)}, s32[2,32]{1,0:T(2,128)S(1)}, u32[]{:S(2)}, u32[]{:S(2)}) collective-permute-start(s32[2,32]{1,0:T(2,128)S(1)} %add_select_fusion.4), channel_id=1, source_target_pairs={{0,8},{4,12},{8,0},{12,4},{16,24},{20,28},{24,16},{28,20},{32,40},... | collective-permute-start | bytes 776 | tf_op jit(solution)/shard_map/ppermute | solution.py:34
  25.0 1.0 collective-permute-done.3
  26.0 1.3 collective-permute-start.4
  27.3 1.6 collective-permute-done.4
  28.9 2.8 %collective-permute-start.5 = (s32[8,32]{1,0:T(8,128)S(1)}, s32[8,32]{1,0:T(8,128)S(1)}, u32[]{:S(2)}, u32[]{:S(2)}) collective-permute-start(s32[8,32]{1,0:T(8,128)S(1)} %add_select_fusion.2), channel_id=1, source_target_pairs={{0,32},{4,36},{8,40},{12,44},{16,48},{20,52},{24,56},{28,60},{32,0... | collective-permute-start | bytes 3080 | tf_op jit(solution)/shard_map/ppermute | solution.py:34
  31.7 12.7 %collective-permute-done = bf16[1024,512]{1,0:T(8,128)(2,1)} collective-permute-done((bf16[1024,512]{1,0:T(8,128)(2,1)S(1)}, bf16[1024,512]{1,0:T(8,128)(2,1)}, u32[]{:S(2)}, u32[]{:S(2)}) %collective-permute-start) | collective-permute-done | bytes 1048608 | tf_op jit(solution)/shard_map/ppermute | solution.py:19
  44.4 2.7 %pad_maximum_fusion.1 = bf16[2,1024,512]{2,1,0:T(8,128)(2,1)} fusion(bf16[1,1024,512]{2,1,0:T(8,128)(2,1)} %bitcast.9, bf16[1,1024,512]{2,1,0:T(8,128)(2,1)S(1)} %bitcast.31), kind=kLoop, calls=%fused_computation.23 | loop fusion | flops 1048576 | bytes 4194304 | tf_op jit(solution)/shard_map/stack | solution.py:20
  47.2 1.3 collective-permute-start.1
  48.4 0.0 collective-permute-done.5
  48.4 3.5 %collective-permute-start.6 = (s32[16,32]{1,0:T(8,128)S(1)}, s32[16,32]{1,0:T(8,128)S(1)}, u32[]{:S(2)}, u32[]{:S(2)}) collective-permute-start(s32[16,32]{1,0:T(8,128)S(1)} %add_select_fusion.1), channel_id=1, source_target_pairs={{0,64},{4,68},{8,72},{12,76},{16,80},{20,84},{24,88},{28,92},{32,9... | collective-permute-start | bytes 6152 | tf_op jit(solution)/shard_map/ppermute | solution.py:34
  51.9 1.0 collective-permute-done.6
  53.0 0.2 reduce_window_sum.18
  53.2 0.1 add_bitcast_fusion
  53.2 0.1 copy.18
  53.3 0.1 copy.17
  53.4 0.4 convert_reduce_fusion
  53.8 0.1 subtract_add_fusion
  53.8 0.1 add.176
  53.9 0.2 iota_compare_fusion
  54.1 0.3 lt.95
  54.5 1.0 iota_add_fusion
  55.5 1.3 add.186
  56.9 0.0 collective-permute-done.1
  56.9 3.6 %pad_maximum_fusion = bf16[4,1024,512]{2,1,0:T(8,128)(2,1)} fusion(bf16[2,1024,512]{2,1,0:T(8,128)(2,1)} %collective-permute-done.1, bf16[1,1024,512]{2,1,0:T(8,128)(2,1)} %bitcast.9, bf16[1,1024,512]{2,1,0:T(8,128)(2,1)S(1)} %bitcast.32), kind=kLoop, calls=%fused_computation.9 | loop fusion | flops 4194304 | bytes 8388608 | tf_op jit(solution)/shard_map/concatenate | solution.py:22
  60.5 5.1 %gather_fusion.3 = bf16[4,1024,512]{2,1,0:T(8,128)(2,1)} fusion(bf16[4,1024,512]{2,1,0:T(8,128)(2,1)} %pad_maximum_fusion, s32[1024]{0:T(1024)S(1)} %pad_clamp_fusion.1), kind=kCustom, calls=%fused_computation.3 | custom fusion | bytes 8388624 | tf_op jit(solution)/shard_map/jit(_take)/gather | solution.py:25
  65.6 11.1 %gather_fusion.4 = bf16[2560,512]{1,0:T(8,128)(2,1)} fusion(bf16[4096,512]{1,0:T(8,128)(2,1)} %bitcast.30, s32[3072]{0:T(1024)S(1)} %pad_clamp_fusion), kind=kCustom, calls=%fused_computation.4 | custom fusion | bytes 5253120 | tf_op jit(solution)/shard_map/gather | solution.py:72
  76.7 59.1 %all-gather.2.cloned.1.call-done = bf16[2560,2048]{1,0:T(8,128)(2,1)} async-done(((bf16[80,2048]{1,0:T(8,128)(2,1)}), bf16[2560,2048]{1,0:T(8,128)(2,1)}) %all-gather.2.cloned.1.call-update) | async-done | bytes 10485776 | tf_op jit(solution)/shard_map/all_gather | solution.py:59
  135.7 9.8 %fusion.22 = f32[2560,512]{1,0:T(8,128)} fusion(bf16[2560,2048]{1,0:T(8,128)(2,1)} %all-gather.2.cloned.1.call-done, bf16[512,2048]{1,0:T(8,128)(2,1)S(1)} %copy-done), kind=kOutput, calls=%fused_computation.80 | convolution fusion | flops 5368709120 | bytes 17825792 | tf_op jit(solution)/shard_map/dot_general | solution.py:75
  145.6 7.8 %gather_fusion.6 = f32[1024,512]{1,0:T(8,128)} fusion(f32[2560,512]{1,0:T(8,128)} %fusion.22, s32[1024]{0:T(1024)S(1)} %get-tuple-element.27), kind=kCustom, calls=%fused_computation.6 | custom fusion | bytes 4198400 | tf_op jit(solution)/shard_map/gather | solution.py:92
  153.3 3.2 %broadcast_select_fusion.1 = f32[1024,512]{1,0:T(8,128)} fusion(f32[1024,512]{1,0:T(8,128)} %gather_fusion.6, pred[1024]{0:T(1024)(128)(4,1)S(1)} %get-tuple-element.31), kind=kLoop, calls=%fused_computation.28 | loop fusion | flops 524288 | bytes 4195328 | tf_op jit(solution)/shard_map/jit(_where)/select_n | solution.py:92
  156.5 1.4 collective-permute-start.7
  157.9 7.8 %gather_fusion.5 = f32[1024,512]{1,0:T(8,128)} fusion(f32[2560,512]{1,0:T(8,128)} %fusion.22, s32[1024]{0:T(1024)S(1)} %get-tuple-element.28), kind=kCustom, calls=%fused_computation.5 | custom fusion | bytes 4198400 | tf_op jit(solution)/shard_map/gather | solution.py:92
  165.7 0.0 collective-permute-done.7
  165.7 3.5 %add_convert_fusion = bf16[1024,512]{1,0:T(8,128)(2,1)} fusion(f32[1024,512]{1,0:T(8,128)} %collective-permute-done.7, f32[1024,512]{1,0:T(8,128)} %gather_fusion.5, pred[1024]{0:T(1024)(128)(4,1)S(1)} %get-tuple-element.32), kind=kLoop, calls=%fused_computation.26 | loop fusion | flops 1572864 | bytes 5243904 | tf_op jit(solution)/shard_map/convert_element_type | solution.py:96
  169.2 7.8 %gather_fusion.8 = f32[1024,512]{1,0:T(8,128)} fusion(f32[2560,512]{1,0:T(8,128)} %fusion.22, s32[1024]{0:T(1024)S(1)} %get-tuple-element.26), kind=kCustom, calls=%fused_computation.8 | custom fusion | bytes 4198400 | tf_op jit(solution)/shard_map/gather | solution.py:92
  177.0 3.3 %broadcast_select_fusion = f32[1024,512]{1,0:T(8,128)} fusion(f32[1024,512]{1,0:T(8,128)} %gather_fusion.8, pred[1024]{0:T(1024)(128)(4,1)S(1)} %get-tuple-element.30), kind=kLoop, calls=%fused_computation.27 | loop fusion | flops 524288 | bytes 4195328 | tf_op jit(solution)/shard_map/jit(_where)/select_n | solution.py:92
  180.3 0.0 collective-permute-start.8
  180.3 0.4 collective-permute-start.9
  180.7 0.0 copy-done.3
  180.7 9.8 %fusion.21 = f32[512,2048]{1,0:T(8,128)} fusion(bf16[2560,512]{1,0:T(8,128)(2,1)S(1)} %copy-done.3, bf16[2560,2048]{1,0:T(8,128)(2,1)} %all-gather.2.cloned.1.call-done), kind=kOutput, calls=%fused_computation.79 | convolution fusion | flops 5368709120 | bytes 17301504 | tf_op jit(solution)/shard_map/dot_general | solution.py:101
  190.5 7.9 %gather_fusion.7 = f32[1024,512]{1,0:T(8,128)} fusion(f32[2560,512]{1,0:T(8,128)} %fusion.22, s32[1024]{0:T(1024)S(1)} %get-tuple-element.25), kind=kCustom, calls=%fused_computation.7 | custom fusion | bytes 4198400 | tf_op jit(solution)/shard_map/gather | solution.py:92
  198.4 6.5 %collective-permute-done.9 = bf16[1024,512]{1,0:T(8,128)(2,1)} collective-permute-done((bf16[1024,512]{1,0:T(8,128)(2,1)}, bf16[1024,512]{1,0:T(8,128)(2,1)}, u32[]{:S(2)}, u32[]{:S(2)}) %collective-permute-start.9) | collective-permute-done | bytes 1048608 | tf_op jit(solution)/shard_map/ppermute | solution.py:98
  204.8 0.0 collective-permute-done.8
  204.8 4.6 %multiply_convert_fusion = (bf16[1024,512]{1,0:T(8,128)(2,1)}, bf16[1024,512]{1,0:T(8,128)(2,1)}) fusion(bf16[1024,512]{1,0:T(8,128)(2,1)} %param.11, bf16[1024,512]{1,0:T(8,128)(2,1)} %collective-permute-done.9, f32[1024,512]{1,0:T(8,128)} %collective-permute-done.8, f32[1024,512]{1,0:T(8,128)} %gather_fusion.7, pred[1024]{0:T(1024)(128)(4,1)S(1)} %get-tuple-element.29, ...), kind=kLoop, calls=%fused_computation.24 | loop fusion | flops 9961472 | bytes 9438208 | tf_op jit(solution)/shard_map/convert_element_type | solution.py:106
  (22 shorter events, 0.2 us)
Async XLA Ops:
  7.2 128.6 %copy-start = (bf16[512,2048]{1,0:T(8,128)(2,1)S(1)}, bf16[512,2048]{1,0:T(8,128)(2,1)}, u32[]{:S(2)}) copy-start(bf16[512,2048]{1,0:T(8,128)(2,1)} %param.13) | copy-start | bytes 6291460
  7.2 5.5 %copy-start.1 = (bf16[144,2048]{1,0:T(8,128)(2,1)S(1)}, bf16[144,2048]{1,0:T(8,128)(2,1)}, u32[]{:S(2)}) copy-start(bf16[144,2048]{1,0:T(8,128)(2,1)} %param.7) | copy-start | bytes 1769476
  7.2 128.6 %all-gather.2.cloned.1.call-start = ((), (), s32[]{:S(2)}) async-start(), calls=%async_computation | async-start | bytes 10813440 | tf_op jit(solution)/shard_map/all_gather | solution.py:59
  13.5 5.6 %copy-start.4 = (s32[1,32]{1,0:T(1,128)S(1)}, s32[1,32]{1,0:T(1,128)}, u32[]{:S(2)}) copy-start(s32[1,32]{1,0:T(1,128)} %param.10) | copy-start | bytes 388
  16.6 27.8 %collective-permute-start = (bf16[1024,512]{1,0:T(8,128)(2,1)S(1)}, bf16[1024,512]{1,0:T(8,128)(2,1)}, u32[]{:S(2)}, u32[]{:S(2)}) collective-permute-start(bf16[1024,512]{1,0:T(8,128)(2,1)S(1)} %fusion), channel_id=1, source_target_pairs={{0,2},{1,3},{2,0},{3,1},{4,6},{5,7},{6,4},{7,5},{8,10},{9,11},{10,... | collective-permute-start | bytes 3145736 | tf_op jit(solution)/shard_map/ppermute | solution.py:19
  19.1 2.8 %collective-permute-start.2 = (s32[1,32]{1,0:T(1,128)S(1)}, s32[1,32]{1,0:T(1,128)S(1)}, u32[]{:S(2)}, u32[]{:S(2)}) collective-permute-start(s32[1,32]{1,0:T(1,128)S(1)} %copy-done.4), channel_id=1, source_target_pairs={{0,4},{4,0},{8,12},{12,8},{16,20},{20,16},{24,28},{28,24},{32,36},... | collective-permute-start | bytes 392 | tf_op jit(solution)/shard_map/ppermute | solution.py:34
  22.0 4.0 %collective-permute-start.3 = (s32[2,32]{1,0:T(2,128)S(1)}, s32[2,32]{1,0:T(2,128)S(1)}, u32[]{:S(2)}, u32[]{:S(2)}) collective-permute-start(s32[2,32]{1,0:T(2,128)S(1)} %add_select_fusion.4), channel_id=1, source_target_pairs={{0,8},{4,12},{8,0},{12,4},{16,24},{20,28},{24,16},{28,20},{32,40},... | collective-permute-start | bytes 776 | tf_op jit(solution)/shard_map/ppermute | solution.py:34
  26.0 2.9 %collective-permute-start.4 = (s32[4,32]{1,0:T(4,128)S(1)}, s32[4,32]{1,0:T(4,128)S(1)}, u32[]{:S(2)}, u32[]{:S(2)}) collective-permute-start(s32[4,32]{1,0:T(4,128)S(1)} %add_select_fusion.3), channel_id=1, source_target_pairs={{0,16},{4,20},{8,24},{12,28},{16,0},{20,4},{24,8},{28,12},{32,48},... | collective-permute-start | bytes 1544 | tf_op jit(solution)/shard_map/ppermute | solution.py:34
  28.9 19.5 %collective-permute-start.5 = (s32[8,32]{1,0:T(8,128)S(1)}, s32[8,32]{1,0:T(8,128)S(1)}, u32[]{:S(2)}, u32[]{:S(2)}) collective-permute-start(s32[8,32]{1,0:T(8,128)S(1)} %add_select_fusion.2), channel_id=1, source_target_pairs={{0,32},{4,36},{8,40},{12,44},{16,48},{20,52},{24,56},{28,60},{32,0... | collective-permute-start | bytes 3080 | tf_op jit(solution)/shard_map/ppermute | solution.py:34
  47.2 9.8 %collective-permute-start.1 = (bf16[2,1024,512]{2,1,0:T(8,128)(2,1)}, bf16[2,1024,512]{2,1,0:T(8,128)(2,1)}, u32[]{:S(2)}, u32[]{:S(2)}) collective-permute-start(bf16[2,1024,512]{2,1,0:T(8,128)(2,1)} %pad_maximum_fusion.1), channel_id=1, source_target_pairs={{0,1},{1,0},{2,3},{3,2},{4,5},{5,4},{6,7},{7,6},{8,9},{9,8},{10,11... | collective-permute-start | bytes 6291464 | tf_op jit(solution)/shard_map/ppermute | solution.py:21
  48.4 4.5 %collective-permute-start.6 = (s32[16,32]{1,0:T(8,128)S(1)}, s32[16,32]{1,0:T(8,128)S(1)}, u32[]{:S(2)}, u32[]{:S(2)}) collective-permute-start(s32[16,32]{1,0:T(8,128)S(1)} %add_select_fusion.1), channel_id=1, source_target_pairs={{0,64},{4,68},{8,72},{12,76},{16,80},{20,84},{24,88},{28,92},{32,9... | collective-permute-start | bytes 6152 | tf_op jit(solution)/shard_map/ppermute | solution.py:34
  156.5 9.2 %collective-permute-start.7 = (f32[1024,512]{1,0:T(8,128)}, f32[1024,512]{1,0:T(8,128)}, u32[]{:S(2)}, u32[]{:S(2)}) collective-permute-start(f32[1024,512]{1,0:T(8,128)} %broadcast_select_fusion.1), channel_id=1, source_target_pairs={{0,1},{1,0},{2,3},{3,2},{4,5},{5,4},{6,7},{7,6},{8,9},{9,8},{10,11... | collective-permute-start | bytes 6291464 | tf_op jit(solution)/shard_map/ppermute | solution.py:95
  177.0 3.7 %copy-start.3 = (bf16[2560,512]{1,0:T(8,128)(2,1)S(1)}, bf16[2560,512]{1,0:T(8,128)(2,1)}, u32[]{:S(2)}) copy-start(bf16[2560,512]{1,0:T(8,128)(2,1)} %gather_fusion.4) | copy-start | bytes 7864324
  180.3 24.5 %collective-permute-start.8 = (f32[1024,512]{1,0:T(8,128)}, f32[1024,512]{1,0:T(8,128)}, u32[]{:S(2)}, u32[]{:S(2)}) collective-permute-start(f32[1024,512]{1,0:T(8,128)} %broadcast_select_fusion), channel_id=1, source_target_pairs={{0,1},{1,0},{2,3},{3,2},{4,5},{5,4},{6,7},{7,6},{8,9},{9,8},{10,11... | collective-permute-start | bytes 6291464 | tf_op jit(solution)/shard_map/ppermute | solution.py:99
  180.3 24.5 %collective-permute-start.9 = (bf16[1024,512]{1,0:T(8,128)(2,1)}, bf16[1024,512]{1,0:T(8,128)(2,1)}, u32[]{:S(2)}, u32[]{:S(2)}) collective-permute-start(bf16[1024,512]{1,0:T(8,128)(2,1)} %add_convert_fusion), channel_id=1, source_target_pairs={{0,2},{1,3},{2,0},{3,1},{4,6},{5,7},{6,4},{7,5},{8,10},{9,11},{10,... | collective-permute-start | bytes 3145736 | tf_op jit(solution)/shard_map/ppermute | solution.py:98
  190.5 14.3 %copy-start.2 = (bf16[1024,512]{1,0:T(8,128)(2,1)S(1)}, bf16[1024,512]{1,0:T(8,128)(2,1)}, u32[]{:S(2)}) copy-start(bf16[1024,512]{1,0:T(8,128)(2,1)} %param.12) | copy-start | bytes 3145732
Sparse Core Ops, SparseCore 0:
  14.5 121.1 all-gather.1

commit v8 on v7

--- a/solution.py
+++ b/solution.py
@@ -86,10 +86,7 @@
     rows_per = hidden.shape[0]
 
     def partial_block(partial, b):
-        at = b * rows_per
-        src = lax.dynamic_slice_in_dim(source, at, rows_per)
-        keep = lax.dynamic_slice_in_dim(live, at, rows_per)
-        return jnp.where(keep[:, None], partial[src], 0.0)
+        return partial[lax.dynamic_slice_in_dim(source, b * rows_per, rows_per)]
 
     pairs_core = [(i, i ^ 1) for i in range(n_mp)]
     from_core = lax.ppermute(partial_block(partial_live, me ^ 3), "mp", pairs_core)
@@ -102,6 +99,7 @@
         hidden_live, everything, (((0,), (0,)), ((), ())), preferred_element_type=jnp.float32
     )
     hidden_grad = (own_part + from_core_own) + from_chip.astype(jnp.float32)
+    hidden_grad = jnp.where(lax.dynamic_slice_in_dim(live, me * rows_per, rows_per)[:, None], hidden_grad, 0.0)
     grad_gate = (hidden_grad * up_in * slopes).astype(jnp.bfloat16)
     grad_up = (hidden_grad * activated).astype(jnp.bfloat16)
     return (grad_down, grad_gate, grad_up)

time: 217 us -> 210 us (0.968)
  other arithmetic: 27.8 us -> 21.4 us
    select_n x2 -> x0, other arithmetic: 6.5 us -> none  [partial_block(): return jnp.where(keep[:, None], partial[src], 0.0)]
    all_gather x1, waiting for transfers between devices: 59.1 us -> 54.4 us  [shards(): gathered = lax.all_gather(sent, 'dp', axis=0, tiled=True)]
    ppermute x1, waiting for transfers between devices: 12.7 us -> 17.2 us  [mp_gather(): lax.ppermute(hidden, 'mp', [(i, (i + half) % n_mp) for i in range(n_mp)])]
  transfers between devices with their start and end apart: 11 -> 11, of which waited for: 7 -> 7; matrix products, arithmetic and copies ran while one was open for 25% -> 26% of each run, Pallas kernels for 0% -> 0%
where the time goes in v8:
time: 210 us
  waiting for transfers between devices  82.9 us (39%)
  local copies, waits for them, and re-layouts  53.7 us (26%)
  other arithmetic  21.4 us (10%)
  matrix products  20.2 us (10%)
  starting transfers between devices  17.4 us (8%)
  between operations  14.2 us (7%)
    all_gather x1, waiting for transfers between devices, shards(): gathered = lax.all_gather(sent, 'dp', axis=0, tiled=True)  54.4 us
    gather x4, local copies, waits for them, and re-layouts, partial_block(): return partial[lax.dynamic_slice_in_dim(source, b * rows_per, rows_per)]  31.2 us
    ppermute x1, waiting for transfers between devices, mp_gather(): lax.ppermute(hidden, 'mp', [(i, (i + half) % n_mp) for i in range(n_mp)])  17.2 us
    ppermute x5, starting transfers between devices, dp_gather_small(): theirs = lax.ppermute(held, 'dp', [(i, i ^ step) for i in range(n)])  11.8 us
    gather x1, local copies, waits for them, and re-layouts, shards(): hidden_live = hidden_all[slot_of]  11.1 us
    dot_general x1, matrix products, shards(): lax.dot_general(hidden_live, everything, (((0,), (0,)), ((), ())), prefer...  10.4 us
    dot_general x1, matrix products, shards(): lax.dot_general(everything, down_weight, (((1,), (1,)), ((), ())), prefer...  9.82 us
    ppermute x1, waiting for transfers between devices, shards(): from_chip = lax.ppermute(to_chip, 'mp', [(i, i ^ 2) for i in range(n_mp)])  5.87 us
  transfers between devices with their start and end apart: 11, of which 7 were waited for; matrix products, arithmetic and copies ran while one was open for 26% of the time, Pallas kernels for 0%

profile of v8, /device:TPU:1, one launch (start us, length us, event | category | flops | bytes accessed | tf_op | source)
XLA Modules:
  0.0 209.8 jit_solution(445629079293870821)
XLA Ops:
  7.2 0.0 copy-start
  7.2 0.0 copy-start.1
  7.2 0.0 all-gather.2.cloned.1.call-start
  7.2 0.9 convert_multiply_fusion.4
  8.1 0.7 copy.16
  8.8 0.1 reduce-window.8
  8.9 0.1 reduce
  9.0 0.7 convert_reduce_fusion.1
  9.8 1.6 gather_fusion
  11.4 1.3 gather_fusion.2
  12.7 0.0 copy-done.1
  12.7 0.8 gather_fusion.1
  13.5 0.0 copy-start.4
  13.5 0.8 multiply_convert_fusion.1
  14.4 0.0 all-gather.2.cloned.1.call-update
  14.4 2.2 %fusion = bf16[1024,512]{1,0:T(8,128)(2,1)S(1)} fusion(bf16[1024,512]{1,0:T(8,128)(2,1)} %param.12, bf16[1024,512]{1,0:T(8,128)(2,1)} %param.11), kind=kLoop, calls=%fused_computation.15 | loop fusion | flops 4194304 | bytes 3145728 | tf_op jit(solution)/shard_map/convert_element_type | solution.py:58
  16.6 2.5 %collective-permute-start = (bf16[1024,512]{1,0:T(8,128)(2,1)S(1)}, bf16[1024,512]{1,0:T(8,128)(2,1)}, u32[]{:S(2)}, u32[]{:S(2)}) collective-permute-start(bf16[1024,512]{1,0:T(8,128)(2,1)S(1)} %fusion), channel_id=1, source_target_pairs={{0,2},{1,3},{2,0},{3,1},{4,6},{5,7},{6,4},{7,5},{8,10},{9,11},{10,... | collective-permute-start | bytes 3145736 | tf_op jit(solution)/shard_map/ppermute | solution.py:19
  19.1 0.0 copy-done.4
  19.1 1.3 collective-permute-start.2
  20.5 1.5 collective-permute-done.2
  22.0 3.0 %collective-permute-start.3 = (s32[2,32]{1,0:T(2,128)S(1)}, s32[2,32]{1,0:T(2,128)S(1)}, u32[]{:S(2)}, u32[]{:S(2)}) collective-permute-start(s32[2,32]{1,0:T(2,128)S(1)} %add_select_fusion.5), channel_id=1, source_target_pairs={{0,8},{4,12},{8,0},{12,4},{16,24},{20,28},{24,16},{28,20},{32,40},... | collective-permute-start | bytes 776 | tf_op jit(solution)/shard_map/ppermute | solution.py:34
  25.0 1.0 collective-permute-done.3
  26.0 1.3 collective-permute-start.4
  27.3 17.2 %collective-permute-done = bf16[1024,512]{1,0:T(8,128)(2,1)} collective-permute-done((bf16[1024,512]{1,0:T(8,128)(2,1)S(1)}, bf16[1024,512]{1,0:T(8,128)(2,1)}, u32[]{:S(2)}, u32[]{:S(2)}) %collective-permute-start) | collective-permute-done | bytes 1048608 | tf_op jit(solution)/shard_map/ppermute | solution.py:19
  44.4 2.7 %pad_maximum_fusion.1 = bf16[2,1024,512]{2,1,0:T(8,128)(2,1)} fusion(bf16[1,1024,512]{2,1,0:T(8,128)(2,1)} %bitcast.9, bf16[1,1024,512]{2,1,0:T(8,128)(2,1)S(1)} %bitcast.31), kind=kLoop, calls=%fused_computation.23 | loop fusion | flops 1048576 | bytes 4194304 | tf_op jit(solution)/shard_map/stack | solution.py:20
  47.2 1.3 collective-permute-start.1
  48.4 0.0 collective-permute-done.4
  48.4 2.8 %collective-permute-start.5 = (s32[8,32]{1,0:T(8,128)S(1)}, s32[8,32]{1,0:T(8,128)S(1)}, u32[]{:S(2)}, u32[]{:S(2)}) collective-permute-start(s32[8,32]{1,0:T(8,128)S(1)} %add_select_fusion.3), channel_id=1, source_target_pairs={{0,32},{4,36},{8,40},{12,44},{16,48},{20,52},{24,56},{28,60},{32,0... | collective-permute-start | bytes 3080 | tf_op jit(solution)/shard_map/ppermute | solution.py:34
  51.3 1.2 collective-permute-done.5
  52.5 3.4 %collective-permute-start.6 = (s32[16,32]{1,0:T(8,128)S(1)}, s32[16,32]{1,0:T(8,128)S(1)}, u32[]{:S(2)}, u32[]{:S(2)}) collective-permute-start(s32[16,32]{1,0:T(8,128)S(1)} %add_select_fusion.2), channel_id=1, source_target_pairs={{0,64},{4,68},{8,72},{12,76},{16,80},{20,84},{24,88},{28,92},{32,9... | collective-permute-start | bytes 6152 | tf_op jit(solution)/shard_map/ppermute | solution.py:34
  55.9 1.7 collective-permute-done.6
  57.6 0.2 reduce_window_sum.18
  57.8 0.1 add_bitcast_fusion
  57.9 0.1 copy.18
  58.0 0.1 copy.17
  58.0 0.4 convert_reduce_fusion
  58.4 0.1 subtract_add_fusion
  58.5 0.1 add.173
  58.6 0.2 iota_compare_fusion
  58.8 0.3 lt.92
  59.2 1.0 iota_add_fusion
  60.1 1.3 add.182
  61.6 0.0 collective-permute-done.1
  61.6 3.6 %pad_maximum_fusion = bf16[4,1024,512]{2,1,0:T(8,128)(2,1)} fusion(bf16[2,1024,512]{2,1,0:T(8,128)(2,1)} %collective-permute-done.1, bf16[1,1024,512]{2,1,0:T(8,128)(2,1)} %bitcast.9, bf16[1,1024,512]{2,1,0:T(8,128)(2,1)S(1)} %bitcast.32), kind=kLoop, calls=%fused_computation.9 | loop fusion | flops 4194304 | bytes 8388608 | tf_op jit(solution)/shard_map/concatenate | solution.py:22
  65.2 5.1 %gather_fusion.3 = bf16[4,1024,512]{2,1,0:T(8,128)(2,1)} fusion(bf16[4,1024,512]{2,1,0:T(8,128)(2,1)} %pad_maximum_fusion, s32[1024]{0:T(1024)S(1)} %pad_clamp_fusion.1), kind=kCustom, calls=%fused_computation.3 | custom fusion | bytes 8388624 | tf_op jit(solution)/shard_map/jit(_take)/gather | solution.py:25
  70.3 11.1 %gather_fusion.4 = bf16[2560,512]{1,0:T(8,128)(2,1)} fusion(bf16[4096,512]{1,0:T(8,128)(2,1)} %bitcast.30, s32[3072]{0:T(1024)S(1)} %pad_clamp_fusion), kind=kCustom, calls=%fused_computation.4 | custom fusion | bytes 5253120 | tf_op jit(solution)/shard_map/gather | solution.py:72
  81.4 54.4 %all-gather.2.cloned.1.call-done = bf16[2560,2048]{1,0:T(8,128)(2,1)} async-done(((bf16[80,2048]{1,0:T(8,128)(2,1)}), bf16[2560,2048]{1,0:T(8,128)(2,1)}) %all-gather.2.cloned.1.call-update) | async-done | bytes 10485776 | tf_op jit(solution)/shard_map/all_gather | solution.py:59
  135.7 0.0 copy-done
  135.7 9.8 %fusion.21 = f32[2560,512]{1,0:T(8,128)} fusion(bf16[2560,2048]{1,0:T(8,128)(2,1)} %all-gather.2.cloned.1.call-done, bf16[512,2048]{1,0:T(8,128)(2,1)S(1)} %copy-done), kind=kOutput, calls=%fused_computation.77 | convolution fusion | flops 5368709120 | bytes 17825792 | tf_op jit(solution)/shard_map/dot_general | solution.py:75
  145.6 7.8 %gather_fusion.6 = f32[1024,512]{1,0:T(8,128)} fusion(f32[2560,512]{1,0:T(8,128)} %fusion.21, s32[1024]{0:T(1024)S(1)} %get-tuple-element.27), kind=kCustom, calls=%fused_computation.6 | custom fusion | bytes 4198400 | tf_op jit(solution)/shard_map/gather | solution.py:89
  153.4 1.4 collective-permute-start.7
  154.8 7.8 %gather_fusion.5 = f32[1024,512]{1,0:T(8,128)} fusion(f32[2560,512]{1,0:T(8,128)} %fusion.21, s32[1024]{0:T(1024)S(1)} %get-tuple-element.28), kind=kCustom, calls=%fused_computation.5 | custom fusion | bytes 4198400 | tf_op jit(solution)/shard_map/gather | solution.py:89
  162.5 0.0 collective-permute-done.7
  162.5 3.5 %add_convert_fusion = bf16[1024,512]{1,0:T(8,128)(2,1)} fusion(f32[1024,512]{1,0:T(8,128)} %gather_fusion.5, f32[1024,512]{1,0:T(8,128)} %collective-permute-done.7), kind=kLoop, calls=%fused_computation.26 | loop fusion | flops 1048576 | bytes 5242880 | tf_op jit(solution)/shard_map/convert_element_type | solution.py:93
  166.1 7.8 %gather_fusion.8 = f32[1024,512]{1,0:T(8,128)} fusion(f32[2560,512]{1,0:T(8,128)} %fusion.21, s32[1024]{0:T(1024)S(1)} %get-tuple-element.25), kind=kCustom, calls=%fused_computation.8 | custom fusion | bytes 4198400 | tf_op jit(solution)/shard_map/gather | solution.py:89
  173.8 0.0 collective-permute-start.8
  173.8 0.0 copy-done.3
  173.8 0.4 collective-permute-start.9
  174.2 10.4 %fusion.20 = f32[512,2048]{1,0:T(8,128)} fusion(bf16[2560,512]{1,0:T(8,128)(2,1)} %gather_fusion.4, bf16[2560,2048]{1,0:T(8,128)(2,1)} %all-gather.2.cloned.1.call-done), kind=kOutput, calls=%fused_computation.76 | convolution fusion | flops 5368709120 | bytes 17301504 | tf_op jit(solution)/shard_map/dot_general | solution.py:98
  184.6 7.9 %gather_fusion.7 = f32[1024,512]{1,0:T(8,128)} fusion(f32[2560,512]{1,0:T(8,128)} %fusion.21, s32[1024]{0:T(1024)S(1)} %get-tuple-element.26), kind=kCustom, calls=%fused_computation.7 | custom fusion | bytes 4198400 | tf_op jit(solution)/shard_map/gather | solution.py:89
  192.5 5.9 %collective-permute-done.9 = bf16[1024,512]{1,0:T(8,128)(2,1)} collective-permute-done((bf16[1024,512]{1,0:T(8,128)(2,1)}, bf16[1024,512]{1,0:T(8,128)(2,1)}, u32[]{:S(2)}, u32[]{:S(2)}) %collective-permute-start.9) | collective-permute-done | bytes 1048608 | tf_op jit(solution)/shard_map/ppermute | solution.py:95
  198.4 0.0 collective-permute-done.8
  198.4 0.0 dynamic-slice-done
  198.4 4.6 %multiply_convert_fusion = (bf16[1024,512]{1,0:T(8,128)(2,1)}, bf16[1024,512]{1,0:T(8,128)(2,1)}) fusion(bf16[1024,512]{1,0:T(8,128)(2,1)} %param.11, bf16[1024,512]{1,0:T(8,128)(2,1)} %collective-permute-done.9, f32[1024,512]{1,0:T(8,128)} %gather_fusion.7, f32[1024,512]{1,0:T(8,128)} %collective-permute-done.8, pred[1024]{0:T(1024)(128)(4,1)S(1)} %dynamic-slice-done, ...), kind=kLoop, calls=%fused_computation.24 | loop fusion | flops 9961472 | bytes 9438208 | tf_op jit(solution)/shard_map/convert_element_type | solution.py:104
  (21 shorter events, 0.2 us)
Async XLA Ops:
  7.2 128.6 %copy-start = (bf16[512,2048]{1,0:T(8,128)(2,1)S(1)}, bf16[512,2048]{1,0:T(8,128)(2,1)}, u32[]{:S(2)}) copy-start(bf16[512,2048]{1,0:T(8,128)(2,1)} %param.13) | copy-start | bytes 6291460
  7.2 5.5 %copy-start.1 = (bf16[144,2048]{1,0:T(8,128)(2,1)S(1)}, bf16[144,2048]{1,0:T(8,128)(2,1)}, u32[]{:S(2)}) copy-start(bf16[144,2048]{1,0:T(8,128)(2,1)} %param.7) | copy-start | bytes 1769476
  7.2 128.5 %all-gather.2.cloned.1.call-start = ((), (), s32[]{:S(2)}) async-start(), calls=%async_computation | async-start | bytes 10813440 | tf_op jit(solution)/shard_map/all_gather | solution.py:59
  13.5 5.6 %copy-start.4 = (s32[1,32]{1,0:T(1,128)S(1)}, s32[1,32]{1,0:T(1,128)}, u32[]{:S(2)}) copy-start(s32[1,32]{1,0:T(1,128)} %param.10) | copy-start | bytes 388
  16.6 27.8 %collective-permute-start = (bf16[1024,512]{1,0:T(8,128)(2,1)S(1)}, bf16[1024,512]{1,0:T(8,128)(2,1)}, u32[]{:S(2)}, u32[]{:S(2)}) collective-permute-start(bf16[1024,512]{1,0:T(8,128)(2,1)S(1)} %fusion), channel_id=1, source_target_pairs={{0,2},{1,3},{2,0},{3,1},{4,6},{5,7},{6,4},{7,5},{8,10},{9,11},{10,... | collective-permute-start | bytes 3145736 | tf_op jit(solution)/shard_map/ppermute | solution.py:19
  19.1 2.8 %collective-permute-start.2 = (s32[1,32]{1,0:T(1,128)S(1)}, s32[1,32]{1,0:T(1,128)S(1)}, u32[]{:S(2)}, u32[]{:S(2)}) collective-permute-start(s32[1,32]{1,0:T(1,128)S(1)} %copy-done.4), channel_id=1, source_target_pairs={{0,4},{4,0},{8,12},{12,8},{16,20},{20,16},{24,28},{28,24},{32,36},... | collective-permute-start | bytes 392 | tf_op jit(solution)/shard_map/ppermute | solution.py:34
  22.0 4.0 %collective-permute-start.3 = (s32[2,32]{1,0:T(2,128)S(1)}, s32[2,32]{1,0:T(2,128)S(1)}, u32[]{:S(2)}, u32[]{:S(2)}) collective-permute-start(s32[2,32]{1,0:T(2,128)S(1)} %add_select_fusion.5), channel_id=1, source_target_pairs={{0,8},{4,12},{8,0},{12,4},{16,24},{20,28},{24,16},{28,20},{32,40},... | collective-permute-start | bytes 776 | tf_op jit(solution)/shard_map/ppermute | solution.py:34
  26.0 22.4 %collective-permute-start.4 = (s32[4,32]{1,0:T(4,128)S(1)}, s32[4,32]{1,0:T(4,128)S(1)}, u32[]{:S(2)}, u32[]{:S(2)}) collective-permute-start(s32[4,32]{1,0:T(4,128)S(1)} %add_select_fusion.4), channel_id=1, source_target_pairs={{0,16},{4,20},{8,24},{12,28},{16,0},{20,4},{24,8},{28,12},{32,48},... | collective-permute-start | bytes 1544 | tf_op jit(solution)/shard_map/ppermute | solution.py:34
  47.2 14.4 %collective-permute-start.1 = (bf16[2,1024,512]{2,1,0:T(8,128)(2,1)}, bf16[2,1024,512]{2,1,0:T(8,128)(2,1)}, u32[]{:S(2)}, u32[]{:S(2)}) collective-permute-start(bf16[2,1024,512]{2,1,0:T(8,128)(2,1)} %pad_maximum_fusion.1), channel_id=1, source_target_pairs={{0,1},{1,0},{2,3},{3,2},{4,5},{5,4},{6,7},{7,6},{8,9},{9,8},{10,11... | collective-permute-start | bytes 6291464 | tf_op jit(solution)/shard_map/ppermute | solution.py:21
  48.4 4.0 %collective-permute-start.5 = (s32[8,32]{1,0:T(8,128)S(1)}, s32[8,32]{1,0:T(8,128)S(1)}, u32[]{:S(2)}, u32[]{:S(2)}) collective-permute-start(s32[8,32]{1,0:T(8,128)S(1)} %add_select_fusion.3), channel_id=1, source_target_pairs={{0,32},{4,36},{8,40},{12,44},{16,48},{20,52},{24,56},{28,60},{32,0... | collective-permute-start | bytes 3080 | tf_op jit(solution)/shard_map/ppermute | solution.py:34
  52.5 5.2 %collective-permute-start.6 = (s32[16,32]{1,0:T(8,128)S(1)}, s32[16,32]{1,0:T(8,128)S(1)}, u32[]{:S(2)}, u32[]{:S(2)}) collective-permute-start(s32[16,32]{1,0:T(8,128)S(1)} %add_select_fusion.2), channel_id=1, source_target_pairs={{0,64},{4,68},{8,72},{12,76},{16,80},{20,84},{24,88},{28,92},{32,9... | collective-permute-start | bytes 6152 | tf_op jit(solution)/shard_map/ppermute | solution.py:34
  59.1 114.7 %copy-start.3 = (pred[4096]{0:T(1024)(128)(4,1)}, pred[4096]{0:T(1024)(128)(4,1)S(1)}, u32[]{:S(2)}) copy-start(pred[4096]{0:T(1024)(128)(4,1)S(1)} %lt.92) | copy-start | bytes 12292
  153.4 9.2 %collective-permute-start.7 = (f32[1024,512]{1,0:T(8,128)}, f32[1024,512]{1,0:T(8,128)}, u32[]{:S(2)}, u32[]{:S(2)}) collective-permute-start(f32[1024,512]{1,0:T(8,128)} %gather_fusion.6), channel_id=1, source_target_pairs={{0,1},{1,0},{2,3},{3,2},{4,5},{5,4},{6,7},{7,6},{8,9},{9,8},{10,11... | collective-permute-start | bytes 6291464 | tf_op jit(solution)/shard_map/ppermute | solution.py:92
  173.8 24.5 %collective-permute-start.8 = (f32[1024,512]{1,0:T(8,128)}, f32[1024,512]{1,0:T(8,128)}, u32[]{:S(2)}, u32[]{:S(2)}) collective-permute-start(f32[1024,512]{1,0:T(8,128)} %gather_fusion.8), channel_id=1, source_target_pairs={{0,1},{1,0},{2,3},{3,2},{4,5},{5,4},{6,7},{7,6},{8,9},{9,8},{10,11... | collective-permute-start | bytes 6291464 | tf_op jit(solution)/shard_map/ppermute | solution.py:96
  173.8 24.5 %collective-permute-start.9 = (bf16[1024,512]{1,0:T(8,128)(2,1)}, bf16[1024,512]{1,0:T(8,128)(2,1)}, u32[]{:S(2)}, u32[]{:S(2)}) collective-permute-start(bf16[1024,512]{1,0:T(8,128)(2,1)} %add_convert_fusion), channel_id=1, source_target_pairs={{0,2},{1,3},{2,0},{3,1},{4,6},{5,7},{6,4},{7,5},{8,10},{9,11},{10,... | collective-permute-start | bytes 3145736 | tf_op jit(solution)/shard_map/ppermute | solution.py:95
  184.6 13.7 %copy-start.2 = (bf16[1024,512]{1,0:T(8,128)(2,1)S(1)}, bf16[1024,512]{1,0:T(8,128)(2,1)}, u32[]{:S(2)}) copy-start(bf16[1024,512]{1,0:T(8,128)(2,1)} %param.12) | copy-start | bytes 3145732
  184.6 13.7 %dynamic-slice-start = ((pred[4096]{0:T(1024)(128)(4,1)}, s32[]{:T(128)}), pred[1024]{0:T(1024)(128)(4,1)S(1)}, s32[]{:S(2)}) async-start(pred[4096]{0:T(1024)(128)(4,1)} %copy-done.3, s32[]{:T(128)} %select_n.172), calls=%async_computation.1 | async-start | bytes 2560 | tf_op jit(solution)/shard_map/dynamic_slice | solution.py:102
Sparse Core Ops, SparseCore 0:
  14.5 121.1 all-gather.1

commit v9 on v8

--- a/solution.py
+++ b/solution.py
@@ -2,6 +2,7 @@
 import jax.numpy as jnp
 from jax import lax
 from jax.sharding import PartitionSpec as P
+
 
 SLOTS = 128
 LIVE = SLOTS * 5 // 8
@@ -38,7 +39,7 @@
     return held
 
 
-def shards(sample_grad, advantage, route_rows, route_count, gate_pre, up_pre, down_weight):
+def body(sample_grad, advantage, route_rows, route_count, gate_pre, up_pre, down_weight):
     learners = lax.axis_size("dp")
     capacity = SLOTS // learners
 
@@ -48,9 +49,13 @@
     before = own_end[None, :] <= pos[:, None]
     own_m = jnp.sum(before.astype(jnp.int32), axis=1)
     own_c = pos - jnp.sum(jnp.where(before, own[None, :], 0), axis=1)
-    picked = route_rows[0][own_m * capacity + own_c]
     weights = advantage.astype(jnp.float32) * (1.0 / 4096.0)
-    scaled = (sample_grad[picked].astype(jnp.float32) * weights[picked][:, None]).astype(jnp.bfloat16)
+    scaled_all = (sample_grad.astype(jnp.float32) * weights[:, None]).astype(jnp.bfloat16)
+    q_of = own_m * capacity + own_c
+    q_pick = (jnp.arange(SLOTS, dtype=jnp.int32)[None, :] == q_of[:, None]).astype(jnp.bfloat16)
+    r_pick = (route_rows[0][:SLOTS, None] == jnp.arange(sample_grad.shape[0], dtype=jnp.int32)[None, :])
+    pick = jnp.dot(q_pick, r_pick.astype(jnp.bfloat16), preferred_element_type=jnp.float32).astype(jnp.bfloat16)
+    scaled = jnp.dot(pick, scaled_all, preferred_element_type=jnp.float32).astype(jnp.bfloat16)
     sent, gate_late, up_late, own_late = lax.optimization_barrier((scaled, gate_pre, up_pre, route_count))
     gate_in = gate_late.astype(jnp.float32)
     up_in = up_late.astype(jnp.float32)
@@ -116,7 +121,7 @@
         P("dp", "mp"),
     )
     return jax.shard_map(
-        shards,
+        body,
         mesh=mesh,
         in_specs=placed,
         out_specs=(P("dp", "mp"), P("mp", "dp"), P("mp", "dp")),

time: 210 us -> 209 us (level)
  local copies, waits for them, and re-layouts: 53.7 us -> 50.8 us
  matrix products: 20.2 us -> 22.6 us
    gather x4 -> x1, local copies, waits for them, and re-layouts: 14.8 us -> 11.1 us  [body(): hidden_live = hidden_all[slot_of]]
    dot_general x2 -> x3, matrix products: 20.2 us -> 22.6 us  [the longest x1 10.4 us: body(): lax.dot_general(hidden_live, everything, (((0,), (0,)), ((), ())), prefer...]
    convert_element_type x4 -> x3, other arithmetic: 11.2 us -> 10.3 us  [the longest x1 4.61 us: body(): grad_up = (hidden_grad * activated).astype(jnp.bfloat16)]
where the time goes in v9:
time: 209 us; the launch traced here: 208 us
  waiting for transfers between devices  83 us (40%)
  local copies, waits for them, and re-layouts  50.8 us (24%)
  matrix products  22.6 us (11%)
  other arithmetic  20.3 us (10%)
  starting transfers between devices  17.5 us (8%)
  between operations  14.2 us (7%)
    all_gather x1, waiting for transfers between devices, body(): gathered = lax.all_gather(sent, 'dp', axis=0, tiled=True)  54.4 us
    gather x4, local copies, waits for them, and re-layouts, partial_block(): return partial[lax.dynamic_slice_in_dim(source, b * rows_per, rows_per)]  31.2 us
    ppermute x1, waiting for transfers between devices, mp_gather(): lax.ppermute(hidden, 'mp', [(i, (i + half) % n_mp) for i in range(n_mp)])  17.2 us
    ppermute x5, starting transfers between devices, dp_gather_small(): theirs = lax.ppermute(held, 'dp', [(i, i ^ step) for i in range(n)])  11.8 us
    gather x1, local copies, waits for them, and re-layouts, body(): hidden_live = hidden_all[slot_of]  11.1 us
    dot_general x1, matrix products, body(): lax.dot_general(hidden_live, everything, (((0,), (0,)), ((), ())), prefer...  10.4 us
    dot_general x1, matrix products, body(): lax.dot_general(everything, down_weight, (((1,), (1,)), ((), ())), prefer...  9.8 us
    ppermute x1, waiting for transfers between devices, body(): from_chip = lax.ppermute(to_chip, 'mp', [(i, i ^ 2) for i in range(n_mp)])  5.99 us
  transfers between devices with their start and end apart: 11, of which 7 were waited for; matrix products, arithmetic and copies ran while one was open for 26% of the time, Pallas kernels for 0%

profile of v9, /device:TPU:1, one launch (start us, length us, event | category | flops | bytes accessed | tf_op | source)
XLA Modules:
  0.0 208.4 jit_solution(468735442637707036)
XLA Ops:
  7.2 0.0 copy-start
  7.2 0.0 all-gather.2.cloned.1.call-start
  7.2 0.8 slice_bitcast_fusion
  8.0 0.7 convert_multiply_fusion.4
  8.7 0.7 copy.16
  9.4 0.1 reduce-window.8
  9.5 0.1 reduce
  9.6 0.7 convert_reduce_fusion.1
  10.4 0.0 copy-start.3
  10.4 2.4 %convolution_convert_fusion = bf16[80,2048]{1,0:T(8,128)(2,1)} fusion(bf16[144,2048]{1,0:T(8,128)(2,1)} %param.7, f32[144]{0:T(256)S(1)} %convert_multiply_fusion.4, s32[128]{0:T(128)S(1)} %slice_bitcast_fusion, s32[80]{0:T(128)S(1)} %subtract_add_fusion.1), kind=kOutput, calls=%fused_computation.12 | convolution fusion | flops 51223808 | bytes 918912 | tf_op jit(solution)/shard_map/dot_general | solution.py:58
  12.8 0.0 all-gather.2.cloned.1.call-update
  12.8 2.2 %fusion = bf16[1024,512]{1,0:T(8,128)(2,1)S(1)} fusion(bf16[1024,512]{1,0:T(8,128)(2,1)} %param.12, bf16[1024,512]{1,0:T(8,128)(2,1)} %param.11), kind=kLoop, calls=%fused_computation.13 | loop fusion | flops 4194304 | bytes 3145728 | tf_op jit(solution)/shard_map/convert_element_type | solution.py:63
  15.0 2.5 %collective-permute-start = (bf16[1024,512]{1,0:T(8,128)(2,1)S(1)}, bf16[1024,512]{1,0:T(8,128)(2,1)}, u32[]{:S(2)}, u32[]{:S(2)}) collective-permute-start(bf16[1024,512]{1,0:T(8,128)(2,1)S(1)} %fusion), channel_id=1, source_target_pairs={{0,2},{1,3},{2,0},{3,1},{4,6},{5,7},{6,4},{7,5},{8,10},{9,11},{10,... | collective-permute-start | bytes 3145736 | tf_op jit(solution)/shard_map/ppermute | solution.py:20
  17.5 0.0 copy-done.3
  17.5 1.3 collective-permute-start.2
  18.8 1.5 collective-permute-done.2
  20.3 3.0 %collective-permute-start.3 = (s32[2,32]{1,0:T(2,128)S(1)}, s32[2,32]{1,0:T(2,128)S(1)}, u32[]{:S(2)}, u32[]{:S(2)}) collective-permute-start(s32[2,32]{1,0:T(2,128)S(1)} %add_select_fusion.5), channel_id=1, source_target_pairs={{0,8},{4,12},{8,0},{12,4},{16,24},{20,28},{24,16},{28,20},{32,40},... | collective-permute-start | bytes 776 | tf_op jit(solution)/shard_map/ppermute | solution.py:35
  23.3 1.0 collective-permute-done.3
  24.4 1.3 collective-permute-start.4
  25.6 17.2 %collective-permute-done = bf16[1024,512]{1,0:T(8,128)(2,1)} collective-permute-done((bf16[1024,512]{1,0:T(8,128)(2,1)S(1)}, bf16[1024,512]{1,0:T(8,128)(2,1)}, u32[]{:S(2)}, u32[]{:S(2)}) %collective-permute-start) | collective-permute-done | bytes 1048608 | tf_op jit(solution)/shard_map/ppermute | solution.py:20
  42.8 2.7 %pad_maximum_fusion.1 = bf16[2,1024,512]{2,1,0:T(8,128)(2,1)} fusion(bf16[1,1024,512]{2,1,0:T(8,128)(2,1)} %bitcast.4, bf16[1,1024,512]{2,1,0:T(8,128)(2,1)S(1)} %bitcast.17), kind=kLoop, calls=%fused_computation.21 | loop fusion | flops 1048576 | bytes 4194304 | tf_op jit(solution)/shard_map/stack | solution.py:21
  45.5 1.3 collective-permute-start.1
  46.8 0.0 collective-permute-done.4
  46.8 2.8 %collective-permute-start.5 = (s32[8,32]{1,0:T(8,128)S(1)}, s32[8,32]{1,0:T(8,128)S(1)}, u32[]{:S(2)}, u32[]{:S(2)}) collective-permute-start(s32[8,32]{1,0:T(8,128)S(1)} %add_select_fusion.3), channel_id=1, source_target_pairs={{0,32},{4,36},{8,40},{12,44},{16,48},{20,52},{24,56},{28,60},{32,0... | collective-permute-start | bytes 3080 | tf_op jit(solution)/shard_map/ppermute | solution.py:35
  49.6 1.2 collective-permute-done.5
  50.9 3.4 %collective-permute-start.6 = (s32[16,32]{1,0:T(8,128)S(1)}, s32[16,32]{1,0:T(8,128)S(1)}, u32[]{:S(2)}, u32[]{:S(2)}) collective-permute-start(s32[16,32]{1,0:T(8,128)S(1)} %add_select_fusion.2), channel_id=1, source_target_pairs={{0,64},{4,68},{8,72},{12,76},{16,80},{20,84},{24,88},{28,92},{32,9... | collective-permute-start | bytes 6152 | tf_op jit(solution)/shard_map/ppermute | solution.py:35
  54.3 1.7 collective-permute-done.6
  56.0 0.2 reduce_window_sum.18
  56.2 0.1 add_bitcast_fusion
  56.3 0.1 copy.18
  56.4 0.1 copy.17
  56.4 0.4 convert_reduce_fusion
  56.8 0.1 subtract_add_fusion
  56.9 0.1 add.147
  57.0 0.2 iota_compare_fusion
  57.2 0.3 lt.69
  57.5 0.0 copy-start.2
  57.5 1.0 iota_add_fusion
  58.5 1.3 add.156
  59.9 0.0 collective-permute-done.1
  60.0 3.6 %pad_maximum_fusion = bf16[4,1024,512]{2,1,0:T(8,128)(2,1)} fusion(bf16[2,1024,512]{2,1,0:T(8,128)(2,1)} %collective-permute-done.1, bf16[1,1024,512]{2,1,0:T(8,128)(2,1)} %bitcast.4, bf16[1,1024,512]{2,1,0:T(8,128)(2,1)S(1)} %bitcast.18), kind=kLoop, calls=%fused_computation.6 | loop fusion | flops 4194304 | bytes 8388608 | tf_op jit(solution)/shard_map/concatenate | solution.py:23
  63.5 5.1 %gather_fusion = bf16[4,1024,512]{2,1,0:T(8,128)(2,1)} fusion(bf16[4,1024,512]{2,1,0:T(8,128)(2,1)} %pad_maximum_fusion, s32[1024]{0:T(1024)S(1)} %pad_clamp_fusion.1), kind=kCustom, calls=%fused_computation | custom fusion | bytes 8388624 | tf_op jit(solution)/shard_map/jit(_take)/gather | solution.py:26
  68.7 11.1 %gather_fusion.1 = bf16[2560,512]{1,0:T(8,128)(2,1)} fusion(bf16[4096,512]{1,0:T(8,128)(2,1)} %bitcast.16, s32[3072]{0:T(1024)S(1)} %pad_clamp_fusion), kind=kCustom, calls=%fused_computation.1 | custom fusion | bytes 5253120 | tf_op jit(solution)/shard_map/gather | solution.py:77
  79.7 54.4 %all-gather.2.cloned.1.call-done = bf16[2560,2048]{1,0:T(8,128)(2,1)} async-done(((bf16[80,2048]{1,0:T(8,128)(2,1)}), bf16[2560,2048]{1,0:T(8,128)(2,1)}) %all-gather.2.cloned.1.call-update) | async-done | bytes 10485776 | tf_op jit(solution)/shard_map/all_gather | solution.py:64
  134.1 0.0 copy-done
  134.1 9.8 %fusion.23 = f32[2560,512]{1,0:T(8,128)} fusion(bf16[2560,2048]{1,0:T(8,128)(2,1)} %all-gather.2.cloned.1.call-done, bf16[512,2048]{1,0:T(8,128)(2,1)S(1)} %copy-done), kind=kOutput, calls=%fused_computation.75 | convolution fusion | flops 5368709120 | bytes 17825792 | tf_op jit(solution)/shard_map/dot_general | solution.py:80
  143.9 7.8 %gather_fusion.3 = f32[1024,512]{1,0:T(8,128)} fusion(f32[2560,512]{1,0:T(8,128)} %fusion.23, s32[1024]{0:T(1024)S(1)} %get-tuple-element.27), kind=kCustom, calls=%fused_computation.3 | custom fusion | bytes 4198400 | tf_op jit(solution)/shard_map/gather | solution.py:94
  151.7 1.4 collective-permute-start.7
  153.1 7.8 %gather_fusion.2 = f32[1024,512]{1,0:T(8,128)} fusion(f32[2560,512]{1,0:T(8,128)} %fusion.23, s32[1024]{0:T(1024)S(1)} %get-tuple-element.28), kind=kCustom, calls=%fused_computation.2 | custom fusion | bytes 4198400 | tf_op jit(solution)/shard_map/gather | solution.py:94
  160.9 0.0 collective-permute-done.7
  160.9 3.5 %add_convert_fusion = bf16[1024,512]{1,0:T(8,128)(2,1)} fusion(f32[1024,512]{1,0:T(8,128)} %gather_fusion.2, f32[1024,512]{1,0:T(8,128)} %collective-permute-done.7), kind=kLoop, calls=%fused_computation.24 | loop fusion | flops 1048576 | bytes 5242880 | tf_op jit(solution)/shard_map/convert_element_type | solution.py:98
  164.4 7.8 %gather_fusion.5 = f32[1024,512]{1,0:T(8,128)} fusion(f32[2560,512]{1,0:T(8,128)} %fusion.23, s32[1024]{0:T(1024)S(1)} %get-tuple-element.25), kind=kCustom, calls=%fused_computation.5 | custom fusion | bytes 4198400 | tf_op jit(solution)/shard_map/gather | solution.py:94
  172.2 0.0 collective-permute-start.8
  172.2 0.0 copy-done.2
  172.2 0.5 collective-permute-start.9
  172.7 10.4 %fusion.22 = f32[512,2048]{1,0:T(8,128)} fusion(bf16[2560,512]{1,0:T(8,128)(2,1)} %gather_fusion.1, bf16[2560,2048]{1,0:T(8,128)(2,1)} %all-gather.2.cloned.1.call-done), kind=kOutput, calls=%fused_computation.74 | convolution fusion | flops 5368709120 | bytes 17301504 | tf_op jit(solution)/shard_map/dot_general | solution.py:103
  183.1 0.0 copy-start.1
  183.1 0.0 dynamic-slice-start
  183.1 7.9 %gather_fusion.4 = f32[1024,512]{1,0:T(8,128)} fusion(f32[2560,512]{1,0:T(8,128)} %fusion.23, s32[1024]{0:T(1024)S(1)} %get-tuple-element.26), kind=kCustom, calls=%fused_computation.4 | custom fusion | bytes 4198400 | tf_op jit(solution)/shard_map/gather | solution.py:94
  191.0 6.0 %collective-permute-done.9 = bf16[1024,512]{1,0:T(8,128)(2,1)} collective-permute-done((bf16[1024,512]{1,0:T(8,128)(2,1)}, bf16[1024,512]{1,0:T(8,128)(2,1)}, u32[]{:S(2)}, u32[]{:S(2)}) %collective-permute-start.9) | collective-permute-done | bytes 1048608 | tf_op jit(solution)/shard_map/ppermute | solution.py:100
  196.9 0.0 collective-permute-done.8
  196.9 0.0 copy-done.1
  196.9 0.0 dynamic-slice-done
  196.9 4.6 %multiply_convert_fusion = (bf16[1024,512]{1,0:T(8,128)(2,1)}, bf16[1024,512]{1,0:T(8,128)(2,1)}) fusion(bf16[1024,512]{1,0:T(8,128)(2,1)} %param.11, bf16[1024,512]{1,0:T(8,128)(2,1)} %collective-permute-done.9, f32[1024,512]{1,0:T(8,128)} %gather_fusion.4, f32[1024,512]{1,0:T(8,128)} %collective-permute-done.8, pred[1024]{0:T(1024)(128)(4,1)S(1)} %dynamic-slice-done, ...), kind=kLoop, calls=%fused_computation.22 | loop fusion | flops 9961472 | bytes 9438208 | tf_op jit(solution)/shard_map/convert_element_type | solution.py:109
  (14 shorter events, 0.1 us)
Async XLA Ops:
  7.2 127.0 %copy-start = (bf16[512,2048]{1,0:T(8,128)(2,1)S(1)}, bf16[512,2048]{1,0:T(8,128)(2,1)}, u32[]{:S(2)}) copy-start(bf16[512,2048]{1,0:T(8,128)(2,1)} %param.13) | copy-start | bytes 6291460
  7.2 126.9 %all-gather.2.cloned.1.call-start = ((), (), s32[]{:S(2)}) async-start(), calls=%async_computation | async-start | bytes 10813440 | tf_op jit(solution)/shard_map/all_gather | solution.py:64
  10.4 7.1 %copy-start.3 = (s32[1,32]{1,0:T(1,128)S(1)}, s32[1,32]{1,0:T(1,128)}, u32[]{:S(2)}) copy-start(s32[1,32]{1,0:T(1,128)} %param.10) | copy-start | bytes 388
  15.0 27.8 %collective-permute-start = (bf16[1024,512]{1,0:T(8,128)(2,1)S(1)}, bf16[1024,512]{1,0:T(8,128)(2,1)}, u32[]{:S(2)}, u32[]{:S(2)}) collective-permute-start(bf16[1024,512]{1,0:T(8,128)(2,1)S(1)} %fusion), channel_id=1, source_target_pairs={{0,2},{1,3},{2,0},{3,1},{4,6},{5,7},{6,4},{7,5},{8,10},{9,11},{10,... | collective-permute-start | bytes 3145736 | tf_op jit(solution)/shard_map/ppermute | solution.py:20
  17.5 2.8 %collective-permute-start.2 = (s32[1,32]{1,0:T(1,128)S(1)}, s32[1,32]{1,0:T(1,128)S(1)}, u32[]{:S(2)}, u32[]{:S(2)}) collective-permute-start(s32[1,32]{1,0:T(1,128)S(1)} %copy-done.3), channel_id=1, source_target_pairs={{0,4},{4,0},{8,12},{12,8},{16,20},{20,16},{24,28},{28,24},{32,36},... | collective-permute-start | bytes 392 | tf_op jit(solution)/shard_map/ppermute | solution.py:35
  20.3 4.0 %collective-permute-start.3 = (s32[2,32]{1,0:T(2,128)S(1)}, s32[2,32]{1,0:T(2,128)S(1)}, u32[]{:S(2)}, u32[]{:S(2)}) collective-permute-start(s32[2,32]{1,0:T(2,128)S(1)} %add_select_fusion.5), channel_id=1, source_target_pairs={{0,8},{4,12},{8,0},{12,4},{16,24},{20,28},{24,16},{28,20},{32,40},... | collective-permute-start | bytes 776 | tf_op jit(solution)/shard_map/ppermute | solution.py:35
  24.4 22.4 %collective-permute-start.4 = (s32[4,32]{1,0:T(4,128)S(1)}, s32[4,32]{1,0:T(4,128)S(1)}, u32[]{:S(2)}, u32[]{:S(2)}) collective-permute-start(s32[4,32]{1,0:T(4,128)S(1)} %add_select_fusion.4), channel_id=1, source_target_pairs={{0,16},{4,20},{8,24},{12,28},{16,0},{20,4},{24,8},{28,12},{32,48},... | collective-permute-start | bytes 1544 | tf_op jit(solution)/shard_map/ppermute | solution.py:35
  45.5 14.4 %collective-permute-start.1 = (bf16[2,1024,512]{2,1,0:T(8,128)(2,1)}, bf16[2,1024,512]{2,1,0:T(8,128)(2,1)}, u32[]{:S(2)}, u32[]{:S(2)}) collective-permute-start(bf16[2,1024,512]{2,1,0:T(8,128)(2,1)} %pad_maximum_fusion.1), channel_id=1, source_target_pairs={{0,1},{1,0},{2,3},{3,2},{4,5},{5,4},{6,7},{7,6},{8,9},{9,8},{10,11... | collective-permute-start | bytes 6291464 | tf_op jit(solution)/shard_map/ppermute | solution.py:22
  46.8 4.0 %collective-permute-start.5 = (s32[8,32]{1,0:T(8,128)S(1)}, s32[8,32]{1,0:T(8,128)S(1)}, u32[]{:S(2)}, u32[]{:S(2)}) collective-permute-start(s32[8,32]{1,0:T(8,128)S(1)} %add_select_fusion.3), channel_id=1, source_target_pairs={{0,32},{4,36},{8,40},{12,44},{16,48},{20,52},{24,56},{28,60},{32,0... | collective-permute-start | bytes 3080 | tf_op jit(solution)/shard_map/ppermute | solution.py:35
  50.9 5.2 %collective-permute-start.6 = (s32[16,32]{1,0:T(8,128)S(1)}, s32[16,32]{1,0:T(8,128)S(1)}, u32[]{:S(2)}, u32[]{:S(2)}) collective-permute-start(s32[16,32]{1,0:T(8,128)S(1)} %add_select_fusion.2), channel_id=1, source_target_pairs={{0,64},{4,68},{8,72},{12,76},{16,80},{20,84},{24,88},{28,92},{32,9... | collective-permute-start | bytes 6152 | tf_op jit(solution)/shard_map/ppermute | solution.py:35
  57.5 114.7 %copy-start.2 = (pred[4096]{0:T(1024)(128)(4,1)}, pred[4096]{0:T(1024)(128)(4,1)S(1)}, u32[]{:S(2)}) copy-start(pred[4096]{0:T(1024)(128)(4,1)S(1)} %lt.69) | copy-start | bytes 12292
  151.7 9.2 %collective-permute-start.7 = (f32[1024,512]{1,0:T(8,128)}, f32[1024,512]{1,0:T(8,128)}, u32[]{:S(2)}, u32[]{:S(2)}) collective-permute-start(f32[1024,512]{1,0:T(8,128)} %gather_fusion.3), channel_id=1, source_target_pairs={{0,1},{1,0},{2,3},{3,2},{4,5},{5,4},{6,7},{7,6},{8,9},{9,8},{10,11... | collective-permute-start | bytes 6291464 | tf_op jit(solution)/shard_map/ppermute | solution.py:97
  172.2 24.8 %collective-permute-start.8 = (f32[1024,512]{1,0:T(8,128)}, f32[1024,512]{1,0:T(8,128)}, u32[]{:S(2)}, u32[]{:S(2)}) collective-permute-start(f32[1024,512]{1,0:T(8,128)} %gather_fusion.5), channel_id=1, source_target_pairs={{0,1},{1,0},{2,3},{3,2},{4,5},{5,4},{6,7},{7,6},{8,9},{9,8},{10,11... | collective-permute-start | bytes 6291464 | tf_op jit(solution)/shard_map/ppermute | solution.py:101
  172.2 24.7 %collective-permute-start.9 = (bf16[1024,512]{1,0:T(8,128)(2,1)}, bf16[1024,512]{1,0:T(8,128)(2,1)}, u32[]{:S(2)}, u32[]{:S(2)}) collective-permute-start(bf16[1024,512]{1,0:T(8,128)(2,1)} %add_convert_fusion), channel_id=1, source_target_pairs={{0,2},{1,3},{2,0},{3,1},{4,6},{5,7},{6,4},{7,5},{8,10},{9,11},{10,... | collective-permute-start | bytes 3145736 | tf_op jit(solution)/shard_map/ppermute | solution.py:100
  183.1 13.9 %copy-start.1 = (bf16[1024,512]{1,0:T(8,128)(2,1)S(1)}, bf16[1024,512]{1,0:T(8,128)(2,1)}, u32[]{:S(2)}) copy-start(bf16[1024,512]{1,0:T(8,128)(2,1)} %param.12) | copy-start | bytes 3145732
  183.1 13.9 %dynamic-slice-start = ((pred[4096]{0:T(1024)(128)(4,1)}, s32[]{:T(128)}), pred[1024]{0:T(1024)(128)(4,1)S(1)}, s32[]{:S(2)}) async-start(pred[4096]{0:T(1024)(128)(4,1)} %copy-done.2, s32[]{:T(128)} %select_n.149), calls=%async_computation.1 | async-start | bytes 2560 | tf_op jit(solution)/shard_map/dynamic_slice | solution.py:107
Sparse Core Ops, SparseCore 0:
  12.9 121.1 all-gather.1

commit v10 on v9

--- a/solution.py
+++ b/solution.py
@@ -75,20 +75,25 @@
     sender = jnp.arange(learners, dtype=jnp.int32)[:, None]
     slot_of = (m_of * SLOTS + sender * capacity + c_of).reshape(-1)
     hidden_live = hidden_all[slot_of]
-    everything, hidden_live = lax.optimization_barrier((everything, hidden_live))
+    me = lax.axis_index("mp")
+    rows_per = hidden.shape[0]
+    lane = jnp.arange(capacity, dtype=jnp.int32)
+    live = (lane[None, None, :] < counts.T[:, :, None]).reshape(-1)
+    keep = lax.dynamic_slice_in_dim(live, me * rows_per, rows_per)[:, None]
+    gate_factor = jnp.where(keep, up_in * slopes, 0.0)
+    up_factor = jnp.where(keep, activated, 0.0)
+    everything, hidden_live, gate_factor, up_factor = lax.optimization_barrier(
+        (everything, hidden_live, gate_factor, up_factor)
+    )
 
     partial_live = lax.dot_general(
         everything, down_weight, (((1,), (1,)), ((), ())), preferred_element_type=jnp.float32
     )
 
-    lane = jnp.arange(capacity, dtype=jnp.int32)
-    live = (lane[None, None, :] < counts.T[:, :, None]).reshape(-1)
     first = jnp.arange(learners, dtype=jnp.int32)[None, :] * LIVE + starts.T
     source = jnp.where(live, (first[:, :, None] + lane[None, None, :]).reshape(-1), 0)
 
-    me = lax.axis_index("mp")
     n_mp = lax.axis_size("mp")
-    rows_per = hidden.shape[0]
 
     def partial_block(partial, b):
         return partial[lax.dynamic_slice_in_dim(source, b * rows_per, rows_per)]
@@ -104,9 +109,8 @@
         hidden_live, everything, (((0,), (0,)), ((), ())), preferred_element_type=jnp.float32
     )
     hidden_grad = (own_part + from_core_own) + from_chip.astype(jnp.float32)
-    hidden_grad = jnp.where(lax.dynamic_slice_in_dim(live, me * rows_per, rows_per)[:, None], hidden_grad, 0.0)
-    grad_gate = (hidden_grad * up_in * slopes).astype(jnp.bfloat16)
-    grad_up = (hidden_grad * activated).astype(jnp.bfloat16)
+    grad_gate = (hidden_grad * gate_factor).astype(jnp.bfloat16)
+    grad_up = (hidden_grad * up_factor).astype(jnp.bfloat16)
     return (grad_down, grad_gate, grad_up)
 
 

time: 209 us -> 215 us (1.029)
  starting transfers between devices: 17.5 us -> 26.1 us
  waiting for transfers between devices: 83 us -> 78.9 us
  other arithmetic: 20.3 us -> 22.5 us
    all_gather x1, waiting for transfers between devices: 54.4 us -> 42.6 us  [body(): gathered = lax.all_gather(sent, 'dp', axis=0, tiled=True)]
    ppermute x1, starting transfers between devices: 1.25 us -> 9.86 us  [mp_gather(): near = lax.ppermute(pair, 'mp', [(i, i ^ 1) for i in range(n_mp)])]
    ppermute x1, waiting for transfers between devices: 17.2 us -> 23.9 us  [mp_gather(): lax.ppermute(hidden, 'mp', [(i, (i + half) % n_mp) for i in range(n_mp)])]
    select_n x0 -> x1, other arithmetic: none -> 4.06 us  [body(): gate_factor = jnp.where(keep, up_in * slopes, 0.0)]
    convert_element_type x2 -> x1, other arithmetic: 6.8 us -> 6.27 us  [body(): grad_up = (hidden_grad * up_factor).astype(jnp.bfloat16)]
  transfers between devices with their start and end apart: 11 -> 11, of which waited for: 7 -> 9; matrix products, arithmetic and copies ran while one was open for 26% -> 26% of each run, Pallas kernels for 0% -> 0%
where the time goes in v10:
time: 215 us
  waiting for transfers between devices  78.9 us (37%)
  local copies, waits for them, and re-layouts  50.7 us (24%)
  starting transfers between devices  26.1 us (12%)
  matrix products  22.6 us (11%)
  other arithmetic  22.5 us (10%)
  between operations  14.1 us (7%)
    all_gather x1, waiting for transfers between devices, body(): gathered = lax.all_gather(sent, 'dp', axis=0, tiled=True)  42.6 us
    gather x4, local copies, waits for them, and re-layouts, partial_block(): return partial[lax.dynamic_slice_in_dim(source, b * rows_per, rows_per)]  31.1 us
    ppermute x1, waiting for transfers between devices, mp_gather(): lax.ppermute(hidden, 'mp', [(i, (i + half) % n_mp) for i in range(n_mp)])  23.9 us
    ppermute x5, starting transfers between devices, dp_gather_small(): theirs = lax.ppermute(held, 'dp', [(i, i ^ step) for i in range(n)])  13.3 us
    gather x1, local copies, waits for them, and re-layouts, body(): hidden_live = hidden_all[slot_of]  11.1 us
    dot_general x1, matrix products, body(): lax.dot_general(hidden_live, everything, (((0,), (0,)), ((), ())), prefer...  10.4 us
    ppermute x1, starting transfers between devices, mp_gather(): near = lax.ppermute(pair, 'mp', [(i, i ^ 1) for i in range(n_mp)])  9.86 us
    dot_general x1, matrix products, body(): lax.dot_general(everything, down_weight, (((1,), (1,)), ((), ())), prefer...  9.8 us
  transfers between devices with their start and end apart: 11, of which 9 were waited for; matrix products, arithmetic and copies ran while one was open for 26% of the time, Pallas kernels for 0%

profile of v10, /device:TPU:1, one launch (start us, length us, event | category | flops | bytes accessed | tf_op | source)
XLA Modules:
  0.0 214.9 jit_solution(5428274886911451320)
XLA Ops:
  7.2 0.0 copy-start
  7.2 0.0 all-gather.2.cloned.1.call-start
  7.2 0.8 slice_bitcast_fusion
  8.0 0.7 convert_multiply_fusion.4
  8.7 0.7 copy.16
  9.4 0.1 reduce-window.8
  9.5 0.1 reduce
  9.6 0.7 convert_reduce_fusion.1
  10.4 2.4 %convolution_convert_fusion = bf16[80,2048]{1,0:T(8,128)(2,1)} fusion(bf16[144,2048]{1,0:T(8,128)(2,1)} %param.7, f32[144]{0:T(256)S(1)} %convert_multiply_fusion.4, s32[128]{0:T(128)S(1)} %slice_bitcast_fusion, s32[80]{0:T(128)S(1)} %subtract_add_fusion.1), kind=kOutput, calls=%fused_computation.12 | convolution fusion | flops 51223808 | bytes 918912 | tf_op jit(solution)/shard_map/dot_general | solution.py:58
  12.8 0.0 all-gather.2.cloned.1.call-update
  12.8 2.2 %collective-permute-start.2 = (s32[1,32]{1,0:T(1,128)}, s32[1,32]{1,0:T(1,128)S(1)}, u32[]{:S(2)}, u32[]{:S(2)}) collective-permute-start(s32[1,32]{1,0:T(1,128)} %param.10), channel_id=1, source_target_pairs={{0,4},{4,0},{8,12},{12,8},{16,20},{20,16},{24,28},{28,24},{32,36},... | collective-permute-start | bytes 392 | tf_op jit(solution)/shard_map/ppermute | solution.py:35
  15.0 1.1 collective-permute-done.2
  16.1 0.7 add_select_fusion.4
  16.8 3.1 %collective-permute-start.3 = (s32[2,32]{1,0:T(2,128)S(1)}, s32[2,32]{1,0:T(2,128)S(1)}, u32[]{:S(2)}, u32[]{:S(2)}) collective-permute-start(s32[2,32]{1,0:T(2,128)S(1)} %add_select_fusion.4), channel_id=1, source_target_pairs={{0,8},{4,12},{8,0},{12,4},{16,24},{20,28},{24,16},{28,20},{32,40},... | collective-permute-start | bytes 776 | tf_op jit(solution)/shard_map/ppermute | solution.py:35
  19.9 1.0 collective-permute-done.3
  20.9 1.3 collective-permute-start.4
  22.2 1.2 collective-permute-done.4
  23.4 2.9 %collective-permute-start.5 = (s32[8,32]{1,0:T(8,128)S(1)}, s32[8,32]{1,0:T(8,128)S(1)}, u32[]{:S(2)}, u32[]{:S(2)}) collective-permute-start(s32[8,32]{1,0:T(8,128)S(1)} %add_select_fusion.2), channel_id=1, source_target_pairs={{0,32},{4,36},{8,40},{12,44},{16,48},{20,52},{24,56},{28,60},{32,0... | collective-permute-start | bytes 3080 | tf_op jit(solution)/shard_map/ppermute | solution.py:35
  26.3 1.1 collective-permute-done.5
  27.5 3.7 %collective-permute-start.6 = (s32[16,32]{1,0:T(8,128)S(1)}, s32[16,32]{1,0:T(8,128)S(1)}, u32[]{:S(2)}, u32[]{:S(2)}) collective-permute-start(s32[16,32]{1,0:T(8,128)S(1)} %add_select_fusion.1), channel_id=1, source_target_pairs={{0,64},{4,68},{8,72},{12,76},{16,80},{20,84},{24,88},{28,92},{32,9... | collective-permute-start | bytes 6152 | tf_op jit(solution)/shard_map/ppermute | solution.py:35
  31.2 1.5 collective-permute-done.6
  32.6 0.1 copy.17
  32.7 0.2 iota_compare_fusion
  32.9 0.3 lt.69
  33.3 4.1 %fusion.1 = (f32[1024,512]{1,0:T(8,128)}, bf16[1024,512]{1,0:T(8,128)(2,1)S(1)}, f32[1024,512]{1,0:T(8,128)}) fusion(bf16[1024,512]{1,0:T(8,128)(2,1)} %param.12, bf16[1024,512]{1,0:T(8,128)(2,1)} %param.11, pred[1024]{0:T(1024)(128)(4,1)S(1)} %dynamic_slice.15), kind=kLoop, calls=%fused_computation.14 | loop fusion | flops 7864320 | bytes 7341056 | tf_op jit(solution)/shard_map/jit(_where)/select_n | solution.py:83
  37.3 1.2 collective-permute-start
  38.5 23.9 %collective-permute-done = bf16[1024,512]{1,0:T(8,128)(2,1)S(1)} collective-permute-done((bf16[1024,512]{1,0:T(8,128)(2,1)S(1)}, bf16[1024,512]{1,0:T(8,128)(2,1)S(1)}, u32[]{:S(2)}, u32[]{:S(2)}) %collective-permute-start) | collective-permute-done | bytes 1048608 | tf_op jit(solution)/shard_map/ppermute | solution.py:20
  62.4 0.0 copy-start.1
  62.4 1.6 pad_maximum_fusion.1
  64.1 0.0 copy-done.1
  64.1 9.9 %collective-permute-start.1 = (bf16[2,1024,512]{2,1,0:T(8,128)(2,1)}, bf16[2,1024,512]{2,1,0:T(8,128)(2,1)}, u32[]{:S(2)}, u32[]{:S(2)}) collective-permute-start(bf16[2,1024,512]{2,1,0:T(8,128)(2,1)} %pad_maximum_fusion.1), channel_id=1, source_target_pairs={{0,1},{1,0},{2,3},{3,2},{4,5},{5,4},{6,7},{7,6},{8,9},{9,8},{10,11... | collective-permute-start | bytes 6291464 | tf_op jit(solution)/shard_map/ppermute | solution.py:22
  74.0 0.2 reduce_window_sum.18
  74.2 0.1 add_bitcast_fusion
  74.3 0.1 copy.18
  74.3 0.4 convert_reduce_fusion
  74.7 0.1 subtract_add_fusion
  74.8 0.1 add.147
  74.9 1.0 iota_add_fusion
  75.9 1.3 add.157
  77.3 0.8 collective-permute-done.1
  78.1 3.6 %pad_maximum_fusion = bf16[4,1024,512]{2,1,0:T(8,128)(2,1)} fusion(bf16[2,1024,512]{2,1,0:T(8,128)(2,1)} %collective-permute-done.1, bf16[1,1024,512]{2,1,0:T(8,128)(2,1)} %bitcast.20, bf16[1,1024,512]{2,1,0:T(8,128)(2,1)S(1)} %bitcast.18), kind=kLoop, calls=%fused_computation.6 | loop fusion | flops 4194304 | bytes 8388608 | tf_op jit(solution)/shard_map/concatenate | solution.py:23
  81.7 5.1 %gather_fusion = bf16[4,1024,512]{2,1,0:T(8,128)(2,1)} fusion(bf16[4,1024,512]{2,1,0:T(8,128)(2,1)} %pad_maximum_fusion, s32[1024]{0:T(1024)S(1)} %pad_clamp_fusion.1), kind=kCustom, calls=%fused_computation | custom fusion | bytes 8388624 | tf_op jit(solution)/shard_map/jit(_take)/gather | solution.py:26
  86.7 11.1 %gather_fusion.1 = bf16[2560,512]{1,0:T(8,128)(2,1)} fusion(bf16[4096,512]{1,0:T(8,128)(2,1)} %bitcast.16, s32[3072]{0:T(1024)S(1)} %pad_clamp_fusion), kind=kCustom, calls=%fused_computation.1 | custom fusion | bytes 5253120 | tf_op jit(solution)/shard_map/gather | solution.py:77
  97.8 42.6 %all-gather.2.cloned.1.call-done = bf16[2560,2048]{1,0:T(8,128)(2,1)} async-done(((bf16[80,2048]{1,0:T(8,128)(2,1)}), bf16[2560,2048]{1,0:T(8,128)(2,1)}) %all-gather.2.cloned.1.call-update) | async-done | bytes 10485776 | tf_op jit(solution)/shard_map/all_gather | solution.py:64
  140.4 0.0 copy-done
  140.4 9.8 %fusion.22 = f32[2560,512]{1,0:T(8,128)} fusion(bf16[2560,2048]{1,0:T(8,128)(2,1)} %all-gather.2.cloned.1.call-done, bf16[512,2048]{1,0:T(8,128)(2,1)S(1)} %copy-done), kind=kOutput, calls=%fused_computation.76 | convolution fusion | flops 5368709120 | bytes 17825792 | tf_op jit(solution)/shard_map/dot_general | solution.py:89
  150.2 7.8 %gather_fusion.3 = f32[1024,512]{1,0:T(8,128)} fusion(f32[2560,512]{1,0:T(8,128)} %fusion.22, s32[1024]{0:T(1024)S(1)} %get-tuple-element.34), kind=kCustom, calls=%fused_computation.3 | custom fusion | bytes 4198400 | tf_op jit(solution)/shard_map/gather | solution.py:99
  158.0 1.4 collective-permute-start.7
  159.4 7.8 %gather_fusion.2 = f32[1024,512]{1,0:T(8,128)} fusion(f32[2560,512]{1,0:T(8,128)} %fusion.22, s32[1024]{0:T(1024)S(1)} %get-tuple-element.35), kind=kCustom, calls=%fused_computation.2 | custom fusion | bytes 4198400 | tf_op jit(solution)/shard_map/gather | solution.py:99
  167.1 0.0 collective-permute-done.7
  167.1 2.6 %add_convert_fusion = bf16[1024,512]{1,0:T(8,128)(2,1)S(1)} fusion(f32[1024,512]{1,0:T(8,128)} %gather_fusion.2, f32[1024,512]{1,0:T(8,128)} %collective-permute-done.7), kind=kLoop, calls=%fused_computation.24 | loop fusion | flops 1048576 | bytes 5242880 | tf_op jit(solution)/shard_map/convert_element_type | solution.py:103
  169.7 7.8 %gather_fusion.5 = f32[1024,512]{1,0:T(8,128)} fusion(f32[2560,512]{1,0:T(8,128)} %fusion.22, s32[1024]{0:T(1024)S(1)} %get-tuple-element.32), kind=kCustom, calls=%fused_computation.5 | custom fusion | bytes 4198400 | tf_op jit(solution)/shard_map/gather | solution.py:99
  177.5 0.0 collective-permute-start.8
  177.5 0.4 collective-permute-start.9
  177.9 10.4 %fusion.21 = f32[512,2048]{1,0:T(8,128)} fusion(bf16[2560,512]{1,0:T(8,128)(2,1)} %gather_fusion.1, bf16[2560,2048]{1,0:T(8,128)(2,1)} %all-gather.2.cloned.1.call-done), kind=kOutput, calls=%fused_computation.75 | convolution fusion | flops 5368709120 | bytes 17301504 | tf_op jit(solution)/shard_map/dot_general | solution.py:108
  188.3 7.8 %gather_fusion.4 = f32[1024,512]{1,0:T(8,128)} fusion(f32[2560,512]{1,0:T(8,128)} %fusion.22, s32[1024]{0:T(1024)S(1)} %get-tuple-element.33), kind=kCustom, calls=%fused_computation.4 | custom fusion | bytes 4198400 | tf_op jit(solution)/shard_map/gather | solution.py:99
  196.1 5.8 %collective-permute-done.9 = bf16[1024,512]{1,0:T(8,128)(2,1)} collective-permute-done((bf16[1024,512]{1,0:T(8,128)(2,1)S(1)}, bf16[1024,512]{1,0:T(8,128)(2,1)}, u32[]{:S(2)}, u32[]{:S(2)}) %collective-permute-start.9) | collective-permute-done | bytes 1048608 | tf_op jit(solution)/shard_map/ppermute | solution.py:105
  201.8 0.0 collective-permute-done.8
  201.8 6.3 %multiply_convert_fusion = (bf16[1024,512]{1,0:T(8,128)(2,1)}, bf16[1024,512]{1,0:T(8,128)(2,1)}) fusion(f32[1024,512]{1,0:T(8,128)} %get-tuple-element.22, bf16[1024,512]{1,0:T(8,128)(2,1)} %collective-permute-done.9, f32[1024,512]{1,0:T(8,128)} %gather_fusion.4, f32[1024,512]{1,0:T(8,128)} %collective-permute-done.8, f32[1024,512]{1,0:T(8,128)} %get-tuple-element.21), kind=kLoop, calls=%fused_computation.21 | loop fusion | flops 3670016 | bytes 11534336 | tf_op jit(solution)/shard_map/convert_element_type | solution.py:113
  (14 shorter events, 0.1 us)
Async XLA Ops:
  7.2 133.2 %copy-start = (bf16[512,2048]{1,0:T(8,128)(2,1)S(1)}, bf16[512,2048]{1,0:T(8,128)(2,1)}, u32[]{:S(2)}) copy-start(bf16[512,2048]{1,0:T(8,128)(2,1)} %param.13) | copy-start | bytes 6291460
  7.2 133.2 %all-gather.2.cloned.1.call-start = ((), (), s32[]{:S(2)}) async-start(), calls=%async_computation | async-start | bytes 10813440 | tf_op jit(solution)/shard_map/all_gather | solution.py:64
  12.8 3.3 %collective-permute-start.2 = (s32[1,32]{1,0:T(1,128)}, s32[1,32]{1,0:T(1,128)S(1)}, u32[]{:S(2)}, u32[]{:S(2)}) collective-permute-start(s32[1,32]{1,0:T(1,128)} %param.10), channel_id=1, source_target_pairs={{0,4},{4,0},{8,12},{12,8},{16,20},{20,16},{24,28},{28,24},{32,36},... | collective-permute-start | bytes 392 | tf_op jit(solution)/shard_map/ppermute | solution.py:35
  16.8 4.1 %collective-permute-start.3 = (s32[2,32]{1,0:T(2,128)S(1)}, s32[2,32]{1,0:T(2,128)S(1)}, u32[]{:S(2)}, u32[]{:S(2)}) collective-permute-start(s32[2,32]{1,0:T(2,128)S(1)} %add_select_fusion.4), channel_id=1, source_target_pairs={{0,8},{4,12},{8,0},{12,4},{16,24},{20,28},{24,16},{28,20},{32,40},... | collective-permute-start | bytes 776 | tf_op jit(solution)/shard_map/ppermute | solution.py:35
  20.9 2.5 %collective-permute-start.4 = (s32[4,32]{1,0:T(4,128)S(1)}, s32[4,32]{1,0:T(4,128)S(1)}, u32[]{:S(2)}, u32[]{:S(2)}) collective-permute-start(s32[4,32]{1,0:T(4,128)S(1)} %add_select_fusion.3), channel_id=1, source_target_pairs={{0,16},{4,20},{8,24},{12,28},{16,0},{20,4},{24,8},{28,12},{32,48},... | collective-permute-start | bytes 1544 | tf_op jit(solution)/shard_map/ppermute | solution.py:35
  23.4 4.0 %collective-permute-start.5 = (s32[8,32]{1,0:T(8,128)S(1)}, s32[8,32]{1,0:T(8,128)S(1)}, u32[]{:S(2)}, u32[]{:S(2)}) collective-permute-start(s32[8,32]{1,0:T(8,128)S(1)} %add_select_fusion.2), channel_id=1, source_target_pairs={{0,32},{4,36},{8,40},{12,44},{16,48},{20,52},{24,56},{28,60},{32,0... | collective-permute-start | bytes 3080 | tf_op jit(solution)/shard_map/ppermute | solution.py:35
  27.5 5.2 %collective-permute-start.6 = (s32[16,32]{1,0:T(8,128)S(1)}, s32[16,32]{1,0:T(8,128)S(1)}, u32[]{:S(2)}, u32[]{:S(2)}) collective-permute-start(s32[16,32]{1,0:T(8,128)S(1)} %add_select_fusion.1), channel_id=1, source_target_pairs={{0,64},{4,68},{8,72},{12,76},{16,80},{20,84},{24,88},{28,92},{32,9... | collective-permute-start | bytes 6152 | tf_op jit(solution)/shard_map/ppermute | solution.py:35
  37.3 25.1 %collective-permute-start = (bf16[1024,512]{1,0:T(8,128)(2,1)S(1)}, bf16[1024,512]{1,0:T(8,128)(2,1)S(1)}, u32[]{:S(2)}, u32[]{:S(2)}) collective-permute-start(bf16[1024,512]{1,0:T(8,128)(2,1)S(1)} %get-tuple-element.30), channel_id=1, source_target_pairs={{0,2},{1,3},{2,0},{3,1},{4,6},{5,7},{6,4},{7,5},{8,10},{9,11},{10,... | collective-permute-start | bytes 3145736 | tf_op jit(solution)/shard_map/ppermute | solution.py:20
  62.4 1.7 copy-start.1
  64.1 14.0 %collective-permute-start.1 = (bf16[2,1024,512]{2,1,0:T(8,128)(2,1)}, bf16[2,1024,512]{2,1,0:T(8,128)(2,1)}, u32[]{:S(2)}, u32[]{:S(2)}) collective-permute-start(bf16[2,1024,512]{2,1,0:T(8,128)(2,1)} %pad_maximum_fusion.1), channel_id=1, source_target_pairs={{0,1},{1,0},{2,3},{3,2},{4,5},{5,4},{6,7},{7,6},{8,9},{9,8},{10,11... | collective-permute-start | bytes 6291464 | tf_op jit(solution)/shard_map/ppermute | solution.py:22
  158.0 9.2 %collective-permute-start.7 = (f32[1024,512]{1,0:T(8,128)}, f32[1024,512]{1,0:T(8,128)}, u32[]{:S(2)}, u32[]{:S(2)}) collective-permute-start(f32[1024,512]{1,0:T(8,128)} %gather_fusion.3), channel_id=1, source_target_pairs={{0,1},{1,0},{2,3},{3,2},{4,5},{5,4},{6,7},{7,6},{8,9},{9,8},{10,11... | collective-permute-start | bytes 6291464 | tf_op jit(solution)/shard_map/ppermute | solution.py:102
  177.5 24.3 %collective-permute-start.8 = (f32[1024,512]{1,0:T(8,128)}, f32[1024,512]{1,0:T(8,128)}, u32[]{:S(2)}, u32[]{:S(2)}) collective-permute-start(f32[1024,512]{1,0:T(8,128)} %gather_fusion.5), channel_id=1, source_target_pairs={{0,1},{1,0},{2,3},{3,2},{4,5},{5,4},{6,7},{7,6},{8,9},{9,8},{10,11... | collective-permute-start | bytes 6291464 | tf_op jit(solution)/shard_map/ppermute | solution.py:106
  177.5 24.3 %collective-permute-start.9 = (bf16[1024,512]{1,0:T(8,128)(2,1)S(1)}, bf16[1024,512]{1,0:T(8,128)(2,1)}, u32[]{:S(2)}, u32[]{:S(2)}) collective-permute-start(bf16[1024,512]{1,0:T(8,128)(2,1)S(1)} %add_convert_fusion), channel_id=1, source_target_pairs={{0,2},{1,3},{2,0},{3,1},{4,6},{5,7},{6,4},{7,5},{8,10},{9,11},{10,... | collective-permute-start | bytes 3145736 | tf_op jit(solution)/shard_map/ppermute | solution.py:105
Sparse Core Ops, SparseCore 0:
  12.9 127.4 all-gather.1

commit v11 on v9

--- a/solution.py
+++ b/solution.py
@@ -74,7 +74,7 @@
     c_of = pos[None, :] - jnp.sum(jnp.where(done, counts[:, None, :], 0), axis=2)
     sender = jnp.arange(learners, dtype=jnp.int32)[:, None]
     slot_of = (m_of * SLOTS + sender * capacity + c_of).reshape(-1)
-    hidden_live = hidden_all[slot_of]
+    hidden_live = hidden_all.at[slot_of].get(mode="promise_in_bounds")
     everything, hidden_live = lax.optimization_barrier((everything, hidden_live))
 
     partial_live = lax.dot_general(
@@ -91,7 +91,8 @@
     rows_per = hidden.shape[0]
 
     def partial_block(partial, b):
-        return partial[lax.dynamic_slice_in_dim(source, b * rows_per, rows_per)]
+        rows = lax.dynamic_slice_in_dim(source, b * rows_per, rows_per)
+        return partial.at[rows].get(mode="promise_in_bounds")
 
     pairs_core = [(i, i ^ 1) for i in range(n_mp)]
     from_core = lax.ppermute(partial_block(partial_live, me ^ 3), "mp", pairs_core)

time: 209 us -> 209 us (level)
  no operation moved by 1% of the time
where the time goes in v11:
time: 209 us; the launch traced here: 208 us
  waiting for transfers between devices  83 us (40%)
  local copies, waits for them, and re-layouts  50.8 us (24%)
  matrix products  22.6 us (11%)
  other arithmetic  20.3 us (10%)
  starting transfers between devices  17.5 us (8%)
  between operations  14.2 us (7%)
    all_gather x1, waiting for transfers between devices, body(): gathered = lax.all_gather(sent, 'dp', axis=0, tiled=True)  54.4 us
    gather x4, local copies, waits for them, and re-layouts, partial_block(): return partial.at[rows].get(mode='promise_in_bounds')  31.2 us
    ppermute x1, waiting for transfers between devices, mp_gather(): lax.ppermute(hidden, 'mp', [(i, (i + half) % n_mp) for i in range(n_mp)])  17.2 us
    ppermute x5, starting transfers between devices, dp_gather_small(): theirs = lax.ppermute(held, 'dp', [(i, i ^ step) for i in range(n)])  11.8 us
    gather x1, local copies, waits for them, and re-layouts, body(): hidden_live = hidden_all.at[slot_of].get(mode='promise_in_bounds')  11.1 us
    dot_general x1, matrix products, body(): lax.dot_general(hidden_live, everything, (((0,), (0,)), ((), ())), prefer...  10.4 us
    dot_general x1, matrix products, body(): lax.dot_general(everything, down_weight, (((1,), (1,)), ((), ())), prefer...  9.8 us
    ppermute x1, waiting for transfers between devices, body(): from_chip = lax.ppermute(to_chip, 'mp', [(i, i ^ 2) for i in range(n_mp)])  5.99 us
  transfers between devices with their start and end apart: 11, of which 7 were waited for; matrix products, arithmetic and copies ran while one was open for 26% of the time, Pallas kernels for 0%

profile of v11, /device:TPU:1, one launch (start us, length us, event | category | flops | bytes accessed | tf_op | source)
XLA Modules:
  0.0 208.4 jit_solution(468735442637707036)
XLA Ops:
  7.2 0.0 copy-start
  7.2 0.0 all-gather.2.cloned.1.call-start
  7.2 0.8 slice_bitcast_fusion
  8.0 0.7 convert_multiply_fusion.4
  8.7 0.7 copy.16
  9.4 0.1 reduce-window.8
  9.5 0.1 reduce
  9.6 0.7 convert_reduce_fusion.1
  10.4 0.0 copy-start.3
  10.4 2.4 %convolution_convert_fusion = bf16[80,2048]{1,0:T(8,128)(2,1)} fusion(bf16[144,2048]{1,0:T(8,128)(2,1)} %param.7, f32[144]{0:T(256)S(1)} %convert_multiply_fusion.4, s32[128]{0:T(128)S(1)} %slice_bitcast_fusion, s32[80]{0:T(128)S(1)} %subtract_add_fusion.1), kind=kOutput, calls=%fused_computation.12 | convolution fusion | flops 51223808 | bytes 918912 | tf_op jit(solution)/shard_map/dot_general | solution.py:58
  12.8 0.0 all-gather.2.cloned.1.call-update
  12.8 2.2 %fusion = bf16[1024,512]{1,0:T(8,128)(2,1)S(1)} fusion(bf16[1024,512]{1,0:T(8,128)(2,1)} %param.12, bf16[1024,512]{1,0:T(8,128)(2,1)} %param.11), kind=kLoop, calls=%fused_computation.13 | loop fusion | flops 4194304 | bytes 3145728 | tf_op jit(solution)/shard_map/convert_element_type | solution.py:63
  15.0 2.5 %collective-permute-start = (bf16[1024,512]{1,0:T(8,128)(2,1)S(1)}, bf16[1024,512]{1,0:T(8,128)(2,1)}, u32[]{:S(2)}, u32[]{:S(2)}) collective-permute-start(bf16[1024,512]{1,0:T(8,128)(2,1)S(1)} %fusion), channel_id=1, source_target_pairs={{0,2},{1,3},{2,0},{3,1},{4,6},{5,7},{6,4},{7,5},{8,10},{9,11},{10,... | collective-permute-start | bytes 3145736 | tf_op jit(solution)/shard_map/ppermute | solution.py:20
  17.5 0.0 copy-done.3
  17.5 1.3 collective-permute-start.2
  18.8 1.5 collective-permute-done.2
  20.3 3.0 %collective-permute-start.3 = (s32[2,32]{1,0:T(2,128)S(1)}, s32[2,32]{1,0:T(2,128)S(1)}, u32[]{:S(2)}, u32[]{:S(2)}) collective-permute-start(s32[2,32]{1,0:T(2,128)S(1)} %add_select_fusion.5), channel_id=1, source_target_pairs={{0,8},{4,12},{8,0},{12,4},{16,24},{20,28},{24,16},{28,20},{32,40},... | collective-permute-start | bytes 776 | tf_op jit(solution)/shard_map/ppermute | solution.py:35
  23.3 1.0 collective-permute-done.3
  24.4 1.3 collective-permute-start.4
  25.6 17.2 %collective-permute-done = bf16[1024,512]{1,0:T(8,128)(2,1)} collective-permute-done((bf16[1024,512]{1,0:T(8,128)(2,1)S(1)}, bf16[1024,512]{1,0:T(8,128)(2,1)}, u32[]{:S(2)}, u32[]{:S(2)}) %collective-permute-start) | collective-permute-done | bytes 1048608 | tf_op jit(solution)/shard_map/ppermute | solution.py:20
  42.8 2.7 %pad_maximum_fusion.1 = bf16[2,1024,512]{2,1,0:T(8,128)(2,1)} fusion(bf16[1,1024,512]{2,1,0:T(8,128)(2,1)} %bitcast.4, bf16[1,1024,512]{2,1,0:T(8,128)(2,1)S(1)} %bitcast.17), kind=kLoop, calls=%fused_computation.21 | loop fusion | flops 1048576 | bytes 4194304 | tf_op jit(solution)/shard_map/stack | solution.py:21
  45.5 1.3 collective-permute-start.1
  46.8 0.0 collective-permute-done.4
  46.8 2.8 %collective-permute-start.5 = (s32[8,32]{1,0:T(8,128)S(1)}, s32[8,32]{1,0:T(8,128)S(1)}, u32[]{:S(2)}, u32[]{:S(2)}) collective-permute-start(s32[8,32]{1,0:T(8,128)S(1)} %add_select_fusion.3), channel_id=1, source_target_pairs={{0,32},{4,36},{8,40},{12,44},{16,48},{20,52},{24,56},{28,60},{32,0... | collective-permute-start | bytes 3080 | tf_op jit(solution)/shard_map/ppermute | solution.py:35
  49.6 1.2 collective-permute-done.5
  50.9 3.4 %collective-permute-start.6 = (s32[16,32]{1,0:T(8,128)S(1)}, s32[16,32]{1,0:T(8,128)S(1)}, u32[]{:S(2)}, u32[]{:S(2)}) collective-permute-start(s32[16,32]{1,0:T(8,128)S(1)} %add_select_fusion.2), channel_id=1, source_target_pairs={{0,64},{4,68},{8,72},{12,76},{16,80},{20,84},{24,88},{28,92},{32,9... | collective-permute-start | bytes 6152 | tf_op jit(solution)/shard_map/ppermute | solution.py:35
  54.3 1.7 collective-permute-done.6
  56.0 0.2 reduce_window_sum.18
  56.2 0.1 add_bitcast_fusion
  56.3 0.1 copy.18
  56.4 0.1 copy.17
  56.4 0.4 convert_reduce_fusion
  56.8 0.1 subtract_add_fusion
  56.9 0.1 add.147
  57.0 0.2 iota_compare_fusion
  57.2 0.3 lt.69
  57.5 0.0 copy-start.2
  57.5 1.0 iota_add_fusion
  58.5 1.3 add.156
  59.9 0.0 collective-permute-done.1
  60.0 3.6 %pad_maximum_fusion = bf16[4,1024,512]{2,1,0:T(8,128)(2,1)} fusion(bf16[2,1024,512]{2,1,0:T(8,128)(2,1)} %collective-permute-done.1, bf16[1,1024,512]{2,1,0:T(8,128)(2,1)} %bitcast.4, bf16[1,1024,512]{2,1,0:T(8,128)(2,1)S(1)} %bitcast.18), kind=kLoop, calls=%fused_computation.6 | loop fusion | flops 4194304 | bytes 8388608 | tf_op jit(solution)/shard_map/concatenate | solution.py:23
  63.5 5.1 %gather_fusion = bf16[4,1024,512]{2,1,0:T(8,128)(2,1)} fusion(bf16[4,1024,512]{2,1,0:T(8,128)(2,1)} %pad_maximum_fusion, s32[1024]{0:T(1024)S(1)} %pad_clamp_fusion.1), kind=kCustom, calls=%fused_computation | custom fusion | bytes 8388624 | tf_op jit(solution)/shard_map/jit(_take)/gather | solution.py:26
  68.7 11.1 %gather_fusion.1 = bf16[2560,512]{1,0:T(8,128)(2,1)} fusion(bf16[4096,512]{1,0:T(8,128)(2,1)} %bitcast.16, s32[3072]{0:T(1024)S(1)} %pad_clamp_fusion), kind=kCustom, calls=%fused_computation.1 | custom fusion | bytes 5253120 | tf_op jit(solution)/shard_map/gather | solution.py:77
  79.7 54.4 %all-gather.2.cloned.1.call-done = bf16[2560,2048]{1,0:T(8,128)(2,1)} async-done(((bf16[80,2048]{1,0:T(8,128)(2,1)}), bf16[2560,2048]{1,0:T(8,128)(2,1)}) %all-gather.2.cloned.1.call-update) | async-done | bytes 10485776 | tf_op jit(solution)/shard_map/all_gather | solution.py:64
  134.1 0.0 copy-done
  134.1 9.8 %fusion.23 = f32[2560,512]{1,0:T(8,128)} fusion(bf16[2560,2048]{1,0:T(8,128)(2,1)} %all-gather.2.cloned.1.call-done, bf16[512,2048]{1,0:T(8,128)(2,1)S(1)} %copy-done), kind=kOutput, calls=%fused_computation.75 | convolution fusion | flops 5368709120 | bytes 17825792 | tf_op jit(solution)/shard_map/dot_general | solution.py:80
  143.9 7.8 %gather_fusion.3 = f32[1024,512]{1,0:T(8,128)} fusion(f32[2560,512]{1,0:T(8,128)} %fusion.23, s32[1024]{0:T(1024)S(1)} %get-tuple-element.27), kind=kCustom, calls=%fused_computation.3 | custom fusion | bytes 4198400 | tf_op jit(solution)/shard_map/gather | solution.py:95
  151.7 1.4 collective-permute-start.7
  153.1 7.8 %gather_fusion.2 = f32[1024,512]{1,0:T(8,128)} fusion(f32[2560,512]{1,0:T(8,128)} %fusion.23, s32[1024]{0:T(1024)S(1)} %get-tuple-element.28), kind=kCustom, calls=%fused_computation.2 | custom fusion | bytes 4198400 | tf_op jit(solution)/shard_map/gather | solution.py:95
  160.9 0.0 collective-permute-done.7
  160.9 3.5 %add_convert_fusion = bf16[1024,512]{1,0:T(8,128)(2,1)} fusion(f32[1024,512]{1,0:T(8,128)} %gather_fusion.2, f32[1024,512]{1,0:T(8,128)} %collective-permute-done.7), kind=kLoop, calls=%fused_computation.24 | loop fusion | flops 1048576 | bytes 5242880 | tf_op jit(solution)/shard_map/convert_element_type | solution.py:99
  164.4 7.8 %gather_fusion.5 = f32[1024,512]{1,0:T(8,128)} fusion(f32[2560,512]{1,0:T(8,128)} %fusion.23, s32[1024]{0:T(1024)S(1)} %get-tuple-element.25), kind=kCustom, calls=%fused_computation.5 | custom fusion | bytes 4198400 | tf_op jit(solution)/shard_map/gather | solution.py:95
  172.2 0.0 collective-permute-start.8
  172.2 0.0 copy-done.2
  172.2 0.5 collective-permute-start.9
  172.7 10.4 %fusion.22 = f32[512,2048]{1,0:T(8,128)} fusion(bf16[2560,512]{1,0:T(8,128)(2,1)} %gather_fusion.1, bf16[2560,2048]{1,0:T(8,128)(2,1)} %all-gather.2.cloned.1.call-done), kind=kOutput, calls=%fused_computation.74 | convolution fusion | flops 5368709120 | bytes 17301504 | tf_op jit(solution)/shard_map/dot_general | solution.py:104
  183.1 0.0 copy-start.1
  183.1 0.0 dynamic-slice-start
  183.1 7.9 %gather_fusion.4 = f32[1024,512]{1,0:T(8,128)} fusion(f32[2560,512]{1,0:T(8,128)} %fusion.23, s32[1024]{0:T(1024)S(1)} %get-tuple-element.26), kind=kCustom, calls=%fused_computation.4 | custom fusion | bytes 4198400 | tf_op jit(solution)/shard_map/gather | solution.py:95
  191.0 6.0 %collective-permute-done.9 = bf16[1024,512]{1,0:T(8,128)(2,1)} collective-permute-done((bf16[1024,512]{1,0:T(8,128)(2,1)}, bf16[1024,512]{1,0:T(8,128)(2,1)}, u32[]{:S(2)}, u32[]{:S(2)}) %collective-permute-start.9) | collective-permute-done | bytes 1048608 | tf_op jit(solution)/shard_map/ppermute | solution.py:101
  196.9 0.0 collective-permute-done.8
  196.9 0.0 copy-done.1
  196.9 0.0 dynamic-slice-done
  196.9 4.6 %multiply_convert_fusion = (bf16[1024,512]{1,0:T(8,128)(2,1)}, bf16[1024,512]{1,0:T(8,128)(2,1)}) fusion(bf16[1024,512]{1,0:T(8,128)(2,1)} %param.11, bf16[1024,512]{1,0:T(8,128)(2,1)} %collective-permute-done.9, f32[1024,512]{1,0:T(8,128)} %gather_fusion.4, f32[1024,512]{1,0:T(8,128)} %collective-permute-done.8, pred[1024]{0:T(1024)(128)(4,1)S(1)} %dynamic-slice-done, ...), kind=kLoop, calls=%fused_computation.22 | loop fusion | flops 9961472 | bytes 9438208 | tf_op jit(solution)/shard_map/convert_element_type | solution.py:110
  (14 shorter events, 0.1 us)
Async XLA Ops:
  7.2 127.0 %copy-start = (bf16[512,2048]{1,0:T(8,128)(2,1)S(1)}, bf16[512,2048]{1,0:T(8,128)(2,1)}, u32[]{:S(2)}) copy-start(bf16[512,2048]{1,0:T(8,128)(2,1)} %param.13) | copy-start | bytes 6291460
  7.2 126.9 %all-gather.2.cloned.1.call-start = ((), (), s32[]{:S(2)}) async-start(), calls=%async_computation | async-start | bytes 10813440 | tf_op jit(solution)/shard_map/all_gather | solution.py:64
  10.4 7.1 %copy-start.3 = (s32[1,32]{1,0:T(1,128)S(1)}, s32[1,32]{1,0:T(1,128)}, u32[]{:S(2)}) copy-start(s32[1,32]{1,0:T(1,128)} %param.10) | copy-start | bytes 388
  15.0 27.8 %collective-permute-start = (bf16[1024,512]{1,0:T(8,128)(2,1)S(1)}, bf16[1024,512]{1,0:T(8,128)(2,1)}, u32[]{:S(2)}, u32[]{:S(2)}) collective-permute-start(bf16[1024,512]{1,0:T(8,128)(2,1)S(1)} %fusion), channel_id=1, source_target_pairs={{0,2},{1,3},{2,0},{3,1},{4,6},{5,7},{6,4},{7,5},{8,10},{9,11},{10,... | collective-permute-start | bytes 3145736 | tf_op jit(solution)/shard_map/ppermute | solution.py:20
  17.5 2.8 %collective-permute-start.2 = (s32[1,32]{1,0:T(1,128)S(1)}, s32[1,32]{1,0:T(1,128)S(1)}, u32[]{:S(2)}, u32[]{:S(2)}) collective-permute-start(s32[1,32]{1,0:T(1,128)S(1)} %copy-done.3), channel_id=1, source_target_pairs={{0,4},{4,0},{8,12},{12,8},{16,20},{20,16},{24,28},{28,24},{32,36},... | collective-permute-start | bytes 392 | tf_op jit(solution)/shard_map/ppermute | solution.py:35
  20.3 4.0 %collective-permute-start.3 = (s32[2,32]{1,0:T(2,128)S(1)}, s32[2,32]{1,0:T(2,128)S(1)}, u32[]{:S(2)}, u32[]{:S(2)}) collective-permute-start(s32[2,32]{1,0:T(2,128)S(1)} %add_select_fusion.5), channel_id=1, source_target_pairs={{0,8},{4,12},{8,0},{12,4},{16,24},{20,28},{24,16},{28,20},{32,40},... | collective-permute-start | bytes 776 | tf_op jit(solution)/shard_map/ppermute | solution.py:35
  24.4 22.4 %collective-permute-start.4 = (s32[4,32]{1,0:T(4,128)S(1)}, s32[4,32]{1,0:T(4,128)S(1)}, u32[]{:S(2)}, u32[]{:S(2)}) collective-permute-start(s32[4,32]{1,0:T(4,128)S(1)} %add_select_fusion.4), channel_id=1, source_target_pairs={{0,16},{4,20},{8,24},{12,28},{16,0},{20,4},{24,8},{28,12},{32,48},... | collective-permute-start | bytes 1544 | tf_op jit(solution)/shard_map/ppermute | solution.py:35
  45.5 14.4 %collective-permute-start.1 = (bf16[2,1024,512]{2,1,0:T(8,128)(2,1)}, bf16[2,1024,512]{2,1,0:T(8,128)(2,1)}, u32[]{:S(2)}, u32[]{:S(2)}) collective-permute-start(bf16[2,1024,512]{2,1,0:T(8,128)(2,1)} %pad_maximum_fusion.1), channel_id=1, source_target_pairs={{0,1},{1,0},{2,3},{3,2},{4,5},{5,4},{6,7},{7,6},{8,9},{9,8},{10,11... | collective-permute-start | bytes 6291464 | tf_op jit(solution)/shard_map/ppermute | solution.py:22
  46.8 4.0 %collective-permute-start.5 = (s32[8,32]{1,0:T(8,128)S(1)}, s32[8,32]{1,0:T(8,128)S(1)}, u32[]{:S(2)}, u32[]{:S(2)}) collective-permute-start(s32[8,32]{1,0:T(8,128)S(1)} %add_select_fusion.3), channel_id=1, source_target_pairs={{0,32},{4,36},{8,40},{12,44},{16,48},{20,52},{24,56},{28,60},{32,0... | collective-permute-start | bytes 3080 | tf_op jit(solution)/shard_map/ppermute | solution.py:35
  50.9 5.2 %collective-permute-start.6 = (s32[16,32]{1,0:T(8,128)S(1)}, s32[16,32]{1,0:T(8,128)S(1)}, u32[]{:S(2)}, u32[]{:S(2)}) collective-permute-start(s32[16,32]{1,0:T(8,128)S(1)} %add_select_fusion.2), channel_id=1, source_target_pairs={{0,64},{4,68},{8,72},{12,76},{16,80},{20,84},{24,88},{28,92},{32,9... | collective-permute-start | bytes 6152 | tf_op jit(solution)/shard_map/ppermute | solution.py:35
  57.5 114.7 %copy-start.2 = (pred[4096]{0:T(1024)(128)(4,1)}, pred[4096]{0:T(1024)(128)(4,1)S(1)}, u32[]{:S(2)}) copy-start(pred[4096]{0:T(1024)(128)(4,1)S(1)} %lt.69) | copy-start | bytes 12292
  151.7 9.2 %collective-permute-start.7 = (f32[1024,512]{1,0:T(8,128)}, f32[1024,512]{1,0:T(8,128)}, u32[]{:S(2)}, u32[]{:S(2)}) collective-permute-start(f32[1024,512]{1,0:T(8,128)} %gather_fusion.3), channel_id=1, source_target_pairs={{0,1},{1,0},{2,3},{3,2},{4,5},{5,4},{6,7},{7,6},{8,9},{9,8},{10,11... | collective-permute-start | bytes 6291464 | tf_op jit(solution)/shard_map/ppermute | solution.py:98
  172.2 24.8 %collective-permute-start.8 = (f32[1024,512]{1,0:T(8,128)}, f32[1024,512]{1,0:T(8,128)}, u32[]{:S(2)}, u32[]{:S(2)}) collective-permute-start(f32[1024,512]{1,0:T(8,128)} %gather_fusion.5), channel_id=1, source_target_pairs={{0,1},{1,0},{2,3},{3,2},{4,5},{5,4},{6,7},{7,6},{8,9},{9,8},{10,11... | collective-permute-start | bytes 6291464 | tf_op jit(solution)/shard_map/ppermute | solution.py:102
  172.2 24.7 %collective-permute-start.9 = (bf16[1024,512]{1,0:T(8,128)(2,1)}, bf16[1024,512]{1,0:T(8,128)(2,1)}, u32[]{:S(2)}, u32[]{:S(2)}) collective-permute-start(bf16[1024,512]{1,0:T(8,128)(2,1)} %add_convert_fusion), channel_id=1, source_target_pairs={{0,2},{1,3},{2,0},{3,1},{4,6},{5,7},{6,4},{7,5},{8,10},{9,11},{10,... | collective-permute-start | bytes 3145736 | tf_op jit(solution)/shard_map/ppermute | solution.py:101
  183.1 13.9 %copy-start.1 = (bf16[1024,512]{1,0:T(8,128)(2,1)S(1)}, bf16[1024,512]{1,0:T(8,128)(2,1)}, u32[]{:S(2)}) copy-start(bf16[1024,512]{1,0:T(8,128)(2,1)} %param.12) | copy-start | bytes 3145732
  183.1 13.9 %dynamic-slice-start = ((pred[4096]{0:T(1024)(128)(4,1)}, s32[]{:T(128)}), pred[1024]{0:T(1024)(128)(4,1)S(1)}, s32[]{:S(2)}) async-start(pred[4096]{0:T(1024)(128)(4,1)} %copy-done.2, s32[]{:T(128)} %select_n.149), calls=%async_computation.1 | async-start | bytes 2560 | tf_op jit(solution)/shard_map/dynamic_slice | solution.py:108
Sparse Core Ops, SparseCore 0:
  12.9 121.1 all-gather.1

commit v12 on v9

--- a/solution.py
+++ b/solution.py
@@ -98,8 +98,12 @@
     to_chip = (partial_block(partial_live, me ^ 2) + from_core).astype(jnp.bfloat16)
     to_chip, partial_late = lax.optimization_barrier((to_chip, partial_live))
     from_chip = lax.ppermute(to_chip, "mp", [(i, i ^ 2) for i in range(n_mp)])
-    from_core_own = lax.ppermute(partial_block(partial_late, me ^ 1), "mp", pairs_core)
-    own_part = partial_block(partial_late, me)
+    rows = jnp.concatenate(
+        [lax.dynamic_slice_in_dim(source, b * rows_per, rows_per) for b in (me ^ 1, me)]
+    )
+    late_blocks = partial_late[rows]
+    from_core_own = lax.ppermute(late_blocks[:rows_per], "mp", pairs_core)
+    own_part = late_blocks[rows_per:]
     grad_down = lax.dot_general(
         hidden_live, everything, (((0,), (0,)), ((), ())), preferred_element_type=jnp.float32
     )

time: 209 us -> 212 us (1.014)
  waiting for transfers between devices: 83 us -> 90.9 us
  other arithmetic: 20.3 us -> 17.5 us
    gather x4 -> x2, local copies, waits for them, and re-layouts: 31.2 us -> 15.6 us  [partial_block(): return partial[lax.dynamic_slice_in_dim(source, b * rows_per, rows_per)]]
    gather x0 -> x1, local copies, waits for them, and re-layouts: none -> 12 us  [body(): late_blocks = partial_late[rows]]
    ppermute x1, waiting for transfers between devices: 5.99 us -> 13.9 us  [body(): from_chip = lax.ppermute(to_chip, 'mp', [(i, i ^ 2) for i in range(n_mp)])]
  transfers between devices with their start and end apart: 11 -> 11, of which waited for: 7 -> 7; matrix products, arithmetic and copies ran while one was open for 26% -> 22% of each run, Pallas kernels for 0% -> 0%
where the time goes in v12:
time: 212 us
  waiting for transfers between devices  90.9 us (43%)
  local copies, waits for them, and re-layouts  49.2 us (23%)
  matrix products  22.2 us (10%)
  starting transfers between devices  17.8 us (8%)
  other arithmetic  17.5 us (8%)
  between operations  14.2 us (7%)
    all_gather x1, waiting for transfers between devices, body(): gathered = lax.all_gather(sent, 'dp', axis=0, tiled=True)  54.4 us
    ppermute x1, waiting for transfers between devices, mp_gather(): lax.ppermute(hidden, 'mp', [(i, (i + half) % n_mp) for i in range(n_mp)])  17.2 us
    gather x2, local copies, waits for them, and re-layouts, partial_block(): return partial[lax.dynamic_slice_in_dim(source, b * rows_per, rows_per)]  15.6 us
    ppermute x1, waiting for transfers between devices, body(): from_chip = lax.ppermute(to_chip, 'mp', [(i, i ^ 2) for i in range(n_mp)])  13.9 us
    gather x1, local copies, waits for them, and re-layouts, body(): late_blocks = partial_late[rows]  12 us
    ppermute x5, starting transfers between devices, dp_gather_small(): theirs = lax.ppermute(held, 'dp', [(i, i ^ step) for i in range(n)])  11.8 us
    gather x1, local copies, waits for them, and re-layouts, body(): hidden_live = hidden_all[slot_of]  11.1 us
    dot_general x1, matrix products, body(): lax.dot_general(hidden_live, everything, (((0,), (0,)), ((), ())), prefer...  10 us
  transfers between devices with their start and end apart: 11, of which 7 were waited for; matrix products, arithmetic and copies ran while one was open for 22% of the time, Pallas kernels for 0%

profile of v12, /device:TPU:1, one launch (start us, length us, event | category | flops | bytes accessed | tf_op | source)
XLA Modules:
  0.0 211.8 jit_solution(2701573971347124318)
XLA Ops:
  7.2 0.0 copy-start
  7.2 0.0 all-gather.2.cloned.1.call-start
  7.2 0.8 slice_bitcast_fusion
  8.0 0.7 convert_multiply_fusion.4
  8.7 0.7 copy.16
  9.4 0.1 reduce-window.8
  9.5 0.1 reduce
  9.6 0.7 convert_reduce_fusion.1
  10.4 0.0 copy-start.6
  10.4 2.4 %convolution_convert_fusion = bf16[80,2048]{1,0:T(8,128)(2,1)} fusion(bf16[144,2048]{1,0:T(8,128)(2,1)} %param.7, f32[144]{0:T(256)S(1)} %convert_multiply_fusion.4, s32[128]{0:T(128)S(1)} %slice_bitcast_fusion, s32[80]{0:T(128)S(1)} %subtract_add_fusion.1), kind=kOutput, calls=%fused_computation.11 | convolution fusion | flops 51223808 | bytes 918912 | tf_op jit(solution)/shard_map/dot_general | solution.py:58
  12.8 0.0 all-gather.2.cloned.1.call-update
  12.8 2.2 %fusion = bf16[1024,512]{1,0:T(8,128)(2,1)S(1)} fusion(bf16[1024,512]{1,0:T(8,128)(2,1)} %param.12, bf16[1024,512]{1,0:T(8,128)(2,1)} %param.11), kind=kLoop, calls=%fused_computation.12 | loop fusion | flops 4194304 | bytes 3145728 | tf_op jit(solution)/shard_map/convert_element_type | solution.py:63
  15.0 2.5 %collective-permute-start = (bf16[1024,512]{1,0:T(8,128)(2,1)S(1)}, bf16[1024,512]{1,0:T(8,128)(2,1)}, u32[]{:S(2)}, u32[]{:S(2)}) collective-permute-start(bf16[1024,512]{1,0:T(8,128)(2,1)S(1)} %fusion), channel_id=1, source_target_pairs={{0,2},{1,3},{2,0},{3,1},{4,6},{5,7},{6,4},{7,5},{8,10},{9,11},{10,... | collective-permute-start | bytes 3145736 | tf_op jit(solution)/shard_map/ppermute | solution.py:20
  17.5 0.0 copy-done.6
  17.5 1.3 collective-permute-start.2
  18.8 1.5 collective-permute-done.2
  20.3 3.0 %collective-permute-start.3 = (s32[2,32]{1,0:T(2,128)S(1)}, s32[2,32]{1,0:T(2,128)S(1)}, u32[]{:S(2)}, u32[]{:S(2)}) collective-permute-start(s32[2,32]{1,0:T(2,128)S(1)} %add_select_fusion.4), channel_id=1, source_target_pairs={{0,8},{4,12},{8,0},{12,4},{16,24},{20,28},{24,16},{28,20},{32,40},... | collective-permute-start | bytes 776 | tf_op jit(solution)/shard_map/ppermute | solution.py:35
  23.3 1.0 collective-permute-done.3
  24.4 1.3 collective-permute-start.4
  25.6 17.2 %collective-permute-done = bf16[1024,512]{1,0:T(8,128)(2,1)} collective-permute-done((bf16[1024,512]{1,0:T(8,128)(2,1)S(1)}, bf16[1024,512]{1,0:T(8,128)(2,1)}, u32[]{:S(2)}, u32[]{:S(2)}) %collective-permute-start) | collective-permute-done | bytes 1048608 | tf_op jit(solution)/shard_map/ppermute | solution.py:20
  42.8 2.7 %pad_maximum_fusion.1 = bf16[2,1024,512]{2,1,0:T(8,128)(2,1)} fusion(bf16[1,1024,512]{2,1,0:T(8,128)(2,1)} %bitcast.4, bf16[1,1024,512]{2,1,0:T(8,128)(2,1)S(1)} %bitcast.20), kind=kLoop, calls=%fused_computation.23 | loop fusion | flops 1048576 | bytes 4194304 | tf_op jit(solution)/shard_map/stack | solution.py:21
  45.5 1.3 collective-permute-start.1
  46.8 0.0 collective-permute-done.4
  46.8 2.8 %collective-permute-start.5 = (s32[8,32]{1,0:T(8,128)S(1)}, s32[8,32]{1,0:T(8,128)S(1)}, u32[]{:S(2)}, u32[]{:S(2)}) collective-permute-start(s32[8,32]{1,0:T(8,128)S(1)} %add_select_fusion.2), channel_id=1, source_target_pairs={{0,32},{4,36},{8,40},{12,44},{16,48},{20,52},{24,56},{28,60},{32,0... | collective-permute-start | bytes 3080 | tf_op jit(solution)/shard_map/ppermute | solution.py:35
  49.6 1.2 collective-permute-done.5
  50.9 3.4 %collective-permute-start.6 = (s32[16,32]{1,0:T(8,128)S(1)}, s32[16,32]{1,0:T(8,128)S(1)}, u32[]{:S(2)}, u32[]{:S(2)}) collective-permute-start(s32[16,32]{1,0:T(8,128)S(1)} %add_select_fusion.1), channel_id=1, source_target_pairs={{0,64},{4,68},{8,72},{12,76},{16,80},{20,84},{24,88},{28,92},{32,9... | collective-permute-start | bytes 6152 | tf_op jit(solution)/shard_map/ppermute | solution.py:35
  54.3 1.7 collective-permute-done.6
  56.0 0.2 reduce_window_sum.18
  56.2 0.1 add_bitcast_fusion
  56.3 0.1 copy.18
  56.4 0.1 copy.17
  56.4 0.4 convert_reduce_fusion
  56.8 0.1 subtract_add_fusion
  56.9 0.1 add.154
  57.0 0.2 iota_compare_fusion
  57.2 0.3 lt.76
  57.5 1.0 iota_add_fusion
  58.5 1.3 add.163
  59.9 0.0 collective-permute-done.1
  60.0 3.6 %pad_maximum_fusion = bf16[4,1024,512]{2,1,0:T(8,128)(2,1)} fusion(bf16[2,1024,512]{2,1,0:T(8,128)(2,1)} %collective-permute-done.1, bf16[1,1024,512]{2,1,0:T(8,128)(2,1)} %bitcast.4, bf16[1,1024,512]{2,1,0:T(8,128)(2,1)S(1)} %bitcast.21), kind=kLoop, calls=%fused_computation.5 | loop fusion | flops 4194304 | bytes 8388608 | tf_op jit(solution)/shard_map/concatenate | solution.py:23
  63.5 5.1 %gather_fusion = bf16[4,1024,512]{2,1,0:T(8,128)(2,1)} fusion(bf16[4,1024,512]{2,1,0:T(8,128)(2,1)} %pad_maximum_fusion, s32[1024]{0:T(1024)S(1)} %pad_clamp_fusion.1), kind=kCustom, calls=%fused_computation | custom fusion | bytes 8388624 | tf_op jit(solution)/shard_map/jit(_take)/gather | solution.py:26
  68.7 11.1 %gather_fusion.1 = bf16[2560,512]{1,0:T(8,128)(2,1)} fusion(bf16[4096,512]{1,0:T(8,128)(2,1)} %bitcast.19, s32[3072]{0:T(1024)S(1)} %pad_clamp_fusion), kind=kCustom, calls=%fused_computation.1 | custom fusion | bytes 5253120 | tf_op jit(solution)/shard_map/gather | solution.py:77
  79.7 54.4 %all-gather.2.cloned.1.call-done = bf16[2560,2048]{1,0:T(8,128)(2,1)} async-done(((bf16[80,2048]{1,0:T(8,128)(2,1)}), bf16[2560,2048]{1,0:T(8,128)(2,1)}) %all-gather.2.cloned.1.call-update) | async-done | bytes 10485776 | tf_op jit(solution)/shard_map/all_gather | solution.py:64
  134.1 0.0 copy-done
  134.1 9.8 %fusion.24 = f32[2560,512]{1,0:T(8,128)} fusion(bf16[2560,2048]{1,0:T(8,128)(2,1)} %all-gather.2.cloned.1.call-done, bf16[512,2048]{1,0:T(8,128)(2,1)S(1)} %copy-done), kind=kOutput, calls=%fused_computation.75 | convolution fusion | flops 5368709120 | bytes 17825792 | tf_op jit(solution)/shard_map/dot_general | solution.py:80
  143.9 7.8 %gather_fusion.3 = f32[1024,512]{1,0:T(8,128)} fusion(f32[2560,512]{1,0:T(8,128)} %fusion.24, s32[1024]{0:T(1024)S(1)} %get-tuple-element.27), kind=kCustom, calls=%fused_computation.3 | custom fusion | bytes 4198400 | tf_op jit(solution)/shard_map/gather | solution.py:94
  151.7 1.4 collective-permute-start.7
  153.1 7.8 %gather_fusion.2 = f32[1024,512]{1,0:T(8,128)} fusion(f32[2560,512]{1,0:T(8,128)} %fusion.24, s32[1024]{0:T(1024)S(1)} %get-tuple-element.28), kind=kCustom, calls=%fused_computation.2 | custom fusion | bytes 4198400 | tf_op jit(solution)/shard_map/gather | solution.py:94
  160.9 0.0 collective-permute-done.7
  160.9 2.6 %add_convert_fusion = bf16[1024,512]{1,0:T(8,128)(2,1)S(1)} fusion(f32[1024,512]{1,0:T(8,128)} %gather_fusion.2, f32[1024,512]{1,0:T(8,128)} %collective-permute-done.7), kind=kLoop, calls=%fused_computation.25 | loop fusion | flops 1048576 | bytes 5242880 | tf_op jit(solution)/shard_map/convert_element_type | solution.py:98
  163.5 12.0 %gather_fusion.4 = f32[2048,512]{1,0:T(8,128)} fusion(f32[2560,512]{1,0:T(8,128)} %fusion.24, s32[2048]{0:T(1024)S(1)} %broadcast_clamp_fusion), kind=kCustom, calls=%fused_computation.4 | custom fusion | bytes 8396800 | tf_op jit(solution)/shard_map/gather | solution.py:104
  175.5 1.9 slice.24
  177.5 0.3 collective-permute-start.8
  177.7 0.0 copy-done.5
  177.8 0.0 copy-start.2
  177.8 0.0 copy-start.3
  177.8 0.0 dynamic-slice-start
  177.8 0.5 collective-permute-start.9
  178.2 0.0 copy-done.4
  178.2 10.0 %fusion.23 = f32[512,2048]{1,0:T(8,128)} fusion(bf16[2560,512]{1,0:T(8,128)(2,1)S(1)} %copy-done.4, bf16[2560,2048]{1,0:T(8,128)(2,1)} %all-gather.2.cloned.1.call-done), kind=kOutput, calls=%fused_computation.74 | convolution fusion | flops 5368709120 | bytes 17301504 | tf_op jit(solution)/shard_map/dot_general | solution.py:107
  188.3 13.9 %collective-permute-done.9 = bf16[1024,512]{1,0:T(8,128)(2,1)S(1)} collective-permute-done((bf16[1024,512]{1,0:T(8,128)(2,1)S(1)}, bf16[1024,512]{1,0:T(8,128)(2,1)S(1)}, u32[]{:S(2)}, u32[]{:S(2)}) %collective-permute-start.9) | collective-permute-done | bytes 1048608 | tf_op jit(solution)/shard_map/ppermute | solution.py:100
  202.1 0.0 collective-permute-done.8
  202.1 0.0 copy-done.1
  202.2 2.8 %multiply_convert_fusion = (bf16[1024,512]{1,0:T(8,128)(2,1)}, bf16[1024,512]{1,0:T(8,128)(2,1)}) fusion(bf16[1024,512]{1,0:T(8,128)(2,1)S(1)} %copy-done.3, bf16[1024,512]{1,0:T(8,128)(2,1)S(1)} %collective-permute-done.9, f32[1024,512]{1,0:T(8,128)S(1)} %collective-permute-done.8, f32[2048,512]{1,0:T(8,128)S(1)} %copy-done.1, ...), kind=kLoop, calls=%fused_computation.24 | loop fusion | flops 9961472 | bytes 9438208 | tf_op jit(solution)/shard_map/convert_element_type | solution.py:113
  (22 shorter events, 0.2 us)
Async XLA Ops:
  7.2 127.0 %copy-start = (bf16[512,2048]{1,0:T(8,128)(2,1)S(1)}, bf16[512,2048]{1,0:T(8,128)(2,1)}, u32[]{:S(2)}) copy-start(bf16[512,2048]{1,0:T(8,128)(2,1)} %param.13) | copy-start | bytes 6291460
  7.2 126.9 %all-gather.2.cloned.1.call-start = ((), (), s32[]{:S(2)}) async-start(), calls=%async_computation | async-start | bytes 10813440 | tf_op jit(solution)/shard_map/all_gather | solution.py:64
  10.4 7.1 %copy-start.6 = (s32[1,32]{1,0:T(1,128)S(1)}, s32[1,32]{1,0:T(1,128)}, u32[]{:S(2)}) copy-start(s32[1,32]{1,0:T(1,128)} %param.10) | copy-start | bytes 388
  15.0 27.8 %collective-permute-start = (bf16[1024,512]{1,0:T(8,128)(2,1)S(1)}, bf16[1024,512]{1,0:T(8,128)(2,1)}, u32[]{:S(2)}, u32[]{:S(2)}) collective-permute-start(bf16[1024,512]{1,0:T(8,128)(2,1)S(1)} %fusion), channel_id=1, source_target_pairs={{0,2},{1,3},{2,0},{3,1},{4,6},{5,7},{6,4},{7,5},{8,10},{9,11},{10,... | collective-permute-start | bytes 3145736 | tf_op jit(solution)/shard_map/ppermute | solution.py:20
  17.5 2.8 %collective-permute-start.2 = (s32[1,32]{1,0:T(1,128)S(1)}, s32[1,32]{1,0:T(1,128)S(1)}, u32[]{:S(2)}, u32[]{:S(2)}) collective-permute-start(s32[1,32]{1,0:T(1,128)S(1)} %copy-done.6), channel_id=1, source_target_pairs={{0,4},{4,0},{8,12},{12,8},{16,20},{20,16},{24,28},{28,24},{32,36},... | collective-permute-start | bytes 392 | tf_op jit(solution)/shard_map/ppermute | solution.py:35
  20.3 4.0 %collective-permute-start.3 = (s32[2,32]{1,0:T(2,128)S(1)}, s32[2,32]{1,0:T(2,128)S(1)}, u32[]{:S(2)}, u32[]{:S(2)}) collective-permute-start(s32[2,32]{1,0:T(2,128)S(1)} %add_select_fusion.4), channel_id=1, source_target_pairs={{0,8},{4,12},{8,0},{12,4},{16,24},{20,28},{24,16},{28,20},{32,40},... | collective-permute-start | bytes 776 | tf_op jit(solution)/shard_map/ppermute | solution.py:35
  24.4 22.4 %collective-permute-start.4 = (s32[4,32]{1,0:T(4,128)S(1)}, s32[4,32]{1,0:T(4,128)S(1)}, u32[]{:S(2)}, u32[]{:S(2)}) collective-permute-start(s32[4,32]{1,0:T(4,128)S(1)} %add_select_fusion.3), channel_id=1, source_target_pairs={{0,16},{4,20},{8,24},{12,28},{16,0},{20,4},{24,8},{28,12},{32,48},... | collective-permute-start | bytes 1544 | tf_op jit(solution)/shard_map/ppermute | solution.py:35
  45.5 14.4 %collective-permute-start.1 = (bf16[2,1024,512]{2,1,0:T(8,128)(2,1)}, bf16[2,1024,512]{2,1,0:T(8,128)(2,1)}, u32[]{:S(2)}, u32[]{:S(2)}) collective-permute-start(bf16[2,1024,512]{2,1,0:T(8,128)(2,1)} %pad_maximum_fusion.1), channel_id=1, source_target_pairs={{0,1},{1,0},{2,3},{3,2},{4,5},{5,4},{6,7},{7,6},{8,9},{9,8},{10,11... | collective-permute-start | bytes 6291464 | tf_op jit(solution)/shard_map/ppermute | solution.py:22
  46.8 4.0 %collective-permute-start.5 = (s32[8,32]{1,0:T(8,128)S(1)}, s32[8,32]{1,0:T(8,128)S(1)}, u32[]{:S(2)}, u32[]{:S(2)}) collective-permute-start(s32[8,32]{1,0:T(8,128)S(1)} %add_select_fusion.2), channel_id=1, source_target_pairs={{0,32},{4,36},{8,40},{12,44},{16,48},{20,52},{24,56},{28,60},{32,0... | collective-permute-start | bytes 3080 | tf_op jit(solution)/shard_map/ppermute | solution.py:35
  50.9 5.2 %collective-permute-start.6 = (s32[16,32]{1,0:T(8,128)S(1)}, s32[16,32]{1,0:T(8,128)S(1)}, u32[]{:S(2)}, u32[]{:S(2)}) collective-permute-start(s32[16,32]{1,0:T(8,128)S(1)} %add_select_fusion.1), channel_id=1, source_target_pairs={{0,64},{4,68},{8,72},{12,76},{16,80},{20,84},{24,88},{28,92},{32,9... | collective-permute-start | bytes 6152 | tf_op jit(solution)/shard_map/ppermute | solution.py:35
  57.5 120.2 %copy-start.5 = (pred[4096]{0:T(1024)(128)(4,1)}, pred[4096]{0:T(1024)(128)(4,1)S(1)}, u32[]{:S(2)}) copy-start(pred[4096]{0:T(1024)(128)(4,1)S(1)} %lt.76) | copy-start | bytes 12292
  151.7 9.2 %collective-permute-start.7 = (f32[1024,512]{1,0:T(8,128)}, f32[1024,512]{1,0:T(8,128)}, u32[]{:S(2)}, u32[]{:S(2)}) collective-permute-start(f32[1024,512]{1,0:T(8,128)} %gather_fusion.3), channel_id=1, source_target_pairs={{0,1},{1,0},{2,3},{3,2},{4,5},{5,4},{6,7},{7,6},{8,9},{9,8},{10,11... | collective-permute-start | bytes 6291464 | tf_op jit(solution)/shard_map/ppermute | solution.py:97
  175.5 2.7 %copy-start.4 = (bf16[2560,512]{1,0:T(8,128)(2,1)S(1)}, bf16[2560,512]{1,0:T(8,128)(2,1)}, u32[]{:S(2)}) copy-start(bf16[2560,512]{1,0:T(8,128)(2,1)} %gather_fusion.1) | copy-start | bytes 7864324
  177.5 24.7 %collective-permute-start.8 = (f32[1024,512]{1,0:T(8,128)S(1)}, f32[1024,512]{1,0:T(8,128)S(1)}, u32[]{:S(2)}, u32[]{:S(2)}) collective-permute-start(f32[1024,512]{1,0:T(8,128)S(1)} %slice.24), channel_id=1, source_target_pairs={{0,1},{1,0},{2,3},{3,2},{4,5},{5,4},{6,7},{7,6},{8,9},{9,8},{10,11... | collective-permute-start | bytes 6291464 | tf_op jit(solution)/shard_map/ppermute | solution.py:105
  177.7 24.4 %copy-start.1 = (f32[2048,512]{1,0:T(8,128)S(1)}, f32[2048,512]{1,0:T(8,128)}, u32[]{:S(2)}) copy-start(f32[2048,512]{1,0:T(8,128)} %gather_fusion.4) | copy-start | bytes 12582916
  177.8 24.4 %copy-start.2 = (bf16[1024,512]{1,0:T(8,128)(2,1)S(1)}, bf16[1024,512]{1,0:T(8,128)(2,1)}, u32[]{:S(2)}) copy-start(bf16[1024,512]{1,0:T(8,128)(2,1)} %param.12) | copy-start | bytes 3145732
  177.8 24.4 %copy-start.3 = (bf16[1024,512]{1,0:T(8,128)(2,1)S(1)}, bf16[1024,512]{1,0:T(8,128)(2,1)}, u32[]{:S(2)}) copy-start(bf16[1024,512]{1,0:T(8,128)(2,1)} %param.11) | copy-start | bytes 3145732
  177.8 24.4 %dynamic-slice-start = ((pred[4096]{0:T(1024)(128)(4,1)}, s32[]{:T(128)}), pred[1024]{0:T(1024)(128)(4,1)S(1)}, s32[]{:S(2)}) async-start(pred[4096]{0:T(1024)(128)(4,1)} %copy-done.5, s32[]{:T(128)} %select_n.153), calls=%async_computation.1 | async-start | bytes 2560 | tf_op jit(solution)/shard_map/dynamic_slice | solution.py:111
  177.8 24.3 %collective-permute-start.9 = (bf16[1024,512]{1,0:T(8,128)(2,1)S(1)}, bf16[1024,512]{1,0:T(8,128)(2,1)S(1)}, u32[]{:S(2)}, u32[]{:S(2)}) collective-permute-start(bf16[1024,512]{1,0:T(8,128)(2,1)S(1)} %add_convert_fusion), channel_id=1, source_target_pairs={{0,2},{1,3},{2,0},{3,1},{4,6},{5,7},{6,4},{7,5},{8,10},{9,11},{10,... | collective-permute-start | bytes 3145736 | tf_op jit(solution)/shard_map/ppermute | solution.py:100
Sparse Core Ops, SparseCore 0:
  12.9 121.1 all-gather.1

commit v13 on v12

--- a/solution.py
+++ b/solution.py
@@ -98,12 +98,12 @@
     to_chip = (partial_block(partial_live, me ^ 2) + from_core).astype(jnp.bfloat16)
     to_chip, partial_late = lax.optimization_barrier((to_chip, partial_live))
     from_chip = lax.ppermute(to_chip, "mp", [(i, i ^ 2) for i in range(n_mp)])
-    rows = jnp.concatenate(
+    rows = jnp.stack(
         [lax.dynamic_slice_in_dim(source, b * rows_per, rows_per) for b in (me ^ 1, me)]
     )
     late_blocks = partial_late[rows]
-    from_core_own = lax.ppermute(late_blocks[:rows_per], "mp", pairs_core)
-    own_part = late_blocks[rows_per:]
+    from_core_own = lax.ppermute(late_blocks[0], "mp", pairs_core)
+    own_part = late_blocks[1]
     grad_down = lax.dot_general(
         hidden_live, everything, (((0,), (0,)), ((), ())), preferred_element_type=jnp.float32
     )

time: 212 us -> 212 us (level)
  no operation moved by 1% of the time
where the time goes in v13:
time: 212 us
  waiting for transfers between devices  90.9 us (43%)
  local copies, waits for them, and re-layouts  49.2 us (23%)
  matrix products  22.2 us (10%)
  starting transfers between devices  17.8 us (8%)
  other arithmetic  17.5 us (8%)
  between operations  14.2 us (7%)
    all_gather x1, waiting for transfers between devices, body(): gathered = lax.all_gather(sent, 'dp', axis=0, tiled=True)  54.4 us
    ppermute x1, waiting for transfers between devices, mp_gather(): lax.ppermute(hidden, 'mp', [(i, (i + half) % n_mp) for i in range(n_mp)])  17.2 us
    gather x2, local copies, waits for them, and re-layouts, partial_block(): return partial[lax.dynamic_slice_in_dim(source, b * rows_per, rows_per)]  15.6 us
    ppermute x1, waiting for transfers between devices, body(): from_chip = lax.ppermute(to_chip, 'mp', [(i, i ^ 2) for i in range(n_mp)])  13.9 us
    gather x1, local copies, waits for them, and re-layouts, body(): late_blocks = partial_late[rows]  12 us
    ppermute x5, starting transfers between devices, dp_gather_small(): theirs = lax.ppermute(held, 'dp', [(i, i ^ step) for i in range(n)])  11.8 us
    gather x1, local copies, waits for them, and re-layouts, body(): hidden_live = hidden_all[slot_of]  11.1 us
    dot_general x1, matrix products, body(): lax.dot_general(hidden_live, everything, (((0,), (0,)), ((), ())), prefer...  10 us
  transfers between devices with their start and end apart: 11, of which 7 were waited for; matrix products, arithmetic and copies ran while one was open for 22% of the time, Pallas kernels for 0%

profile of v13, /device:TPU:1, one launch (start us, length us, event | category | flops | bytes accessed | tf_op | source)
XLA Modules:
  0.0 211.8 jit_solution(12939371880287210466)
XLA Ops:
  7.2 0.0 copy-start
  7.2 0.0 all-gather.2.cloned.1.call-start
  7.2 0.8 slice_bitcast_fusion
  8.0 0.7 convert_multiply_fusion.4
  8.7 0.7 copy.16
  9.4 0.1 reduce-window.8
  9.5 0.1 reduce
  9.6 0.7 convert_reduce_fusion.1
  10.4 0.0 copy-start.6
  10.4 2.4 %convolution_convert_fusion = bf16[80,2048]{1,0:T(8,128)(2,1)} fusion(bf16[144,2048]{1,0:T(8,128)(2,1)} %param.7, f32[144]{0:T(256)S(1)} %convert_multiply_fusion.4, s32[128]{0:T(128)S(1)} %slice_bitcast_fusion, s32[80]{0:T(128)S(1)} %subtract_add_fusion.1), kind=kOutput, calls=%fused_computation.11 | convolution fusion | flops 51223808 | bytes 918912 | tf_op jit(solution)/shard_map/dot_general | solution.py:58
  12.8 0.0 all-gather.2.cloned.1.call-update
  12.8 2.2 %fusion = bf16[1024,512]{1,0:T(8,128)(2,1)S(1)} fusion(bf16[1024,512]{1,0:T(8,128)(2,1)} %param.12, bf16[1024,512]{1,0:T(8,128)(2,1)} %param.11), kind=kLoop, calls=%fused_computation.12 | loop fusion | flops 4194304 | bytes 3145728 | tf_op jit(solution)/shard_map/convert_element_type | solution.py:63
  15.0 2.5 %collective-permute-start = (bf16[1024,512]{1,0:T(8,128)(2,1)S(1)}, bf16[1024,512]{1,0:T(8,128)(2,1)}, u32[]{:S(2)}, u32[]{:S(2)}) collective-permute-start(bf16[1024,512]{1,0:T(8,128)(2,1)S(1)} %fusion), channel_id=1, source_target_pairs={{0,2},{1,3},{2,0},{3,1},{4,6},{5,7},{6,4},{7,5},{8,10},{9,11},{10,... | collective-permute-start | bytes 3145736 | tf_op jit(solution)/shard_map/ppermute | solution.py:20
  17.5 0.0 copy-done.6
  17.5 1.3 collective-permute-start.2
  18.8 1.5 collective-permute-done.2
  20.3 3.0 %collective-permute-start.3 = (s32[2,32]{1,0:T(2,128)S(1)}, s32[2,32]{1,0:T(2,128)S(1)}, u32[]{:S(2)}, u32[]{:S(2)}) collective-permute-start(s32[2,32]{1,0:T(2,128)S(1)} %add_select_fusion.4), channel_id=1, source_target_pairs={{0,8},{4,12},{8,0},{12,4},{16,24},{20,28},{24,16},{28,20},{32,40},... | collective-permute-start | bytes 776 | tf_op jit(solution)/shard_map/ppermute | solution.py:35
  23.3 1.0 collective-permute-done.3
  24.4 1.3 collective-permute-start.4
  25.6 17.2 %collective-permute-done = bf16[1024,512]{1,0:T(8,128)(2,1)} collective-permute-done((bf16[1024,512]{1,0:T(8,128)(2,1)S(1)}, bf16[1024,512]{1,0:T(8,128)(2,1)}, u32[]{:S(2)}, u32[]{:S(2)}) %collective-permute-start) | collective-permute-done | bytes 1048608 | tf_op jit(solution)/shard_map/ppermute | solution.py:20
  42.8 2.7 %pad_maximum_fusion.1 = bf16[2,1024,512]{2,1,0:T(8,128)(2,1)} fusion(bf16[1,1024,512]{2,1,0:T(8,128)(2,1)} %bitcast.4, bf16[1,1024,512]{2,1,0:T(8,128)(2,1)S(1)} %bitcast.20), kind=kLoop, calls=%fused_computation.23 | loop fusion | flops 1048576 | bytes 4194304 | tf_op jit(solution)/shard_map/stack | solution.py:21
  45.5 1.3 collective-permute-start.1
  46.8 0.0 collective-permute-done.4
  46.8 2.8 %collective-permute-start.5 = (s32[8,32]{1,0:T(8,128)S(1)}, s32[8,32]{1,0:T(8,128)S(1)}, u32[]{:S(2)}, u32[]{:S(2)}) collective-permute-start(s32[8,32]{1,0:T(8,128)S(1)} %add_select_fusion.2), channel_id=1, source_target_pairs={{0,32},{4,36},{8,40},{12,44},{16,48},{20,52},{24,56},{28,60},{32,0... | collective-permute-start | bytes 3080 | tf_op jit(solution)/shard_map/ppermute | solution.py:35
  49.6 1.2 collective-permute-done.5
  50.9 3.4 %collective-permute-start.6 = (s32[16,32]{1,0:T(8,128)S(1)}, s32[16,32]{1,0:T(8,128)S(1)}, u32[]{:S(2)}, u32[]{:S(2)}) collective-permute-start(s32[16,32]{1,0:T(8,128)S(1)} %add_select_fusion.1), channel_id=1, source_target_pairs={{0,64},{4,68},{8,72},{12,76},{16,80},{20,84},{24,88},{28,92},{32,9... | collective-permute-start | bytes 6152 | tf_op jit(solution)/shard_map/ppermute | solution.py:35
  54.3 1.7 collective-permute-done.6
  56.0 0.2 reduce_window_sum.18
  56.2 0.1 add_bitcast_fusion
  56.3 0.1 copy.18
  56.4 0.1 copy.17
  56.4 0.4 convert_reduce_fusion
  56.8 0.1 subtract_add_fusion
  56.9 0.1 add.154
  57.0 0.2 iota_compare_fusion
  57.2 0.3 lt.76
  57.5 1.0 iota_add_fusion
  58.5 1.3 add.163
  59.9 0.0 collective-permute-done.1
  60.0 3.6 %pad_maximum_fusion = bf16[4,1024,512]{2,1,0:T(8,128)(2,1)} fusion(bf16[2,1024,512]{2,1,0:T(8,128)(2,1)} %collective-permute-done.1, bf16[1,1024,512]{2,1,0:T(8,128)(2,1)} %bitcast.4, bf16[1,1024,512]{2,1,0:T(8,128)(2,1)S(1)} %bitcast.21), kind=kLoop, calls=%fused_computation.5 | loop fusion | flops 4194304 | bytes 8388608 | tf_op jit(solution)/shard_map/concatenate | solution.py:23
  63.5 5.1 %gather_fusion = bf16[4,1024,512]{2,1,0:T(8,128)(2,1)} fusion(bf16[4,1024,512]{2,1,0:T(8,128)(2,1)} %pad_maximum_fusion, s32[1024]{0:T(1024)S(1)} %pad_clamp_fusion.1), kind=kCustom, calls=%fused_computation | custom fusion | bytes 8388624 | tf_op jit(solution)/shard_map/jit(_take)/gather | solution.py:26
  68.7 11.1 %gather_fusion.1 = bf16[2560,512]{1,0:T(8,128)(2,1)} fusion(bf16[4096,512]{1,0:T(8,128)(2,1)} %bitcast.19, s32[3072]{0:T(1024)S(1)} %pad_clamp_fusion), kind=kCustom, calls=%fused_computation.1 | custom fusion | bytes 5253120 | tf_op jit(solution)/shard_map/gather | solution.py:77
  79.7 54.4 %all-gather.2.cloned.1.call-done = bf16[2560,2048]{1,0:T(8,128)(2,1)} async-done(((bf16[80,2048]{1,0:T(8,128)(2,1)}), bf16[2560,2048]{1,0:T(8,128)(2,1)}) %all-gather.2.cloned.1.call-update) | async-done | bytes 10485776 | tf_op jit(solution)/shard_map/all_gather | solution.py:64
  134.1 0.0 copy-done
  134.1 9.8 %fusion.24 = f32[2560,512]{1,0:T(8,128)} fusion(bf16[2560,2048]{1,0:T(8,128)(2,1)} %all-gather.2.cloned.1.call-done, bf16[512,2048]{1,0:T(8,128)(2,1)S(1)} %copy-done), kind=kOutput, calls=%fused_computation.75 | convolution fusion | flops 5368709120 | bytes 17825792 | tf_op jit(solution)/shard_map/dot_general | solution.py:80
  143.9 7.8 %gather_fusion.3 = f32[1024,512]{1,0:T(8,128)} fusion(f32[2560,512]{1,0:T(8,128)} %fusion.24, s32[1024]{0:T(1024)S(1)} %get-tuple-element.27), kind=kCustom, calls=%fused_computation.3 | custom fusion | bytes 4198400 | tf_op jit(solution)/shard_map/gather | solution.py:94
  151.7 1.4 collective-permute-start.7
  153.1 7.8 %gather_fusion.2 = f32[1024,512]{1,0:T(8,128)} fusion(f32[2560,512]{1,0:T(8,128)} %fusion.24, s32[1024]{0:T(1024)S(1)} %get-tuple-element.28), kind=kCustom, calls=%fused_computation.2 | custom fusion | bytes 4198400 | tf_op jit(solution)/shard_map/gather | solution.py:94
  160.9 0.0 collective-permute-done.7
  160.9 2.6 %add_convert_fusion = bf16[1024,512]{1,0:T(8,128)(2,1)S(1)} fusion(f32[1024,512]{1,0:T(8,128)} %gather_fusion.2, f32[1024,512]{1,0:T(8,128)} %collective-permute-done.7), kind=kLoop, calls=%fused_computation.25 | loop fusion | flops 1048576 | bytes 5242880 | tf_op jit(solution)/shard_map/convert_element_type | solution.py:98
  163.5 12.0 %gather_fusion.4 = f32[2048,512]{1,0:T(8,128)} fusion(f32[2560,512]{1,0:T(8,128)} %fusion.24, s32[2048]{0:T(1024)S(1)} %broadcast_clamp_fusion), kind=kCustom, calls=%fused_computation.4 | custom fusion | bytes 8396800 | tf_op jit(solution)/shard_map/gather | solution.py:104
  175.5 1.9 slice.26
  177.5 0.3 collective-permute-start.8
  177.7 0.0 copy-done.5
  177.8 0.0 copy-start.2
  177.8 0.0 copy-start.3
  177.8 0.0 dynamic-slice-start
  177.8 0.5 collective-permute-start.9
  178.2 0.0 copy-done.4
  178.2 10.0 %fusion.23 = f32[512,2048]{1,0:T(8,128)} fusion(bf16[2560,512]{1,0:T(8,128)(2,1)S(1)} %copy-done.4, bf16[2560,2048]{1,0:T(8,128)(2,1)} %all-gather.2.cloned.1.call-done), kind=kOutput, calls=%fused_computation.74 | convolution fusion | flops 5368709120 | bytes 17301504 | tf_op jit(solution)/shard_map/dot_general | solution.py:107
  188.3 13.9 %collective-permute-done.9 = bf16[1024,512]{1,0:T(8,128)(2,1)S(1)} collective-permute-done((bf16[1024,512]{1,0:T(8,128)(2,1)S(1)}, bf16[1024,512]{1,0:T(8,128)(2,1)S(1)}, u32[]{:S(2)}, u32[]{:S(2)}) %collective-permute-start.9) | collective-permute-done | bytes 1048608 | tf_op jit(solution)/shard_map/ppermute | solution.py:100
  202.1 0.0 collective-permute-done.8
  202.1 0.0 copy-done.1
  202.2 2.8 %multiply_convert_fusion = (bf16[1024,512]{1,0:T(8,128)(2,1)}, bf16[1024,512]{1,0:T(8,128)(2,1)}) fusion(bf16[1024,512]{1,0:T(8,128)(2,1)S(1)} %copy-done.3, bf16[1024,512]{1,0:T(8,128)(2,1)S(1)} %collective-permute-done.9, f32[1024,512]{1,0:T(8,128)S(1)} %collective-permute-done.8, f32[2048,512]{1,0:T(8,128)S(1)} %copy-done.1, ...), kind=kLoop, calls=%fused_computation.24 | loop fusion | flops 9961472 | bytes 9438208 | tf_op jit(solution)/shard_map/convert_element_type | solution.py:113
  (22 shorter events, 0.2 us)
Async XLA Ops:
  7.2 127.0 %copy-start = (bf16[512,2048]{1,0:T(8,128)(2,1)S(1)}, bf16[512,2048]{1,0:T(8,128)(2,1)}, u32[]{:S(2)}) copy-start(bf16[512,2048]{1,0:T(8,128)(2,1)} %param.13) | copy-start | bytes 6291460
  7.2 126.9 %all-gather.2.cloned.1.call-start = ((), (), s32[]{:S(2)}) async-start(), calls=%async_computation | async-start | bytes 10813440 | tf_op jit(solution)/shard_map/all_gather | solution.py:64
  10.4 7.1 %copy-start.6 = (s32[1,32]{1,0:T(1,128)S(1)}, s32[1,32]{1,0:T(1,128)}, u32[]{:S(2)}) copy-start(s32[1,32]{1,0:T(1,128)} %param.10) | copy-start | bytes 388
  15.0 27.8 %collective-permute-start = (bf16[1024,512]{1,0:T(8,128)(2,1)S(1)}, bf16[1024,512]{1,0:T(8,128)(2,1)}, u32[]{:S(2)}, u32[]{:S(2)}) collective-permute-start(bf16[1024,512]{1,0:T(8,128)(2,1)S(1)} %fusion), channel_id=1, source_target_pairs={{0,2},{1,3},{2,0},{3,1},{4,6},{5,7},{6,4},{7,5},{8,10},{9,11},{10,... | collective-permute-start | bytes 3145736 | tf_op jit(solution)/shard_map/ppermute | solution.py:20
  17.5 2.8 %collective-permute-start.2 = (s32[1,32]{1,0:T(1,128)S(1)}, s32[1,32]{1,0:T(1,128)S(1)}, u32[]{:S(2)}, u32[]{:S(2)}) collective-permute-start(s32[1,32]{1,0:T(1,128)S(1)} %copy-done.6), channel_id=1, source_target_pairs={{0,4},{4,0},{8,12},{12,8},{16,20},{20,16},{24,28},{28,24},{32,36},... | collective-permute-start | bytes 392 | tf_op jit(solution)/shard_map/ppermute | solution.py:35
  20.3 4.0 %collective-permute-start.3 = (s32[2,32]{1,0:T(2,128)S(1)}, s32[2,32]{1,0:T(2,128)S(1)}, u32[]{:S(2)}, u32[]{:S(2)}) collective-permute-start(s32[2,32]{1,0:T(2,128)S(1)} %add_select_fusion.4), channel_id=1, source_target_pairs={{0,8},{4,12},{8,0},{12,4},{16,24},{20,28},{24,16},{28,20},{32,40},... | collective-permute-start | bytes 776 | tf_op jit(solution)/shard_map/ppermute | solution.py:35
  24.4 22.4 %collective-permute-start.4 = (s32[4,32]{1,0:T(4,128)S(1)}, s32[4,32]{1,0:T(4,128)S(1)}, u32[]{:S(2)}, u32[]{:S(2)}) collective-permute-start(s32[4,32]{1,0:T(4,128)S(1)} %add_select_fusion.3), channel_id=1, source_target_pairs={{0,16},{4,20},{8,24},{12,28},{16,0},{20,4},{24,8},{28,12},{32,48},... | collective-permute-start | bytes 1544 | tf_op jit(solution)/shard_map/ppermute | solution.py:35
  45.5 14.4 %collective-permute-start.1 = (bf16[2,1024,512]{2,1,0:T(8,128)(2,1)}, bf16[2,1024,512]{2,1,0:T(8,128)(2,1)}, u32[]{:S(2)}, u32[]{:S(2)}) collective-permute-start(bf16[2,1024,512]{2,1,0:T(8,128)(2,1)} %pad_maximum_fusion.1), channel_id=1, source_target_pairs={{0,1},{1,0},{2,3},{3,2},{4,5},{5,4},{6,7},{7,6},{8,9},{9,8},{10,11... | collective-permute-start | bytes 6291464 | tf_op jit(solution)/shard_map/ppermute | solution.py:22
  46.8 4.0 %collective-permute-start.5 = (s32[8,32]{1,0:T(8,128)S(1)}, s32[8,32]{1,0:T(8,128)S(1)}, u32[]{:S(2)}, u32[]{:S(2)}) collective-permute-start(s32[8,32]{1,0:T(8,128)S(1)} %add_select_fusion.2), channel_id=1, source_target_pairs={{0,32},{4,36},{8,40},{12,44},{16,48},{20,52},{24,56},{28,60},{32,0... | collective-permute-start | bytes 3080 | tf_op jit(solution)/shard_map/ppermute | solution.py:35
  50.9 5.2 %collective-permute-start.6 = (s32[16,32]{1,0:T(8,128)S(1)}, s32[16,32]{1,0:T(8,128)S(1)}, u32[]{:S(2)}, u32[]{:S(2)}) collective-permute-start(s32[16,32]{1,0:T(8,128)S(1)} %add_select_fusion.1), channel_id=1, source_target_pairs={{0,64},{4,68},{8,72},{12,76},{16,80},{20,84},{24,88},{28,92},{32,9... | collective-permute-start | bytes 6152 | tf_op jit(solution)/shard_map/ppermute | solution.py:35
  57.5 120.2 %copy-start.5 = (pred[4096]{0:T(1024)(128)(4,1)}, pred[4096]{0:T(1024)(128)(4,1)S(1)}, u32[]{:S(2)}) copy-start(pred[4096]{0:T(1024)(128)(4,1)S(1)} %lt.76) | copy-start | bytes 12292
  151.7 9.2 %collective-permute-start.7 = (f32[1024,512]{1,0:T(8,128)}, f32[1024,512]{1,0:T(8,128)}, u32[]{:S(2)}, u32[]{:S(2)}) collective-permute-start(f32[1024,512]{1,0:T(8,128)} %gather_fusion.3), channel_id=1, source_target_pairs={{0,1},{1,0},{2,3},{3,2},{4,5},{5,4},{6,7},{7,6},{8,9},{9,8},{10,11... | collective-permute-start | bytes 6291464 | tf_op jit(solution)/shard_map/ppermute | solution.py:97
  175.5 2.7 %copy-start.4 = (bf16[2560,512]{1,0:T(8,128)(2,1)S(1)}, bf16[2560,512]{1,0:T(8,128)(2,1)}, u32[]{:S(2)}) copy-start(bf16[2560,512]{1,0:T(8,128)(2,1)} %gather_fusion.1) | copy-start | bytes 7864324
  177.5 24.7 %collective-permute-start.8 = (f32[1024,512]{1,0:T(8,128)S(1)}, f32[1024,512]{1,0:T(8,128)S(1)}, u32[]{:S(2)}, u32[]{:S(2)}) collective-permute-start(f32[1024,512]{1,0:T(8,128)S(1)} %slice.26), channel_id=1, source_target_pairs={{0,1},{1,0},{2,3},{3,2},{4,5},{5,4},{6,7},{7,6},{8,9},{9,8},{10,11... | collective-permute-start | bytes 6291464 | tf_op jit(solution)/shard_map/ppermute | solution.py:105
  177.7 24.4 %copy-start.1 = (f32[2048,512]{1,0:T(8,128)S(1)}, f32[2048,512]{1,0:T(8,128)}, u32[]{:S(2)}) copy-start(f32[2048,512]{1,0:T(8,128)} %gather_fusion.4) | copy-start | bytes 12582916
  177.8 24.4 %copy-start.2 = (bf16[1024,512]{1,0:T(8,128)(2,1)S(1)}, bf16[1024,512]{1,0:T(8,128)(2,1)}, u32[]{:S(2)}) copy-start(bf16[1024,512]{1,0:T(8,128)(2,1)} %param.12) | copy-start | bytes 3145732
  177.8 24.4 %copy-start.3 = (bf16[1024,512]{1,0:T(8,128)(2,1)S(1)}, bf16[1024,512]{1,0:T(8,128)(2,1)}, u32[]{:S(2)}) copy-start(bf16[1024,512]{1,0:T(8,128)(2,1)} %param.11) | copy-start | bytes 3145732
  177.8 24.4 %dynamic-slice-start = ((pred[4096]{0:T(1024)(128)(4,1)}, s32[]{:T(128)}), pred[1024]{0:T(1024)(128)(4,1)S(1)}, s32[]{:S(2)}) async-start(pred[4096]{0:T(1024)(128)(4,1)} %copy-done.5, s32[]{:T(128)} %select_n.153), calls=%async_computation.1 | async-start | bytes 2560 | tf_op jit(solution)/shard_map/dynamic_slice | solution.py:111
  177.8 24.3 %collective-permute-start.9 = (bf16[1024,512]{1,0:T(8,128)(2,1)S(1)}, bf16[1024,512]{1,0:T(8,128)(2,1)S(1)}, u32[]{:S(2)}, u32[]{:S(2)}) collective-permute-start(bf16[1024,512]{1,0:T(8,128)(2,1)S(1)} %add_convert_fusion), channel_id=1, source_target_pairs={{0,2},{1,3},{2,0},{3,1},{4,6},{5,7},{6,4},{7,5},{8,10},{9,11},{10,... | collective-permute-start | bytes 3145736 | tf_op jit(solution)/shard_map/ppermute | solution.py:100
Sparse Core Ops, SparseCore 0:
  12.9 121.1 all-gather.1
